TPU v7x, 256 devices: a whole 4x4x8 slice. The times are simulated.
256 devices in a mesh: blk: 32 (over y, z), band: 8 (over x, core).
Axes of the slice: x: 4, y: 4, z: 8, core: 2. Of those that a mesh axis runs over, the one named last changes fastest.
Arguments:
- solution: float32 [512, 2, 4096], P('blk', None, 'band'), may hold values from -6 to 6
- residual: float32 [512, 2, 4096], P('blk', None, 'band'), may hold values from -4 to 4
- direction: float32 [512, 2, 4096], P('blk', None, 'band'), may hold values from -6 to 6
- prior_inverse: float32 [4096], P('band'), may hold values from 0.3 to 3
- preconditioner: float32 [4096], P('band'), may hold values from 0.2 to 2
- beam_window: float32 [8, 4096], P('band'), may hold values from 0.3 to 1
- legendre: bfloat16 [512, 64, 4096], P('blk'), may hold values from -4 to 4, as said below
- mode_orders: int32 [512], replicated, may hold values from 0 to 4095, as said below
- noise_weight: float32 [8, 64, 8192], P('band', 'blk'), may hold values from 0.2 to 2
- smoother_blocks: float32 [32, 64, 64], replicated, may hold values from -0.5 to 0.6
- tile_slots: int32 [4096], P('blk'), may hold values from 0 to 255, as said below
- tile_kinds: int32 [4096], P('blk'), may hold values from 0 to 31
Outputs:
- solution_next: float32 [512, 2, 4096], P('blk', None, 'band')
- residual_next: float32 [512, 2, 4096], P('blk', None, 'band')
- direction_next: float32 [512, 2, 4096], P('blk', None, 'band')
Inputs may be any that keep to these rules, and one draw needn't show every extreme that they name: `mode_orders`: 512 distinct orders, among them every order below the larger of 1 and 32. `legendre`: zero wherever the multipole l is below the slot's order in mode_orders. `tile_slots`: within the 128 entries of one cycle group, distinct tile numbers of that group's 2 * 128 tiles.
All inputs are finite; a program needn't handle non-finite values.
Results may differ from a plain program's by a relative error of at most 0.0016.
Values may be sent and summed in bfloat16 or wider, within the bound.
No kernel may reach another device: no remote copies, remote signals or barrier semaphores. Data moves between devices by JAX's collectives and lax.ppermute only.
A program may use at most 128 MiB of HBM per device.

v0:
```python
import math

import jax
import jax.numpy as jnp
from jax import lax
from jax.sharding import PartitionSpec as P

NPHI = 8192
TILE = 64


precise = lax.Precision.HIGHEST


def phases(mode_orders, column_count, stride):
    columns = jnp.arange(column_count, dtype=jnp.int32) * stride
    turn_counts = mode_orders[:, None] * columns[None, :] % NPHI
    angles = turn_counts.astype(jnp.float32) * (2.0 * math.pi / NPHI)
    return (jnp.cos(angles), jnp.sin(angles))


def smooth(pixels, smoother_blocks, tile_slots, tile_kinds):
    tile_rows = pixels.reshape(-1, TILE)
    picked = tile_rows[tile_slots]
    matrices = smoother_blocks[tile_kinds]
    inner_part = jnp.einsum("tij,tj->ti", matrices, picked, precision=precise)
    outer_part = jnp.einsum("tji,tj->ti", matrices, inner_part, precision=precise)
    return jnp.zeros_like(tile_rows).at[tile_slots].add(outer_part).reshape(pixels.shape)


def per_device(
    solution,
    residual,
    direction,
    prior_inverse,
    preconditioner,
    beam_window,
    legendre,
    mode_orders,
    noise_weight,
    smoother_blocks,
    tile_slots,
    tile_kinds,
):
    beam_row = beam_window[0]
    share_width = direction.shape[2]
    norm_scale = 1.0 / math.sqrt(mode_orders.shape[0])
    scaled_res = preconditioner[None, None, :] * residual
    norm_now = lax.psum(jnp.sum(residual * scaled_res), ("blk", "band"))
    weighted_piece = (
        beam_row[None, None, :] * lax.all_gather(direction, "band", axis=2, tiled=True)
    ).astype(jnp.bfloat16)
    coefficients = jnp.einsum(
        "mcl,mrl->mcr", weighted_piece, legendre, preferred_element_type=jnp.float32
    )
    cycle_coefficients = lax.all_to_all(
        coefficients, "blk", split_axis=2, concat_axis=0, tiled=True
    )
    cycle_count = cycle_coefficients.shape[2]
    outer_cos, outer_sin = phases(mode_orders, NPHI // 128, 128)
    inner_cos, inner_sin = phases(mode_orders, 128, 1)
    real_part = cycle_coefficients[:, 0, :, None]
    imag_part = cycle_coefficients[:, 1, :, None]
    upper_part = real_part * outer_cos[:, None, :] - imag_part * outer_sin[:, None, :]
    lower_part = real_part * outer_sin[:, None, :] + imag_part * outer_cos[:, None, :]
    pixel_grid = jnp.einsum("mra,mb->rab", upper_part, inner_cos, precision=precise) - jnp.einsum(
        "mra,mb->rab", lower_part, inner_sin, precision=precise
    )
    pixels = norm_scale * pixel_grid.reshape(cycle_count, NPHI)
    noisy = noise_weight[0] * pixels + smooth(pixels, smoother_blocks, tile_slots, tile_kinds)
    noisy_grid = noisy.reshape(cycle_count, NPHI // 128, 128)
    cos_sums = jnp.einsum("rab,mb->mra", noisy_grid, inner_cos, precision=precise)
    sin_sums = jnp.einsum("rab,mb->mra", noisy_grid, inner_sin, precision=precise)
    real_terms = norm_scale * (
        jnp.einsum("mra,ma->mr", cos_sums, outer_cos, precision=precise)
        - jnp.einsum("mra,ma->mr", sin_sums, outer_sin, precision=precise)
    )
    imag_terms = -norm_scale * (
        jnp.einsum("mra,ma->mr", cos_sums, outer_sin, precision=precise)
        + jnp.einsum("mra,ma->mr", sin_sums, outer_cos, precision=precise)
    )
    cycle_terms = jnp.stack([real_terms, imag_terms], axis=1).astype(jnp.bfloat16)
    mode_terms = lax.all_to_all(cycle_terms, "blk", split_axis=0, concat_axis=2, tiled=True)
    harmonic = jnp.einsum("mcr,mrl->mcl", mode_terms, legendre, preferred_element_type=jnp.float32)
    summed = lax.psum(beam_row[None, None, :] * harmonic, "band")
    image_part = lax.dynamic_slice_in_dim(
        summed, lax.axis_index("band") * share_width, share_width, 2
    )
    image = prior_inverse[None, None, :] * direction + image_part
    curvature_sum = lax.psum(jnp.sum(direction * image), ("blk", "band"))
    step_size = norm_now / curvature_sum
    residual_next = residual - step_size * image
    precond_next = preconditioner[None, None, :] * residual_next
    norm_next = lax.psum(jnp.sum(residual_next * precond_next), ("blk", "band"))
    solution_next = solution + step_size * direction
    direction_next = precond_next + norm_next / norm_now * direction
    return (solution_next, residual_next, direction_next)


def solution(mesh):
    return jax.shard_map(
        per_device,
        mesh=mesh,
        in_specs=(
            P("blk", None, "band"),
            P("blk", None, "band"),
            P("blk", None, "band"),
            P("band"),
            P("band"),
            P("band", None),
            P("blk", None, None),
            P(),
            P("band", "blk", None),
            P(),
            P("blk"),
            P("blk"),
        ),
        out_specs=(P("blk", None, "band"), P("blk", None, "band"), P("blk", None, "band")),
        check_vma=False,
    )
```

profile of v0, /device:TPU:1, one launch (start us, length us, event | category | flops | bytes accessed | tf_op | source)
XLA Modules:
  0.0 316.9 jit_solution(7952585820154048943)
XLA Ops:
  7.2 16.5 %all_gather.3 = f32[16,2,4096]{2,1,0:T(2,128)S(1)} all-gather(f32[16,2,512]{2,1,0:T(2,128)} %param.14), channel_id=1, replica_groups=mesh['blk'=32,'band'=8] {'band'}, dimensions={2}, use_global_device_ids=true | all-gather | bytes 589824 | tf_op jit(solution)/shard_map/all_gather | solution.py:51
  23.7 5.7 %fusion.4 = f32[16,2,64]{2,1,0:T(2,128)S(1)} fusion(bf16[16,64,4096]{2,1,0:T(8,128)(2,1)} %param.18, f32[16,2,4096]{2,1,0:T(2,128)S(1)} %all_gather.3, f32[4096]{0:T(1024)} %bitcast.71), kind=kOutput, calls=%fused_computation.16 | convolution fusion | flops 17039360 | bytes 8937472 | tf_op jit(solution)/shard_map/mcl,mrl->mcr/dot_general | solution.py:53
  29.4 0.7 copy.32
  30.1 9.8 %all-to-all-start = ((f32[16,2,64]{0,1,2:T(2,128)}), f32[16,2,64]{0,1,2:T(2,128)S(1)}, u32[]{:S(2)}, u32[]{:S(2)}) async-start(f32[16,2,64]{0,1,2:T(2,128)} %copy.32), calls=%async_computation | async-start | bytes 131072 | tf_op jit(solution)/shard_map/all_to_all | solution.py:56
  40.3 0.6 fusion.43
  40.9 2.7 gather_fusion
  43.6 5.2 %all-to-all-done = f32[16,2,64]{0,1,2:T(2,128)S(1)} async-done(((f32[16,2,64]{0,1,2:T(2,128)}), f32[16,2,64]{0,1,2:T(2,128)S(1)}, u32[]{:S(2)}, u32[]{:S(2)}) %all-to-all-start) | async-done | bytes 8224 | tf_op jit(solution)/shard_map/all_to_all | solution.py:56
  49.0 1.4 fusion.8
  50.4 1.4 fusion
  51.9 0.6 gather_fusion.1
  52.6 8.6 %convolution_bitcast_fusion.2 = f32[128,64,1]{1,2,0:T(1,128)S(1)} fusion(f32[128,64,64]{2,1,0:T(8,128)} %gather_fusion, f32[128,64,1]{1,2,0:T(1,128)S(1)} %bitcast.66), kind=kOutput, calls=%fused_computation.6 | convolution fusion | flops 6291456 | bytes 2162688 | tf_op jit(solution)/shard_map/tij,tj->ti/dot_general | solution.py:26
  61.2 3.7 %fusion.64 = f32[128,1,64]{2,1,0:T(1,128)S(1)} fusion(f32[128,64,64]{2,1,0:T(8,128)S(1)} %copy-done.1, f32[128,64,1]{1,2,0:T(1,128)S(1)} %convolution_bitcast_fusion.2), kind=kOutput, calls=%fused_computation.97 | convolution fusion | flops 6291456 | bytes 2162688 | tf_op jit(solution)/shard_map/tji,tj->ti/dot_general | solution.py:27
  64.9 1.3 scatter_custom_fusion
  66.3 1.4 convolution_bitcast_fusion
  67.7 1.5 multiply_reduce_fusion.3
  69.4 13.5 %all_to_all.36 = bf16[512,2,2]{2,1,0:T(2,128)(2,1)S(1)} all-to-all(bf16[512,2,2]{2,1,0:T(2,128)(2,1)S(1)} %copy.35), channel_id=1, replica_groups=mesh['blk'=32,'band'=8] {'blk'}, dimensions={0} | all-to-all | bytes 8192 | tf_op jit(solution)/shard_map/all_to_all | solution.py:83
  83.6 5.5 %convolution_multiply_fusion = f32[16,2,4096]{2,1,0:T(2,128)} fusion(bf16[16,2,64]{2,1,0:T(2,128)(2,1)S(1)} %copy.38, bf16[16,64,4096]{2,1,0:T(8,128)(2,1)} %param.18, f32[4096]{0:T(1024)S(1)} %bitcast.72), kind=kOutput, calls=%fused_computation.3 | convolution fusion | flops 16908288 | bytes 8933376 | tf_op jit(solution)/shard_map/mcr,mrl->mcl/dot_general | solution.py:84
  89.1 0.7 fusion.38
  89.8 61.8 %all-reduce.3.cloned.1.call-done = f32[16,2,4096]{2,1,0:T(2,128)} async-done(((f32[16,2,4096]{2,1,0:T(2,128)}), f32[16,2,4096]{2,1,0:T(2,128)}) %all-reduce.3.cloned.1.call-update) | async-done | bytes 524304 | tf_op jit(solution)/shard_map/psum | solution.py:85
  151.6 1.5 multiply_reduce_fusion.4
  153.1 78.5 %all-reduce = (f32[]{:T(128)}, f32[]{:T(128)}) all-reduce(f32[]{:T(128)} %fusion.38, f32[]{:T(128)} %multiply_reduce_fusion.4), channel_id=1, replica_groups=mesh['blk'=32,'band'=8] {'blk','band'}, use_global_device_ids=true, to_apply=%region_1.0 | all-reduce | flops 2 | bytes 16 | tf_op jit(solution)/shard_map/psum | solution.py:49
  233.0 1.5 fusion.37
  234.5 73.4 %psum.31 = f32[]{:T(128)} all-reduce(f32[]{:T(128)} %get-tuple-element.11), channel_id=1, replica_groups=mesh['blk'=32,'band'=8] {'blk','band'}, use_global_device_ids=true, to_apply=%region_7.8 | all-reduce | flops 1 | bytes 8 | tf_op jit(solution)/shard_map/psum | solution.py:94
  309.3 0.7 multiply_add_fusion
  (45 shorter events, 1.5 us)
Async XLA Ops:
  7.2 33.7 %copy-start = (f32[32,64,64]{2,1,0:T(8,128)S(1)}, f32[32,64,64]{2,1,0:T(8,128)}, u32[]{:S(2)}) copy-start(f32[32,64,64]{2,1,0:T(8,128)} %param.21) | copy-start | bytes 1572868
  23.7 16.5 %copy-start.11 = (s32[128]{0:T(128)S(1)}, s32[128]{0:T(128)}, u32[]{:S(2)}) copy-start(s32[128]{0:T(128)} %param.22) | copy-start | bytes 1540
  23.7 16.6 %copy-start.12 = (s32[128]{0:T(128)S(1)}, s32[128]{0:T(128)}, u32[]{:S(2)}) copy-start(s32[128]{0:T(128)} %param.23) | copy-start | bytes 1540
  23.7 16.6 %copy-start.9 = (s32[512]{0:T(512)S(1)}, s32[512]{0:T(512)}, u32[]{:S(2)}) copy-start(s32[512]{0:T(512)} %param.19) | copy-start | bytes 6148
  30.1 18.7 %all-to-all-start = ((f32[16,2,64]{0,1,2:T(2,128)}), f32[16,2,64]{0,1,2:T(2,128)S(1)}, u32[]{:S(2)}, u32[]{:S(2)}) async-start(f32[16,2,64]{0,1,2:T(2,128)} %copy.32), calls=%async_computation | async-start | bytes 131072 | tf_op jit(solution)/shard_map/all_to_all | solution.py:56
  40.0 111.6 %all-reduce.3.cloned.1.call-start = ((), (), s32[]{:S(2)}) async-start(), calls=%async_computation.2 | async-start | bytes 1048576 | tf_op jit(solution)/shard_map/psum | solution.py:85
  52.6 8.6 %copy-start.1 = (f32[128,64,64]{2,1,0:T(8,128)S(1)}, f32[128,64,64]{2,1,0:T(8,128)}, u32[]{:S(2)}) copy-start(f32[128,64,64]{2,1,0:T(8,128)} %gather_fusion) | copy-start | bytes 6291460
  52.6 13.7 %copy-start.10 = (f32[1,2,8192]{2,1,0:T(2,128)S(1)}, f32[1,2,8192]{2,1,0:T(2,128)}, u32[]{:S(2)}) copy-start(f32[1,2,8192]{2,1,0:T(2,128)} %param.20) | copy-start | bytes 196612
  61.1 22.4 %copy-start.5 = (f32[1,4096]{1,0:T(1,128)S(1)}, f32[1,4096]{1,0:T(1,128)}, u32[]{:S(2)}) copy-start(f32[1,4096]{1,0:T(1,128)} %param.17) | copy-start | bytes 49156
  83.5 5.6 %copy-start.4 = (f32[16,2,512]{2,1,0:T(2,128)S(1)}, f32[16,2,512]{2,1,0:T(2,128)}, u32[]{:S(2)}) copy-start(f32[16,2,512]{2,1,0:T(2,128)} %param.13) | copy-start | bytes 196612
  83.6 5.6 %copy-start.7 = (f32[512]{0:T(512)S(1)}, f32[512]{0:T(512)}, u32[]{:S(2)}) copy-start(f32[512]{0:T(512)} %param.16) | copy-start | bytes 6148
  83.6 68.1 %copy-start.2 = (f32[16,2,512]{2,1,0:T(2,128)S(1)}, f32[16,2,512]{2,1,0:T(2,128)}, u32[]{:S(2)}) copy-start(f32[16,2,512]{2,1,0:T(2,128)} %param.14) | copy-start | bytes 196612
  83.6 68.0 %copy-start.8 = (f32[512]{0:T(512)S(1)}, f32[512]{0:T(512)}, u32[]{:S(2)}) copy-start(f32[512]{0:T(512)} %param.15) | copy-start | bytes 6148
  83.6 225.7 %copy-start.6 = (f32[16,2,512]{2,1,0:T(2,128)S(1)}, f32[16,2,512]{2,1,0:T(2,128)}, u32[]{:S(2)}) copy-start(f32[16,2,512]{2,1,0:T(2,128)} %param.12) | copy-start | bytes 196612
  234.5 75.5 %copy-start.3 = (f32[16,2,512]{2,1,0:T(2,128)}, f32[16,2,512]{2,1,0:T(2,128)S(1)}, u32[]{:S(2)}) copy-start(f32[16,2,512]{2,1,0:T(2,128)S(1)} %get-tuple-element.12) | copy-start | bytes 196612
Sparse Core Ops, SparseCore 0:
  89.2 62.3 all-reduce.2
where the time goes:
time: 317 us
  blocking collectives  182 us (57%)
  waiting for transfers between devices  67 us (21%)
  matrix products  29.2 us (9%)
  between operations  17 us (5%)
  starting transfers between devices  10.1 us (3%)
  other arithmetic  6.32 us (2%)
  local copies, waits for them, and re-layouts  5.3 us (2%)
    psum x1, blocking collectives, per_device(): norm_now = lax.psum(jnp.sum(residual * scaled_res), ('blk', 'band'))  78.5 us
    psum x1, blocking collectives, per_device(): norm_next = lax.psum(jnp.sum(residual_next * precond_next), ('blk', 'band'))  73.4 us
    psum x1, waiting for transfers between devices, per_device(): summed = lax.psum(beam_row[None, None, :] * harmonic, 'band')  61.8 us
    all_gather x1, blocking collectives, per_device(): lax.all_gather(direction, 'band', axis=2, tiled=True)  16.5 us
    all_to_all x1, blocking collectives, per_device(): lax.all_to_all(cycle_terms, 'blk', split_axis=0, concat_axis=2, tiled=True)  13.5 us
    all_to_all x1, starting transfers between devices, per_device(): lax.all_to_all(coefficients, 'blk', split_axis=2, concat_axis=0, tiled=True)  9.85 us
    dot_general x1, matrix products, smooth(): inner_part = jnp.einsum('tij,tj->ti', matrices, picked, precision=precise)  8.55 us
  transfers between devices with their start and end apart: 2, of which 2 were waited for; matrix products, arithmetic and copies ran while one was open for 1% of the time, Pallas kernels for 0%

commit v1 on v0

--- a/solution.py
+++ b/solution.py
@@ -10,6 +10,7 @@
 
 
 precise = lax.Precision.HIGHEST
+EVERY = ("blk", "band")
 
 
 def phases(mode_orders, column_count, stride):
@@ -19,12 +20,19 @@
     return (jnp.cos(angles), jnp.sin(angles))
 
 
+def pick_kind(per_kind, tile_kinds):
+    kinds = jnp.arange(per_kind.shape[1], dtype=jnp.int32)
+    chosen = tile_kinds[:, None, None] == kinds[None, :, None]
+    return jnp.sum(jnp.where(chosen, per_kind, 0.0), axis=1)
+
+
 def smooth(pixels, smoother_blocks, tile_slots, tile_kinds):
     tile_rows = pixels.reshape(-1, TILE)
     picked = tile_rows[tile_slots]
-    matrices = smoother_blocks[tile_kinds]
-    inner_part = jnp.einsum("tij,tj->ti", matrices, picked, precision=precise)
-    outer_part = jnp.einsum("tji,tj->ti", matrices, inner_part, precision=precise)
+    inner_all = jnp.einsum("kij,tj->tki", smoother_blocks, picked, precision=precise)
+    inner_part = pick_kind(inner_all, tile_kinds)
+    outer_all = jnp.einsum("kji,tj->tki", smoother_blocks, inner_part, precision=precise)
+    outer_part = pick_kind(outer_all, tile_kinds)
     return jnp.zeros_like(tile_rows).at[tile_slots].add(outer_part).reshape(pixels.shape)
 
 
@@ -42,21 +50,35 @@
     tile_slots,
     tile_kinds,
 ):
-    beam_row = beam_window[0]
-    share_width = direction.shape[2]
-    norm_scale = 1.0 / math.sqrt(mode_orders.shape[0])
-    scaled_res = preconditioner[None, None, :] * residual
-    norm_now = lax.psum(jnp.sum(residual * scaled_res), ("blk", "band"))
-    weighted_piece = (
-        beam_row[None, None, :] * lax.all_gather(direction, "band", axis=2, tiled=True)
-    ).astype(jnp.bfloat16)
-    coefficients = jnp.einsum(
-        "mcl,mrl->mcr", weighted_piece, legendre, preferred_element_type=jnp.float32
+    nblk = lax.axis_size("blk")
+    nband = lax.axis_size("band")
+    band = lax.axis_index("band")
+    orders_dev, parts, width = direction.shape
+    cycles_all = legendre.shape[1]
+    cycles_dev = cycles_all // nblk
+    order_count = mode_orders.shape[0]
+    norm_scale = 1.0 / math.sqrt(order_count)
+
+    beam_here = lax.all_to_all(
+        beam_window.reshape(nband, width), "band", split_axis=0, concat_axis=0, tiled=True
     )
-    cycle_coefficients = lax.all_to_all(
-        coefficients, "blk", split_axis=2, concat_axis=0, tiled=True
+    legendre_here = lax.dynamic_slice_in_dim(legendre, band * width, width, 2)
+
+    weighted = (beam_here[None, :, None, :] * direction[:, None, :, :]).astype(jnp.bfloat16)
+    weighted = weighted.reshape(orders_dev, nband * parts, width)
+    partial = jnp.einsum(
+        "sql,srl->sqr", weighted, legendre_here, preferred_element_type=jnp.float32
     )
-    cycle_count = cycle_coefficients.shape[2]
+    partial = partial.reshape(orders_dev, nband, parts, nblk, cycles_dev)
+    outgoing = partial.transpose(3, 1, 0, 2, 4).reshape(
+        nblk * nband, orders_dev, parts, cycles_dev
+    )
+    incoming = lax.all_to_all(outgoing, EVERY, split_axis=0, concat_axis=0, tiled=True)
+    cycle_coefficients = jnp.sum(
+        incoming.reshape(nblk, nband, orders_dev, parts, cycles_dev), axis=1
+    ).reshape(order_count, parts, cycles_dev)
+
+    cycle_count = cycles_dev
     outer_cos, outer_sin = phases(mode_orders, NPHI // 128, 128)
     inner_cos, inner_sin = phases(mode_orders, 128, 1)
     real_part = cycle_coefficients[:, 0, :, None]
@@ -80,18 +102,36 @@
         + jnp.einsum("mra,ma->mr", sin_sums, outer_cos, precision=precise)
     )
     cycle_terms = jnp.stack([real_terms, imag_terms], axis=1).astype(jnp.bfloat16)
-    mode_terms = lax.all_to_all(cycle_terms, "blk", split_axis=0, concat_axis=2, tiled=True)
-    harmonic = jnp.einsum("mcr,mrl->mcl", mode_terms, legendre, preferred_element_type=jnp.float32)
-    summed = lax.psum(beam_row[None, None, :] * harmonic, "band")
-    image_part = lax.dynamic_slice_in_dim(
-        summed, lax.axis_index("band") * share_width, share_width, 2
+
+    per_owner = cycle_terms.reshape(nblk, 1, orders_dev, parts, cycles_dev)
+    returning = jnp.broadcast_to(
+        per_owner, (nblk, nband, orders_dev, parts, cycles_dev)
+    ).reshape(nblk * nband, orders_dev, parts, cycles_dev)
+    arrived = lax.all_to_all(returning, EVERY, split_axis=0, concat_axis=0, tiled=True)
+    mode_terms = arrived.reshape(nblk, nband, orders_dev, parts, cycles_dev)
+    mode_terms = mode_terms.transpose(2, 1, 3, 0, 4).reshape(orders_dev, nband * parts, cycles_all)
+    harmonic = jnp.einsum(
+        "sqr,srl->sql", mode_terms, legendre_here, preferred_element_type=jnp.float32
+    ).reshape(orders_dev, nband, parts, width)
+    summed = jnp.sum(beam_here[None, :, None, :] * harmonic, axis=1)
+
+    image = prior_inverse[None, None, :] * direction + summed
+    scaled_res = preconditioner[None, None, :] * residual
+    scaled_image = preconditioner[None, None, :] * image
+    local_sums = jnp.stack(
+        [
+            jnp.sum(residual * scaled_res),
+            jnp.sum(direction * image),
+            jnp.sum(scaled_res * image),
+            jnp.sum(scaled_image * image),
+        ]
     )
-    image = prior_inverse[None, None, :] * direction + image_part
-    curvature_sum = lax.psum(jnp.sum(direction * image), ("blk", "band"))
-    step_size = norm_now / curvature_sum
+    totals = lax.psum(local_sums, EVERY)
+    norm_now = totals[0]
+    step_size = norm_now / totals[1]
+    norm_next = norm_now - step_size * (2.0 * totals[2] - step_size * totals[3])
     residual_next = residual - step_size * image
     precond_next = preconditioner[None, None, :] * residual_next
-    norm_next = lax.psum(jnp.sum(residual_next * precond_next), ("blk", "band"))
     solution_next = solution + step_size * direction
     direction_next = precond_next + norm_next / norm_now * direction
     return (solution_next, residual_next, direction_next)

time: 317 us -> 165 us (0.52)
  blocking collectives: 182 us -> 93.5 us
  waiting for transfers between devices: 67 us -> 19.6 us
  matrix products: 29.2 us -> 10.8 us
  between operations: 17 us -> 5.07 us
  starting transfers between devices: 10.1 us -> 19.2 us
    psum x2 -> x1, blocking collectives: 152 us -> 72.6 us  [per_device(): totals = lax.psum(local_sums, EVERY)]
    psum x1 -> x0, waiting for transfers between devices: 61.8 us -> none  [per_device(): summed = lax.psum(beam_row[None, None, :] * harmonic, 'band')]
    dot_general x4 -> x3, matrix products: 23.4 us -> 4.09 us  [the longest x1 1.61 us: per_device(): jnp.einsum('sql,srl->sqr', weighted, legendre_here, preferred_element_typ...]
    all_gather x1 -> x0, blocking collectives: 16.5 us -> none  [per_device(): lax.all_gather(direction, 'band', axis=2, tiled=True)]
    all_to_all x1 -> x2, waiting for transfers between devices: 5.19 us -> 19.6 us  [the longest x1 18.3 us: per_device(): lax.all_to_all(outgoing, EVERY, split_axis=0, concat_axis=0, tiled=True)]
    all_to_all x1 -> x2, starting transfers between devices: 9.85 us -> 19.2 us  [the longest x1 12.7 us: per_device(): lax.all_to_all(outgoing, EVERY, split_axis=0, concat_axis=0, tiled=True)]
    all_to_all x1, blocking collectives: 13.5 us -> 20.9 us  [per_device(): lax.all_to_all(returning, EVERY, split_axis=0, concat_axis=0, tiled=True)]
  transfers between devices with their start and end apart: 2 -> 2, of which waited for: 2 -> 2; matrix products, arithmetic and copies ran while one was open for 1% -> 3% of each run, Pallas kernels for 0% -> 0%
where the time goes in v1:
time: 165 us; the launch traced here: 164 us
  blocking collectives  93.5 us (57%)
  waiting for transfers between devices  19.6 us (12%)
  starting transfers between devices  19.2 us (12%)
  matrix products  10.8 us (7%)
  other arithmetic  8.69 us (5%)
  local copies, waits for them, and re-layouts  7.42 us (4%)
  between operations  5.07 us (3%)
    psum x1, blocking collectives, per_device(): totals = lax.psum(local_sums, EVERY)  72.6 us
    all_to_all x1, blocking collectives, per_device(): lax.all_to_all(returning, EVERY, split_axis=0, concat_axis=0, tiled=True)  20.9 us
    all_to_all x1, waiting for transfers between devices, per_device(): lax.all_to_all(outgoing, EVERY, split_axis=0, concat_axis=0, tiled=True)  18.3 us
    all_to_all x1, starting transfers between devices, per_device(): lax.all_to_all(outgoing, EVERY, split_axis=0, concat_axis=0, tiled=True)  12.7 us
    all_to_all x1, starting transfers between devices, per_device(): lax.all_to_all(beam_window.reshape(nband, width), 'band', split_axis=0, c...  6.58 us
  transfers between devices with their start and end apart: 2, of which 2 were waited for; matrix products, arithmetic and copies ran while one was open for 3% of the time, Pallas kernels for 0%

profile of v1, /device:TPU:1, one launch (start us, length us, event | category | flops | bytes accessed | tf_op | source)
XLA Modules:
  0.0 164.4 jit_solution(6899549537042499709)
XLA Ops:
  0.7 6.6 %all-to-all-start = ((f32[8,1,512]{2,1,0:T(1,128)}), f32[8,1,512]{2,1,0:T(1,128)S(1)}, u32[]{:S(2)}, u32[]{:S(2)}) async-start(f32[8,1,512]{2,1,0:T(1,128)} %bitcast.87), calls=%async_computation | async-start | bytes 32768 | tf_op jit(solution)/shard_map/all_to_all | solution.py:62
  7.2 1.3 fusion.49
  8.5 0.7 iota_compare_fusion
  9.2 1.0 mul.247
  10.5 1.4 all-to-all-done
  12.0 1.6 fusion.4
  14.1 1.2 copy.49
  15.3 12.7 %all-to-all-start.1 = ((f32[256,16,2,2]{1,3,2,0:T(2,128)}), f32[256,16,2,2]{1,3,2,0:T(2,128)S(1)}, u32[]{:S(2)}, u32[]{:S(2)}) async-start(f32[256,16,2,2]{1,3,2,0:T(2,128)} %copy.49), calls=%async_computation.1 | async-start | bytes 1048576 | tf_op jit(solution)/shard_map/all_to_all | solution.py:76
  28.0 0.7 compare_select_fusion
  28.7 1.6 copy.52
  30.2 18.3 %all-to-all-done.1 = f32[256,16,2,2]{1,3,2,0:T(2,128)S(1)} async-done(((f32[256,16,2,2]{1,3,2,0:T(2,128)}), f32[256,16,2,2]{1,3,2,0:T(2,128)S(1)}, u32[]{:S(2)}, u32[]{:S(2)}) %all-to-all-start.1) | async-done | bytes 65568 | tf_op jit(solution)/shard_map/all_to_all | solution.py:76
  48.9 1.4 fusion.12
  50.3 1.4 fusion.1
  52.5 1.0 fusion
  53.5 1.0 fusion.71
  54.7 1.2 scatter_custom_fusion
  56.0 1.4 convolution_bitcast_fusion
  57.4 1.4 multiply_reduce_fusion.4
  59.3 20.9 %all_to_all.19 = bf16[256,16,2,2]{1,3,2,0:T(2,128)(2,1)S(1)} all-to-all(bf16[256,16,2,2]{1,3,2,0:T(2,128)(2,1)S(1)} %bitcast.83), channel_id=1, replica_groups=mesh['blk'=32,'band'=8] {'blk','band'}, dimensions={0} | all-to-all | bytes 65536 | tf_op jit(solution)/shard_map/all_to_all | solution.py:110
  80.7 1.5 fusion.2
  82.8 0.9 fusion.41
  83.6 2.7 %pad_maximum_fusion.1 = f32[4]{0:T(128)S(1)} fusion(f32[1]{0:T(128)} %bitcast.24, f32[1]{0:T(128)} %bitcast.23, f32[1]{0:T(128)} %bitcast.22, f32[1]{0:T(128)} %bitcast.4), kind=kLoop, calls=%fused_computation.88 | loop fusion | flops 12 | bytes 32 | tf_op jit(solution)/shard_map/stack | solution.py:121
  86.3 72.6 %psum.7 = f32[4]{0:T(128)S(1)} all-reduce(f32[4]{0:T(128)S(1)} %pad_maximum_fusion.1), channel_id=1, replica_groups=mesh['blk'=32,'band'=8] {'blk','band'}, use_global_device_ids=true, to_apply=%region_9.10 | all-reduce | flops 4 | bytes 32 | tf_op jit(solution)/shard_map/psum | solution.py:129
  163.6 0.7 multiply_add_fusion
  (45 shorter events, 4.3 us)
Async XLA Ops:
  0.6 48.2 %copy-start.5 = (s32[512]{0:T(512)S(1)}, s32[512]{0:T(512)}, u32[]{:S(2)}) copy-start(s32[512]{0:T(512)} %param.19) | copy-start | bytes 6148
  0.6 51.8 %copy-start = (f32[32,64,64]{2,1,0:T(8,128)S(1)}, f32[32,64,64]{2,1,0:T(8,128)}, u32[]{:S(2)}) copy-start(f32[32,64,64]{2,1,0:T(8,128)} %param.21) | copy-start | bytes 1572868
  0.7 11.3 %all-to-all-start = ((f32[8,1,512]{2,1,0:T(1,128)}), f32[8,1,512]{2,1,0:T(1,128)S(1)}, u32[]{:S(2)}, u32[]{:S(2)}) async-start(f32[8,1,512]{2,1,0:T(1,128)} %bitcast.87), calls=%async_computation | async-start | bytes 32768 | tf_op jit(solution)/shard_map/all_to_all | solution.py:62
  11.9 44.1 %copy-start.7 = (f32[1,2,8192]{2,1,0:T(2,128)S(1)}, f32[1,2,8192]{2,1,0:T(2,128)}, u32[]{:S(2)}) copy-start(f32[1,2,8192]{2,1,0:T(2,128)} %param.20) | copy-start | bytes 196612
  15.3 33.2 %all-to-all-start.1 = ((f32[256,16,2,2]{1,3,2,0:T(2,128)}), f32[256,16,2,2]{1,3,2,0:T(2,128)S(1)}, u32[]{:S(2)}, u32[]{:S(2)}) async-start(f32[256,16,2,2]{1,3,2,0:T(2,128)} %copy.49), calls=%async_computation.1 | async-start | bytes 1048576 | tf_op jit(solution)/shard_map/all_to_all | solution.py:76
  48.7 34.0 %copy-start.1 = (f32[16,2,512]{2,1,0:T(2,128)S(1)}, f32[16,2,512]{2,1,0:T(2,128)}, u32[]{:S(2)}) copy-start(f32[16,2,512]{2,1,0:T(2,128)} %param.14) | copy-start | bytes 196612
  48.7 34.0 %copy-start.2 = (f32[16,2,512]{2,1,0:T(2,128)S(1)}, f32[16,2,512]{2,1,0:T(2,128)}, u32[]{:S(2)}) copy-start(f32[16,2,512]{2,1,0:T(2,128)} %param.13) | copy-start | bytes 196612
  48.7 34.0 %copy-start.4 = (f32[512]{0:T(512)S(1)}, f32[512]{0:T(512)}, u32[]{:S(2)}) copy-start(f32[512]{0:T(512)} %param.16) | copy-start | bytes 6148
  48.7 34.0 %copy-start.6 = (f32[512]{0:T(512)S(1)}, f32[512]{0:T(512)}, u32[]{:S(2)}) copy-start(f32[512]{0:T(512)} %param.15) | copy-start | bytes 6148
  48.9 114.8 %copy-start.3 = (f32[16,2,512]{2,1,0:T(2,128)S(1)}, f32[16,2,512]{2,1,0:T(2,128)}, u32[]{:S(2)}) copy-start(f32[16,2,512]{2,1,0:T(2,128)} %param.12) | copy-start | bytes 196612

commit v2 on v1

--- a/solution.py
+++ b/solution.py
@@ -126,7 +126,8 @@
             jnp.sum(scaled_image * image),
         ]
     )
-    totals = lax.psum(local_sums, EVERY)
+    shared = jnp.broadcast_to(local_sums[None], (nblk * nband, local_sums.shape[0]))
+    totals = jnp.sum(lax.all_to_all(shared, EVERY, split_axis=0, concat_axis=0, tiled=True), axis=0)
     norm_now = totals[0]
     step_size = norm_now / totals[1]
     norm_next = norm_now - step_size * (2.0 * totals[2] - step_size * totals[3])

time: 165 us -> 111 us (0.67)
  blocking collectives: 93.5 us -> 38.8 us
    psum x1 -> x0, blocking collectives: 72.6 us -> none  [per_device(): totals = lax.psum(local_sums, EVERY)]
    all_to_all x0 -> x1, blocking collectives: none -> 17.9 us  [per_device(): lax.all_to_all(shared, EVERY, split_axis=0, concat_axis=0, tiled=True)]
  transfers between devices with their start and end apart: 2 -> 2, of which waited for: 2 -> 2; matrix products, arithmetic and copies ran while one was open for 3% -> 5% of each run, Pallas kernels for 0% -> 0%
where the time goes in v2:
time: 111 us; the launch traced here: 110 us
  blocking collectives  38.8 us (35%)
  waiting for transfers between devices  19.6 us (18%)
  starting transfers between devices  19.2 us (17%)
  matrix products  10.8 us (10%)
  other arithmetic  8.97 us (8%)
  local copies, waits for them, and re-layouts  7.49 us (7%)
  between operations  5.07 us (5%)
    all_to_all x1, blocking collectives, per_device(): lax.all_to_all(returning, EVERY, split_axis=0, concat_axis=0, tiled=True)  20.9 us
    all_to_all x1, waiting for transfers between devices, per_device(): lax.all_to_all(outgoing, EVERY, split_axis=0, concat_axis=0, tiled=True)  18.3 us
    all_to_all x1, blocking collectives, per_device(): lax.all_to_all(shared, EVERY, split_axis=0, concat_axis=0, tiled=True)  17.9 us
    all_to_all x1, starting transfers between devices, per_device(): lax.all_to_all(outgoing, EVERY, split_axis=0, concat_axis=0, tiled=True)  12.7 us
    all_to_all x1, starting transfers between devices, per_device(): lax.all_to_all(beam_window.reshape(nband, width), 'band', split_axis=0, c...  6.58 us
    another operation x1, other arithmetic, per_device(): jnp.stack([jnp.sum(residual * scaled_res), jnp.sum(direction * image), jn...  2.7 us
  transfers between devices with their start and end apart: 2, of which 2 were waited for; matrix products, arithmetic and copies ran while one was open for 5% of the time, Pallas kernels for 0%

profile of v2, /device:TPU:1, one launch (start us, length us, event | category | flops | bytes accessed | tf_op | source)
XLA Modules:
  0.0 110.0 jit_solution(5985631823828836472)
XLA Ops:
  0.7 6.6 %all-to-all-start = ((f32[8,1,512]{2,1,0:T(1,128)}), f32[8,1,512]{2,1,0:T(1,128)S(1)}, u32[]{:S(2)}, u32[]{:S(2)}) async-start(f32[8,1,512]{2,1,0:T(1,128)} %bitcast.87), calls=%async_computation | async-start | bytes 32768 | tf_op jit(solution)/shard_map/all_to_all | solution.py:62
  7.2 1.3 %fusion.49 = (f32[512,64]{0,1:T(8,128)S(1)}, f32[512,64]{0,1:T(8,128)S(1)}) fusion(s32[64]{0:T(128)S(1)} %iota_multiply_fusion, s32[512]{0:T(512)} %param.19), kind=kLoop, calls=%fused_computation.77 | loop fusion | flops 458752 | bytes 264448 | tf_op jit(solution)/shard_map/cos | solution.py:20
  8.5 0.7 iota_compare_fusion
  9.2 1.0 mul.247
  10.5 1.4 %all-to-all-done = f32[8,1,512]{2,1,0:T(1,128)S(1)} async-done(((f32[8,1,512]{2,1,0:T(1,128)}), f32[8,1,512]{2,1,0:T(1,128)S(1)}, u32[]{:S(2)}, u32[]{:S(2)}) %all-to-all-start) | async-done | bytes 16416 | tf_op jit(solution)/shard_map/all_to_all | solution.py:62
  12.0 1.6 %fusion.4 = f32[16,16,64]{2,1,0:T(8,128)S(1)} fusion(bf16[16,64,4096]{2,1,0:T(8,128)(2,1)} %param.18, s32[]{:T(128)S(6)} %select_n.35, f32[16,16,512]{2,1,0:T(8,128)S(1)} %mul.248, f32[16,512]{1,0:T(8,128)S(1)} %mul.245), kind=kOutput, calls=%fused_computation.11 | convolution fusion | flops 17039360 | bytes 1671172 | tf_op jit(solution)/shard_map/sql,srl->sqr/dot_general | solution.py:69
  14.1 1.2 %copy.71 = f32[256,16,2,2]{1,3,2,0:T(2,128)} copy(f32[256,16,2,2]{1,0,3,2:T(8,128)S(1)} %bitcast.81) | data formatting | bytes 131072 | tf_op jit(solution)/shard_map/reshape | solution.py:73
  15.3 12.7 %all-to-all-start.1 = ((f32[256,16,2,2]{1,3,2,0:T(2,128)}), f32[256,16,2,2]{1,3,2,0:T(2,128)S(1)}, u32[]{:S(2)}, u32[]{:S(2)}) async-start(f32[256,16,2,2]{1,3,2,0:T(2,128)} %copy.71), calls=%async_computation.1 | async-start | bytes 1048576 | tf_op jit(solution)/shard_map/all_to_all | solution.py:76
  28.0 0.7 compare_select_fusion
  28.7 1.6 %copy.74 = f32[32,64,64]{1,2,0:T(8,128)S(1)} copy(f32[32,64,64]{2,1,0:T(8,128)} %param.21) | data formatting | bytes 1048576 | tf_op args[9]
  30.2 18.3 %all-to-all-done.1 = f32[256,16,2,2]{1,3,2,0:T(2,128)S(1)} async-done(((f32[256,16,2,2]{1,3,2,0:T(2,128)}), f32[256,16,2,2]{1,3,2,0:T(2,128)S(1)}, u32[]{:S(2)}, u32[]{:S(2)}) %all-to-all-start.1) | async-done | bytes 65568 | tf_op jit(solution)/shard_map/all_to_all | solution.py:76
  48.9 1.4 %fusion.12 = f32[2,64,128]{2,1,0:T(8,128)S(1)} fusion(f32[512,64]{0,1:T(8,128)S(1)} %get-tuple-element.20, f32[512,2]{0,1:T(2,128)S(1)} %get-tuple-element.18, f32[512,64]{0,1:T(8,128)S(1)} %get-tuple-element.19, f32[512,2]{0,1:T(2,128)S(1)} %get-tuple-element.17, s32[512]{0:T(512)S(1)} %copy-done.5), kind=kOutput, calls=%fused_computation.26 | convolution fusion | flops 101777408 | bytes 337920 | tf_op jit(solution)/shard_map/mra,mb->rab/dot_general | solution.py:88
  50.3 1.4 %fusion.1 = f32[2,64,128]{2,1,0:T(8,128)S(1)} fusion(f32[2,64,128]{2,1,0:T(8,128)S(1)} %fusion.12, f32[512,64]{0,1:T(8,128)S(1)} %get-tuple-element.20, f32[512,2]{0,1:T(2,128)S(1)} %get-tuple-element.18, f32[512,64]{0,1:T(8,128)S(1)} %get-tuple-element.19, f32[512,2]{0,1:T(2,128)S(1)} %get-tuple-element.17, s32[512]{0:T(512)S(1)} %copy-done.5), kind=kOutput, calls=%fused_computation.7 | convolution fusion | flops 101810176 | bytes 403456 | tf_op jit(solution)/shard_map/mra,mb->rab/dot_general | solution.py:88
  52.5 1.0 fusion
  53.5 1.0 fusion.71
  54.7 1.2 %scatter_custom_fusion = f32[256,64]{1,0:T(8,128)S(1)} fusion(s32[128]{0:T(128)S(1)} %compare_select_fusion, f32[128,64]{1,0:T(8,128)S(1)} %copy.75, f32[]{:T(128)} %constant.17.clone.1), kind=kCustom, calls=%fused_computation.74 | custom fusion | flops 8192 | bytes 65540 | tf_op jit(solution)/shard_map/scatter-add | solution.py:36
  56.0 1.4 %convolution_bitcast_fusion = f32[512,64,2]{0,1,2:T(8,128)S(1)} fusion(s32[512]{0:T(512)S(1)} %copy-done.5, f32[2,64,128]{2,1,0:T(8,128)S(1)} %reshape.173, f32[2,64,128]{2,1,0:T(8,128)S(1)} %fusion.1, f32[1,2,64,128]{3,1,2,0:T(2,128)S(1)} %bitcast.88), kind=kOutput, calls=%fused_computation.4 | convolution fusion | flops 101613568 | bytes 460800 | tf_op jit(solution)/shard_map/rab,mb->mra/dot_general | solution.py:95
  57.4 1.4 %multiply_reduce_fusion.4 = (f32[512,2]{0,1:T(2,128)S(1)}, f32[512,2]{0,1:T(2,128)S(1)}, f32[512,2]{0,1:T(2,128)S(1)}, f32[512,2]{0,1:T(2,128)S(1)}) fusion(f32[512,64]{0,1:T(8,128)S(1)} %get-tuple-element.19, f32[512,64]{0,1:T(8,128)S(1)} %get-tuple-element.20, f32[512,64,2]{0,1,2:T(8,128)S(1)} %convolution_bitcast_fusion, ...), kind=kOutput, calls=%fused_computation.31 | convolution fusion | flops 102133760 | bytes 739328 | tf_op jit(solution)/shard_map/rab,mb->mra/dot_general | solution.py:94
  59.3 20.9 %all_to_all.25 = bf16[256,16,2,2]{1,3,2,0:T(2,128)(2,1)S(1)} all-to-all(bf16[256,16,2,2]{1,3,2,0:T(2,128)(2,1)S(1)} %bitcast.83), channel_id=1, replica_groups=mesh['blk'=32,'band'=8] {'blk','band'}, dimensions={0} | all-to-all | bytes 65536 | tf_op jit(solution)/shard_map/all_to_all | solution.py:110
  80.7 1.5 %fusion.2 = f32[16,16,512]{2,1,0:T(8,128)S(1)} fusion(bf16[16,16,64]{2,1,0:T(8,128)(2,1)S(1)} %copy.79, bf16[16,64,4096]{2,1,0:T(8,128)(2,1)} %param.18, s32[]{:T(128)S(6)} %select_n.35), kind=kOutput, calls=%fused_computation.9 | convolution fusion | flops 16777216 | bytes 1605636 | tf_op jit(solution)/shard_map/sqr,srl->sql/dot_general | solution.py:113
  82.8 0.9 fusion.41
  83.6 2.7 %pad_maximum_fusion.1 = f32[4]{0:T(128)S(1)} fusion(f32[1]{0:T(128)} %bitcast.24, f32[1]{0:T(128)} %bitcast.23, f32[1]{0:T(128)} %bitcast.22, f32[1]{0:T(128)} %bitcast.4), kind=kLoop, calls=%fused_computation.88 | loop fusion | flops 12 | bytes 32 | tf_op jit(solution)/shard_map/stack | solution.py:121
  86.4 17.9 %all_to_all.26 = f32[256,1,4]{2,1,0:T(1,128)S(1)} all-to-all(f32[256,1,4]{2,1,0:T(1,128)S(1)} %broadcast_in_dim.29), channel_id=1, replica_groups=mesh['blk'=32,'band'=8] {'blk','band'}, dimensions={0} | all-to-all | bytes 8192 | tf_op jit(solution)/shard_map/all_to_all | solution.py:130
  109.3 0.7 multiply_add_fusion
  (47 shorter events, 4.6 us)
Async XLA Ops:
  0.6 48.2 %copy-start.5 = (s32[512]{0:T(512)S(1)}, s32[512]{0:T(512)}, u32[]{:S(2)}) copy-start(s32[512]{0:T(512)} %param.19) | copy-start | bytes 6148
  0.6 51.8 %copy-start = (f32[32,64,64]{2,1,0:T(8,128)S(1)}, f32[32,64,64]{2,1,0:T(8,128)}, u32[]{:S(2)}) copy-start(f32[32,64,64]{2,1,0:T(8,128)} %param.21) | copy-start | bytes 1572868
  0.7 11.3 %all-to-all-start = ((f32[8,1,512]{2,1,0:T(1,128)}), f32[8,1,512]{2,1,0:T(1,128)S(1)}, u32[]{:S(2)}, u32[]{:S(2)}) async-start(f32[8,1,512]{2,1,0:T(1,128)} %bitcast.87), calls=%async_computation | async-start | bytes 32768 | tf_op jit(solution)/shard_map/all_to_all | solution.py:62
  11.9 44.1 %copy-start.7 = (f32[1,2,8192]{2,1,0:T(2,128)S(1)}, f32[1,2,8192]{2,1,0:T(2,128)}, u32[]{:S(2)}) copy-start(f32[1,2,8192]{2,1,0:T(2,128)} %param.20) | copy-start | bytes 196612
  15.3 33.2 %all-to-all-start.1 = ((f32[256,16,2,2]{1,3,2,0:T(2,128)}), f32[256,16,2,2]{1,3,2,0:T(2,128)S(1)}, u32[]{:S(2)}, u32[]{:S(2)}) async-start(f32[256,16,2,2]{1,3,2,0:T(2,128)} %copy.71), calls=%async_computation.1 | async-start | bytes 1048576 | tf_op jit(solution)/shard_map/all_to_all | solution.py:76
  48.7 34.0 %copy-start.1 = (f32[16,2,512]{2,1,0:T(2,128)S(1)}, f32[16,2,512]{2,1,0:T(2,128)}, u32[]{:S(2)}) copy-start(f32[16,2,512]{2,1,0:T(2,128)} %param.14) | copy-start | bytes 196612
  48.7 34.0 %copy-start.2 = (f32[16,2,512]{2,1,0:T(2,128)S(1)}, f32[16,2,512]{2,1,0:T(2,128)}, u32[]{:S(2)}) copy-start(f32[16,2,512]{2,1,0:T(2,128)} %param.13) | copy-start | bytes 196612
  48.7 34.0 %copy-start.4 = (f32[512]{0:T(512)S(1)}, f32[512]{0:T(512)}, u32[]{:S(2)}) copy-start(f32[512]{0:T(512)} %param.16) | copy-start | bytes 6148
  48.7 34.0 %copy-start.6 = (f32[512]{0:T(512)S(1)}, f32[512]{0:T(512)}, u32[]{:S(2)}) copy-start(f32[512]{0:T(512)} %param.15) | copy-start | bytes 6148
  50.3 59.0 %copy-start.3 = (f32[16,2,512]{2,1,0:T(2,128)S(1)}, f32[16,2,512]{2,1,0:T(2,128)}, u32[]{:S(2)}) copy-start(f32[16,2,512]{2,1,0:T(2,128)} %param.12) | copy-start | bytes 196612

commit v3 on v2

--- a/solution.py
+++ b/solution.py
@@ -70,9 +70,8 @@
         "sql,srl->sqr", weighted, legendre_here, preferred_element_type=jnp.float32
     )
     partial = partial.reshape(orders_dev, nband, parts, nblk, cycles_dev)
-    outgoing = partial.transpose(3, 1, 0, 2, 4).reshape(
-        nblk * nband, orders_dev, parts, cycles_dev
-    )
+    chunk = orders_dev * parts * cycles_dev
+    outgoing = partial.transpose(3, 1, 0, 2, 4).reshape(nblk * nband, chunk)
     incoming = lax.all_to_all(outgoing, EVERY, split_axis=0, concat_axis=0, tiled=True)
     cycle_coefficients = jnp.sum(
         incoming.reshape(nblk, nband, orders_dev, parts, cycles_dev), axis=1
@@ -103,10 +102,8 @@
     )
     cycle_terms = jnp.stack([real_terms, imag_terms], axis=1).astype(jnp.bfloat16)
 
-    per_owner = cycle_terms.reshape(nblk, 1, orders_dev, parts, cycles_dev)
-    returning = jnp.broadcast_to(
-        per_owner, (nblk, nband, orders_dev, parts, cycles_dev)
-    ).reshape(nblk * nband, orders_dev, parts, cycles_dev)
+    per_owner = cycle_terms.reshape(nblk, 1, chunk)
+    returning = jnp.broadcast_to(per_owner, (nblk, nband, chunk)).reshape(nblk * nband, chunk)
     arrived = lax.all_to_all(returning, EVERY, split_axis=0, concat_axis=0, tiled=True)
     mode_terms = arrived.reshape(nblk, nband, orders_dev, parts, cycles_dev)
     mode_terms = mode_terms.transpose(2, 1, 3, 0, 4).reshape(orders_dev, nband * parts, cycles_all)

time: 111 us -> 104 us (0.937)
  waiting for transfers between devices: 19.6 us -> 11.9 us
  local copies, waits for them, and re-layouts: 7.49 us -> 10.5 us
  blocking collectives: 38.8 us -> 36.3 us
    all_to_all x1, waiting for transfers between devices: 18.3 us -> 10.6 us  [per_device(): lax.all_to_all(outgoing, EVERY, split_axis=0, concat_axis=0, tiled=True)]
    all_to_all x1, blocking collectives: 20.9 us -> 18.2 us  [per_device(): lax.all_to_all(returning, EVERY, split_axis=0, concat_axis=0, tiled=True)]
    all_to_all x0 -> x3, local copies, waits for them, and re-layouts: none -> 1.35 us  [per_device(): lax.all_to_all(outgoing, EVERY, split_axis=0, concat_axis=0, tiled=True)]
where the time goes in v3:
time: 104 us; the launch traced here: 103 us
  blocking collectives  36.3 us (35%)
  starting transfers between devices  19.2 us (18%)
  waiting for transfers between devices  11.9 us (11%)
  matrix products  10.8 us (10%)
  local copies, waits for them, and re-layouts  10.5 us (10%)
  other arithmetic  9.18 us (9%)
  between operations  5.1 us (5%)
    all_to_all x1, blocking collectives, per_device(): lax.all_to_all(returning, EVERY, split_axis=0, concat_axis=0, tiled=True)  18.2 us
    all_to_all x1, blocking collectives, per_device(): lax.all_to_all(shared, EVERY, split_axis=0, concat_axis=0, tiled=True)  18.2 us
    all_to_all x1, starting transfers between devices, per_device(): lax.all_to_all(outgoing, EVERY, split_axis=0, concat_axis=0, tiled=True)  12.7 us
    all_to_all x1, waiting for transfers between devices, per_device(): lax.all_to_all(outgoing, EVERY, split_axis=0, concat_axis=0, tiled=True)  10.6 us
    all_to_all x1, starting transfers between devices, per_device(): lax.all_to_all(beam_window.reshape(nband, width), 'band', split_axis=0, c...  6.58 us
    another operation x1, other arithmetic, per_device(): jnp.stack([jnp.sum(residual * scaled_res), jnp.sum(direction * image), jn...  2.7 us
  transfers between devices with their start and end apart: 2, of which 2 were waited for; matrix products, arithmetic and copies ran while one was open for 5% of the time, Pallas kernels for 0%

profile of v3, /device:TPU:1, one launch (start us, length us, event | category | flops | bytes accessed | tf_op | source)
XLA Modules:
  0.0 103.0 jit_solution(5124026998635600980)
XLA Ops:
  0.7 6.6 %all-to-all-start = ((f32[8,1,512]{2,1,0:T(1,128)}), f32[8,1,512]{2,1,0:T(1,128)S(1)}, u32[]{:S(2)}, u32[]{:S(2)}) async-start(f32[8,1,512]{2,1,0:T(1,128)} %bitcast.85), calls=%async_computation | async-start | bytes 32768 | tf_op jit(solution)/shard_map/all_to_all | solution.py:62
  7.2 1.3 %fusion.49 = (f32[512,64]{0,1:T(8,128)S(1)}, f32[512,64]{0,1:T(8,128)S(1)}) fusion(s32[64]{0:T(128)S(1)} %iota_multiply_fusion, s32[512]{0:T(512)} %param.19), kind=kLoop, calls=%fused_computation.74 | loop fusion | flops 458752 | bytes 264448 | tf_op jit(solution)/shard_map/cos | solution.py:20
  9.2 1.0 mul.247
  10.5 1.4 %all-to-all-done = f32[8,1,512]{2,1,0:T(1,128)S(1)} async-done(((f32[8,1,512]{2,1,0:T(1,128)}), f32[8,1,512]{2,1,0:T(1,128)S(1)}, u32[]{:S(2)}, u32[]{:S(2)}) %all-to-all-start) | async-done | bytes 16416 | tf_op jit(solution)/shard_map/all_to_all | solution.py:62
  12.0 1.6 %fusion.4 = f32[16,16,64]{2,1,0:T(8,128)S(1)} fusion(bf16[16,64,4096]{2,1,0:T(8,128)(2,1)} %param.18, s32[]{:T(128)S(6)} %select_n.35, f32[16,16,512]{2,1,0:T(8,128)S(1)} %mul.248, f32[16,512]{1,0:T(8,128)S(1)} %mul.245), kind=kOutput, calls=%fused_computation.11 | convolution fusion | flops 17039360 | bytes 1671172 | tf_op jit(solution)/shard_map/sql,srl->sqr/dot_general | solution.py:69
  13.8 0.9 copy.69
  15.3 0.7 copy.70
  16.0 12.7 %all-to-all-start.1 = ((f32[256,1,64]{2,1,0:T(1,128)}), f32[256,1,64]{2,1,0:T(1,128)S(1)}, u32[]{:S(2)}, u32[]{:S(2)}) async-start(f32[256,1,64]{2,1,0:T(1,128)} %copy.70), calls=%async_computation.1 | async-start | bytes 262144 | tf_op jit(solution)/shard_map/all_to_all | solution.py:75
  29.3 1.6 %copy.74 = f32[32,64,64]{1,2,0:T(8,128)S(1)} copy(f32[32,64,64]{2,1,0:T(8,128)} %param.21) | data formatting | bytes 1048576 | tf_op args[9]
  30.9 10.6 %all-to-all-done.1 = f32[256,1,64]{2,1,0:T(1,128)S(1)} async-done(((f32[256,1,64]{2,1,0:T(1,128)}), f32[256,1,64]{2,1,0:T(1,128)S(1)}, u32[]{:S(2)}, u32[]{:S(2)}) %all-to-all-start.1) | async-done | bytes 65568 | tf_op jit(solution)/shard_map/all_to_all | solution.py:75
  42.8 1.4 %fusion.12 = f32[2,64,128]{2,1,0:T(8,128)S(1)} fusion(f32[512,64]{0,1:T(8,128)S(1)} %get-tuple-element.20, f32[512,2]{0,1:T(2,128)S(1)} %get-tuple-element.18, f32[512,64]{0,1:T(8,128)S(1)} %get-tuple-element.19, f32[512,2]{0,1:T(2,128)S(1)} %get-tuple-element.17, s32[512]{0:T(512)S(1)} %copy-done.5), kind=kOutput, calls=%fused_computation.24 | convolution fusion | flops 101777408 | bytes 337920 | tf_op jit(solution)/shard_map/mra,mb->rab/dot_general | solution.py:87
  44.3 1.4 %fusion.1 = f32[2,64,128]{2,1,0:T(8,128)S(1)} fusion(f32[2,64,128]{2,1,0:T(8,128)S(1)} %fusion.12, f32[512,64]{0,1:T(8,128)S(1)} %get-tuple-element.20, f32[512,2]{0,1:T(2,128)S(1)} %get-tuple-element.18, f32[512,64]{0,1:T(8,128)S(1)} %get-tuple-element.19, f32[512,2]{0,1:T(2,128)S(1)} %get-tuple-element.17, s32[512]{0:T(512)S(1)} %copy-done.5), kind=kOutput, calls=%fused_computation.7 | convolution fusion | flops 101810176 | bytes 403456 | tf_op jit(solution)/shard_map/mra,mb->rab/dot_general | solution.py:87
  46.5 1.0 fusion
  47.5 1.0 fusion.73
  48.7 1.2 %scatter_custom_fusion = f32[256,64]{1,0:T(8,128)S(1)} fusion(s32[128]{0:T(128)S(1)} %compare_select_fusion, f32[128,64]{1,0:T(8,128)S(1)} %copy.75, f32[]{:T(128)} %constant.17.clone.1), kind=kCustom, calls=%fused_computation.71 | custom fusion | flops 8192 | bytes 65540 | tf_op jit(solution)/shard_map/scatter-add | solution.py:36
  50.0 1.4 %convolution_bitcast_fusion = f32[512,64,2]{0,1,2:T(8,128)S(1)} fusion(s32[512]{0:T(512)S(1)} %copy-done.5, f32[2,64,128]{2,1,0:T(8,128)S(1)} %reshape.163, f32[2,64,128]{2,1,0:T(8,128)S(1)} %fusion.1, f32[1,2,64,128]{3,1,2,0:T(2,128)S(1)} %bitcast.86), kind=kOutput, calls=%fused_computation.4 | convolution fusion | flops 101613568 | bytes 460800 | tf_op jit(solution)/shard_map/rab,mb->mra/dot_general | solution.py:94
  51.4 1.5 %multiply_reduce_fusion.4 = (f32[512,2]{0,1:T(2,128)S(1)}, f32[512,2]{0,1:T(2,128)S(1)}, f32[512,2]{0,1:T(2,128)S(1)}, f32[512,2]{0,1:T(2,128)S(1)}) fusion(f32[512,64]{0,1:T(8,128)S(1)} %get-tuple-element.19, f32[512,64]{0,1:T(8,128)S(1)} %get-tuple-element.20, f32[512,64,2]{0,1,2:T(8,128)S(1)} %convolution_bitcast_fusion, ...), kind=kOutput, calls=%fused_computation.29 | convolution fusion | flops 102133760 | bytes 739328 | tf_op jit(solution)/shard_map/rab,mb->mra/dot_general | solution.py:93
  53.6 18.2 %all_to_all.33 = bf16[256,1,64]{2,1,0:T(2,128)(2,1)S(1)} all-to-all(bf16[256,1,64]{2,1,0:T(2,128)(2,1)S(1)} %copy.77), channel_id=1, replica_groups=mesh['blk'=32,'band'=8] {'blk','band'}, dimensions={0} | all-to-all | bytes 65536 | tf_op jit(solution)/shard_map/all_to_all | solution.py:107
  72.5 0.8 copy.79
  73.4 1.5 %fusion.2 = f32[16,16,512]{2,1,0:T(8,128)S(1)} fusion(bf16[16,16,64]{2,1,0:T(8,128)(2,1)S(1)} %copy.80, bf16[16,64,4096]{2,1,0:T(8,128)(2,1)} %param.18, s32[]{:T(128)S(6)} %select_n.35), kind=kOutput, calls=%fused_computation.9 | convolution fusion | flops 16777216 | bytes 1605636 | tf_op jit(solution)/shard_map/sqr,srl->sql/dot_general | solution.py:110
  75.5 0.9 fusion.41
  76.4 2.7 %pad_maximum_fusion.1 = f32[4]{0:T(128)S(1)} fusion(f32[1]{0:T(128)} %bitcast.23, f32[1]{0:T(128)} %bitcast.22, f32[1]{0:T(128)} %bitcast.21, f32[1]{0:T(128)} %bitcast.4), kind=kLoop, calls=%fused_computation.88 | loop fusion | flops 12 | bytes 32 | tf_op jit(solution)/shard_map/stack | solution.py:118
  79.1 18.2 %all_to_all.34 = f32[256,1,4]{2,1,0:T(1,128)S(1)} all-to-all(f32[256,1,4]{2,1,0:T(1,128)S(1)} %broadcast_in_dim.29), channel_id=1, replica_groups=mesh['blk'=32,'band'=8] {'blk','band'}, dimensions={0} | all-to-all | bytes 8192 | tf_op jit(solution)/shard_map/all_to_all | solution.py:127
  102.3 0.7 multiply_add_fusion
  (51 shorter events, 7.8 us)
Async XLA Ops:
  0.6 42.1 %copy-start.5 = (s32[512]{0:T(512)S(1)}, s32[512]{0:T(512)}, u32[]{:S(2)}) copy-start(s32[512]{0:T(512)} %param.19) | copy-start | bytes 6148
  0.6 45.8 %copy-start = (f32[32,64,64]{2,1,0:T(8,128)S(1)}, f32[32,64,64]{2,1,0:T(8,128)}, u32[]{:S(2)}) copy-start(f32[32,64,64]{2,1,0:T(8,128)} %param.21) | copy-start | bytes 1572868
  0.7 11.3 %all-to-all-start = ((f32[8,1,512]{2,1,0:T(1,128)}), f32[8,1,512]{2,1,0:T(1,128)S(1)}, u32[]{:S(2)}, u32[]{:S(2)}) async-start(f32[8,1,512]{2,1,0:T(1,128)} %bitcast.85), calls=%async_computation | async-start | bytes 32768 | tf_op jit(solution)/shard_map/all_to_all | solution.py:62
  16.0 25.5 %all-to-all-start.1 = ((f32[256,1,64]{2,1,0:T(1,128)}), f32[256,1,64]{2,1,0:T(1,128)S(1)}, u32[]{:S(2)}, u32[]{:S(2)}) async-start(f32[256,1,64]{2,1,0:T(1,128)} %copy.70), calls=%async_computation.1 | async-start | bytes 262144 | tf_op jit(solution)/shard_map/all_to_all | solution.py:75
  42.6 7.4 %copy-start.7 = (f32[1,2,8192]{2,1,0:T(2,128)S(1)}, f32[1,2,8192]{2,1,0:T(2,128)}, u32[]{:S(2)}) copy-start(f32[1,2,8192]{2,1,0:T(2,128)} %param.20) | copy-start | bytes 196612
  42.8 32.7 %copy-start.1 = (f32[16,2,512]{2,1,0:T(2,128)S(1)}, f32[16,2,512]{2,1,0:T(2,128)}, u32[]{:S(2)}) copy-start(f32[16,2,512]{2,1,0:T(2,128)} %param.14) | copy-start | bytes 196612
  42.8 32.7 %copy-start.2 = (f32[16,2,512]{2,1,0:T(2,128)S(1)}, f32[16,2,512]{2,1,0:T(2,128)}, u32[]{:S(2)}) copy-start(f32[16,2,512]{2,1,0:T(2,128)} %param.13) | copy-start | bytes 196612
  42.8 32.7 %copy-start.4 = (f32[512]{0:T(512)S(1)}, f32[512]{0:T(512)}, u32[]{:S(2)}) copy-start(f32[512]{0:T(512)} %param.16) | copy-start | bytes 6148
  42.8 32.7 %copy-start.6 = (f32[512]{0:T(512)S(1)}, f32[512]{0:T(512)}, u32[]{:S(2)}) copy-start(f32[512]{0:T(512)} %param.15) | copy-start | bytes 6148
  44.3 58.0 %copy-start.3 = (f32[16,2,512]{2,1,0:T(2,128)S(1)}, f32[16,2,512]{2,1,0:T(2,128)}, u32[]{:S(2)}) copy-start(f32[16,2,512]{2,1,0:T(2,128)} %param.12) | copy-start | bytes 196612

commit v4 on v3

--- a/solution.py
+++ b/solution.py
@@ -115,16 +115,17 @@
     image = prior_inverse[None, None, :] * direction + summed
     scaled_res = preconditioner[None, None, :] * residual
     scaled_image = preconditioner[None, None, :] * image
-    local_sums = jnp.stack(
-        [
-            jnp.sum(residual * scaled_res),
-            jnp.sum(direction * image),
-            jnp.sum(scaled_res * image),
-            jnp.sum(scaled_image * image),
-        ]
+    products = jnp.stack(
+        [residual * scaled_res, direction * image, scaled_res * image, scaled_image * image]
     )
+    local_sums = jnp.sum(products.reshape(products.shape[0], -1), axis=1)
     shared = jnp.broadcast_to(local_sums[None], (nblk * nband, local_sums.shape[0]))
-    totals = jnp.sum(lax.all_to_all(shared, EVERY, split_axis=0, concat_axis=0, tiled=True), axis=0)
+    arrived_sums = lax.all_to_all(shared, EVERY, split_axis=0, concat_axis=0, tiled=True)
+    totals = lax.optimization_barrier(
+        jnp.broadcast_to(
+            jnp.sum(arrived_sums, axis=0)[:, None, None, None], (local_sums.shape[0], 1, 1, width)
+        )
+    )
     norm_now = totals[0]
     step_size = norm_now / totals[1]
     norm_next = norm_now - step_size * (2.0 * totals[2] - step_size * totals[3])

time: 104 us -> 96.3 us (0.926)
  between operations: 5.1 us -> 1.05 us
  other arithmetic: 9.18 us -> 6.13 us
    another operation x1 -> x0, other arithmetic: 2.7 us -> none  [per_device(): jnp.stack([jnp.sum(residual * scaled_res), jnp.sum(direction * image), jn...]
  transfers between devices with their start and end apart: 2 -> 2, of which waited for: 2 -> 2; matrix products, arithmetic and copies ran while one was open for 5% -> 6% of each run, Pallas kernels for 0% -> 0%
where the time goes in v4:
time: 96.3 us; the launch traced here: 95.8 us
  blocking collectives  36.3 us (38%)
  starting transfers between devices  19.2 us (20%)
  waiting for transfers between devices  11.9 us (12%)
  matrix products  10.8 us (11%)
  local copies, waits for them, and re-layouts  10.3 us (11%)
  other arithmetic  6.13 us (6%)
  between operations  1.05 us (1%)
    all_to_all x1, blocking collectives, per_device(): lax.all_to_all(shared, EVERY, split_axis=0, concat_axis=0, tiled=True)  18.2 us
    all_to_all x1, blocking collectives, per_device(): lax.all_to_all(returning, EVERY, split_axis=0, concat_axis=0, tiled=True)  18.2 us
    all_to_all x1, starting transfers between devices, per_device(): lax.all_to_all(outgoing, EVERY, split_axis=0, concat_axis=0, tiled=True)  12.7 us
    all_to_all x1, waiting for transfers between devices, per_device(): lax.all_to_all(outgoing, EVERY, split_axis=0, concat_axis=0, tiled=True)  10.6 us
    all_to_all x1, starting transfers between devices, per_device(): lax.all_to_all(beam_window.reshape(nband, width), 'band', split_axis=0, c...  6.58 us
  transfers between devices with their start and end apart: 2, of which 2 were waited for; matrix products, arithmetic and copies ran while one was open for 6% of the time, Pallas kernels for 0%

profile of v4, /device:TPU:1, one launch (start us, length us, event | category | flops | bytes accessed | tf_op | source)
XLA Modules:
  0.0 95.8 jit_solution(6300179062339674678)
XLA Ops:
  0.7 6.6 %all-to-all-start = ((f32[8,1,512]{2,1,0:T(1,128)}), f32[8,1,512]{2,1,0:T(1,128)S(1)}, u32[]{:S(2)}, u32[]{:S(2)}) async-start(f32[8,1,512]{2,1,0:T(1,128)} %bitcast.81), calls=%async_computation | async-start | bytes 32768 | tf_op jit(solution)/shard_map/all_to_all | solution.py:62
  7.2 1.3 %fusion.46 = (f32[512,64]{0,1:T(8,128)S(1)}, f32[512,64]{0,1:T(8,128)S(1)}) fusion(s32[64]{0:T(128)S(1)} %iota_multiply_fusion, s32[512]{0:T(512)} %param.19), kind=kLoop, calls=%fused_computation.71 | loop fusion | flops 458752 | bytes 264448 | tf_op jit(solution)/shard_map/cos | solution.py:20
  8.5 0.7 iota_compare_fusion
  9.2 1.0 %mul.277 = f32[16,8,2,512]{3,2,1,0:T(2,128)S(1)} broadcast(f32[16,2,512]{2,1,0:T(2,128)} %param.14), dimensions={0,2,3} | broadcast | bytes 589824 | tf_op jit(solution)/shard_map/mul | solution.py:67
  10.5 1.4 %all-to-all-done = f32[8,1,512]{2,1,0:T(1,128)S(1)} async-done(((f32[8,1,512]{2,1,0:T(1,128)}), f32[8,1,512]{2,1,0:T(1,128)S(1)}, u32[]{:S(2)}, u32[]{:S(2)}) %all-to-all-start) | async-done | bytes 16416 | tf_op jit(solution)/shard_map/all_to_all | solution.py:62
  12.0 1.6 %fusion.4 = f32[16,16,64]{2,1,0:T(8,128)S(1)} fusion(bf16[16,64,4096]{2,1,0:T(8,128)(2,1)} %param.18, s32[]{:T(128)S(6)} %select_n.35, f32[16,16,512]{2,1,0:T(8,128)S(1)} %mul.278, f32[16,512]{1,0:T(8,128)S(1)} %mul.275), kind=kOutput, calls=%fused_computation.11 | convolution fusion | flops 17039360 | bytes 1671172 | tf_op jit(solution)/shard_map/sql,srl->sqr/dot_general | solution.py:69
  13.8 0.9 copy.69
  15.3 0.7 copy.70
  16.0 12.7 %all-to-all-start.1 = ((f32[256,1,64]{2,1,0:T(1,128)}), f32[256,1,64]{2,1,0:T(1,128)S(1)}, u32[]{:S(2)}, u32[]{:S(2)}) async-start(f32[256,1,64]{2,1,0:T(1,128)} %copy.70), calls=%async_computation.1 | async-start | bytes 262144 | tf_op jit(solution)/shard_map/all_to_all | solution.py:75
  28.7 0.7 compare_select_fusion
  29.3 1.6 %copy.74 = f32[32,64,64]{1,2,0:T(8,128)S(1)} copy(f32[32,64,64]{2,1,0:T(8,128)} %param.21) | data formatting | bytes 1048576 | tf_op args[9]
  30.9 10.6 %all-to-all-done.1 = f32[256,1,64]{2,1,0:T(1,128)S(1)} async-done(((f32[256,1,64]{2,1,0:T(1,128)}), f32[256,1,64]{2,1,0:T(1,128)S(1)}, u32[]{:S(2)}, u32[]{:S(2)}) %all-to-all-start.1) | async-done | bytes 65568 | tf_op jit(solution)/shard_map/all_to_all | solution.py:75
  42.8 1.4 %fusion.12 = f32[2,64,128]{2,1,0:T(8,128)S(1)} fusion(f32[512,64]{0,1:T(8,128)S(1)} %get-tuple-element.26, f32[512,2]{0,1:T(2,128)S(1)} %get-tuple-element.24, f32[512,64]{0,1:T(8,128)S(1)} %get-tuple-element.25, f32[512,2]{0,1:T(2,128)S(1)} %get-tuple-element.23, s32[512]{0:T(512)S(1)} %copy-done.5), kind=kOutput, calls=%fused_computation.25 | convolution fusion | flops 101777408 | bytes 337920 | tf_op jit(solution)/shard_map/mra,mb->rab/dot_general | solution.py:87
  44.3 1.4 %fusion.1 = f32[2,64,128]{2,1,0:T(8,128)S(1)} fusion(f32[2,64,128]{2,1,0:T(8,128)S(1)} %fusion.12, f32[512,64]{0,1:T(8,128)S(1)} %get-tuple-element.26, f32[512,2]{0,1:T(2,128)S(1)} %get-tuple-element.24, f32[512,64]{0,1:T(8,128)S(1)} %get-tuple-element.25, f32[512,2]{0,1:T(2,128)S(1)} %get-tuple-element.23, s32[512]{0:T(512)S(1)} %copy-done.5), kind=kOutput, calls=%fused_computation.7 | convolution fusion | flops 101810176 | bytes 403456 | tf_op jit(solution)/shard_map/mra,mb->rab/dot_general | solution.py:87
  46.5 1.0 %fusion = f32[128,64]{0,1:T(8,128)S(1)} fusion(f32[32,64,64]{2,1,0:T(8,128)S(1)} %copy-done, pred[128,32]{0,1:T(8,128)(4,1)S(1)} %iota_compare_fusion, f32[128,64]{1,0:T(8,128)S(1)} %gather_fusion), kind=kOutput, calls=%fused_computation.3 | convolution fusion | flops 201842688 | bytes 593920 | tf_op jit(solution)/shard_map/kij,tj->tki/dot_general | solution.py:32
  47.5 1.0 %fusion.71 = f32[128,2048]{0,1:S(1)} fusion(f32[128,64]{0,1:T(8,128)S(1)} %fusion, f32[64,2048]{0,1:T(8,128)S(1)} %bitcast.74), kind=kOutput, calls=%fused_computation.108 | convolution fusion | flops 201326592 | bytes 1605632
  48.7 1.2 %scatter_custom_fusion = f32[256,64]{1,0:T(8,128)S(1)} fusion(s32[128]{0:T(128)S(1)} %compare_select_fusion, f32[128,64]{1,0:T(8,128)S(1)} %copy.75, f32[]{:T(128)} %constant.46.clone.1), kind=kCustom, calls=%fused_computation.68 | custom fusion | flops 8192 | bytes 65540 | tf_op jit(solution)/shard_map/scatter-add | solution.py:36
  50.0 1.4 %convolution_bitcast_fusion = f32[512,64,2]{0,1,2:T(8,128)S(1)} fusion(s32[512]{0:T(512)S(1)} %copy-done.5, f32[2,64,128]{2,1,0:T(8,128)S(1)} %reshape.225, f32[2,64,128]{2,1,0:T(8,128)S(1)} %fusion.1, f32[1,2,64,128]{3,1,2,0:T(2,128)S(1)} %bitcast.86), kind=kOutput, calls=%fused_computation.4 | convolution fusion | flops 101613568 | bytes 460800 | tf_op jit(solution)/shard_map/rab,mb->mra/dot_general | solution.py:94
  51.4 1.5 %multiply_reduce_fusion.4 = (f32[512,2]{0,1:T(2,128)S(1)}, f32[512,2]{0,1:T(2,128)S(1)}, f32[512,2]{0,1:T(2,128)S(1)}, f32[512,2]{0,1:T(2,128)S(1)}) fusion(f32[512,64]{0,1:T(8,128)S(1)} %get-tuple-element.25, f32[512,64]{0,1:T(8,128)S(1)} %get-tuple-element.26, f32[512,64,2]{0,1,2:T(8,128)S(1)} %convolution_bitcast_fusion, ...), kind=kOutput, calls=%fused_computation.30 | convolution fusion | flops 102133760 | bytes 739328 | tf_op jit(solution)/shard_map/rab,mb->mra/dot_general | solution.py:93
  53.6 18.2 %all_to_all.33 = bf16[256,1,64]{2,1,0:T(2,128)(2,1)S(1)} all-to-all(bf16[256,1,64]{2,1,0:T(2,128)(2,1)S(1)} %copy.77), channel_id=1, replica_groups=mesh['blk'=32,'band'=8] {'blk','band'}, dimensions={0} | all-to-all | bytes 65536 | tf_op jit(solution)/shard_map/all_to_all | solution.py:107
  72.5 0.8 copy.79
  73.4 1.5 %fusion.2 = f32[16,16,512]{2,1,0:T(8,128)S(1)} fusion(bf16[16,16,64]{2,1,0:T(8,128)(2,1)S(1)} %copy.80, bf16[16,64,4096]{2,1,0:T(8,128)(2,1)} %param.18, s32[]{:T(128)S(6)} %select_n.35), kind=kOutput, calls=%fused_computation.9 | convolution fusion | flops 16777216 | bytes 1605636 | tf_op jit(solution)/shard_map/sqr,srl->sql/dot_general | solution.py:110
  76.5 18.2 %all_to_all.34 = f32[256,1,4]{2,1,0:T(1,128)S(1)} all-to-all(f32[256,1,4]{2,1,0:T(1,128)S(1)} %broadcast_in_dim.31), channel_id=1, replica_groups=mesh['blk'=32,'band'=8] {'blk','band'}, dimensions={0} | all-to-all | bytes 8192 | tf_op jit(solution)/shard_map/all_to_all | solution.py:123
  95.1 0.7 multiply_add_fusion
  (58 shorter events, 6.9 us)
Async XLA Ops:
  0.6 42.1 %copy-start.5 = (s32[512]{0:T(512)S(1)}, s32[512]{0:T(512)}, u32[]{:S(2)}) copy-start(s32[512]{0:T(512)} %param.19) | copy-start | bytes 6148
  0.6 45.8 %copy-start = (f32[32,64,64]{2,1,0:T(8,128)S(1)}, f32[32,64,64]{2,1,0:T(8,128)}, u32[]{:S(2)}) copy-start(f32[32,64,64]{2,1,0:T(8,128)} %param.21) | copy-start | bytes 1572868
  0.7 11.3 %all-to-all-start = ((f32[8,1,512]{2,1,0:T(1,128)}), f32[8,1,512]{2,1,0:T(1,128)S(1)}, u32[]{:S(2)}, u32[]{:S(2)}) async-start(f32[8,1,512]{2,1,0:T(1,128)} %bitcast.81), calls=%async_computation | async-start | bytes 32768 | tf_op jit(solution)/shard_map/all_to_all | solution.py:62
  16.0 25.5 %all-to-all-start.1 = ((f32[256,1,64]{2,1,0:T(1,128)}), f32[256,1,64]{2,1,0:T(1,128)S(1)}, u32[]{:S(2)}, u32[]{:S(2)}) async-start(f32[256,1,64]{2,1,0:T(1,128)} %copy.70), calls=%async_computation.1 | async-start | bytes 262144 | tf_op jit(solution)/shard_map/all_to_all | solution.py:75
  42.6 7.4 %copy-start.7 = (f32[1,2,8192]{2,1,0:T(2,128)S(1)}, f32[1,2,8192]{2,1,0:T(2,128)}, u32[]{:S(2)}) copy-start(f32[1,2,8192]{2,1,0:T(2,128)} %param.20) | copy-start | bytes 196612
  42.8 32.7 %copy-start.1 = (f32[16,2,512]{2,1,0:T(2,128)S(1)}, f32[16,2,512]{2,1,0:T(2,128)}, u32[]{:S(2)}) copy-start(f32[16,2,512]{2,1,0:T(2,128)} %param.14) | copy-start | bytes 196612
  42.8 32.7 %copy-start.6 = (f32[512]{0:T(512)S(1)}, f32[512]{0:T(512)}, u32[]{:S(2)}) copy-start(f32[512]{0:T(512)} %param.15) | copy-start | bytes 6148
  44.2 31.4 %copy-start.2 = (f32[16,2,512]{2,1,0:T(2,128)S(1)}, f32[16,2,512]{2,1,0:T(2,128)}, u32[]{:S(2)}) copy-start(f32[16,2,512]{2,1,0:T(2,128)} %param.13) | copy-start | bytes 196612
  44.2 31.4 %copy-start.4 = (f32[512]{0:T(512)S(1)}, f32[512]{0:T(512)}, u32[]{:S(2)}) copy-start(f32[512]{0:T(512)} %param.16) | copy-start | bytes 6148
  45.7 49.4 %copy-start.3 = (f32[16,2,512]{2,1,0:T(2,128)S(1)}, f32[16,2,512]{2,1,0:T(2,128)}, u32[]{:S(2)}) copy-start(f32[16,2,512]{2,1,0:T(2,128)} %param.12) | copy-start | bytes 196612

commit v5 on v4

--- a/solution.py
+++ b/solution.py
@@ -84,14 +84,18 @@
     imag_part = cycle_coefficients[:, 1, :, None]
     upper_part = real_part * outer_cos[:, None, :] - imag_part * outer_sin[:, None, :]
     lower_part = real_part * outer_sin[:, None, :] + imag_part * outer_cos[:, None, :]
-    pixel_grid = jnp.einsum("mra,mb->rab", upper_part, inner_cos, precision=precise) - jnp.einsum(
-        "mra,mb->rab", lower_part, inner_sin, precision=precise
+    inner_both = jnp.concatenate([inner_cos, inner_sin], axis=0)
+    pixel_grid = jnp.einsum(
+        "mra,mb->rab",
+        jnp.concatenate([upper_part, -lower_part], axis=0),
+        inner_both,
+        precision=precise,
     )
     pixels = norm_scale * pixel_grid.reshape(cycle_count, NPHI)
     noisy = noise_weight[0] * pixels + smooth(pixels, smoother_blocks, tile_slots, tile_kinds)
     noisy_grid = noisy.reshape(cycle_count, NPHI // 128, 128)
-    cos_sums = jnp.einsum("rab,mb->mra", noisy_grid, inner_cos, precision=precise)
-    sin_sums = jnp.einsum("rab,mb->mra", noisy_grid, inner_sin, precision=precise)
+    both_sums = jnp.einsum("rab,mb->mra", noisy_grid, inner_both, precision=precise)
+    cos_sums, sin_sums = both_sums[:order_count], both_sums[order_count:]
     real_terms = norm_scale * (
         jnp.einsum("mra,ma->mr", cos_sums, outer_cos, precision=precise)
         - jnp.einsum("mra,ma->mr", sin_sums, outer_sin, precision=precise)

time: 96.3 us -> 103 us (1.070)
  other arithmetic: 6.13 us -> 12.9 us
  matrix products: 10.8 us -> 8.91 us
  starting transfers between devices: 19.2 us -> 20.6 us
  local copies, waits for them, and re-layouts: 10.3 us -> 11.5 us
    cos x1 -> x2, other arithmetic: 1.27 us -> 4.5 us  [phases(): return (jnp.cos(angles), jnp.sin(angles))]
    dot_general x4 -> x2, matrix products: 5.75 us -> 3.18 us  [the longest x1 1.62 us: per_device(): jnp.einsum('mra,mb->rab', jnp.concatenate([upper_part, -lower_part], axis...]
    all_to_all x1, waiting for transfers between devices: 1.38 us -> 0.01 us  [per_device(): lax.all_to_all(beam_window.reshape(nband, width), 'band', split_axis=0, c...]
    all_to_all x1, starting transfers between devices: 12.7 us -> 14 us  [per_device(): lax.all_to_all(outgoing, EVERY, split_axis=0, concat_axis=0, tiled=True)]
    unnamed x18, local copies, waits for them, and re-layouts: 1.61 us -> 0.37 us
  transfers between devices with their start and end apart: 2 -> 2, of which waited for: 2 -> 1; matrix products, arithmetic and copies ran while one was open for 6% -> 8% of each run, Pallas kernels for 0% -> 0%
where the time goes in v5:
time: 103 us
  blocking collectives  36.6 us (36%)
  starting transfers between devices  20.6 us (20%)
  other arithmetic  12.9 us (13%)
  local copies, waits for them, and re-layouts  11.5 us (11%)
  waiting for transfers between devices  11.2 us (11%)
  matrix products  8.91 us (9%)
    all_to_all x1, blocking collectives, per_device(): lax.all_to_all(returning, EVERY, split_axis=0, concat_axis=0, tiled=True)  18.4 us
    all_to_all x1, blocking collectives, per_device(): lax.all_to_all(shared, EVERY, split_axis=0, concat_axis=0, tiled=True)  18.2 us
    all_to_all x1, starting transfers between devices, per_device(): lax.all_to_all(outgoing, EVERY, split_axis=0, concat_axis=0, tiled=True)  14 us
    all_to_all x1, waiting for transfers between devices, per_device(): lax.all_to_all(outgoing, EVERY, split_axis=0, concat_axis=0, tiled=True)  11.2 us
    all_to_all x1, starting transfers between devices, per_device(): lax.all_to_all(beam_window.reshape(nband, width), 'band', split_axis=0, c...  6.58 us
    cos x2, other arithmetic, phases(): return (jnp.cos(angles), jnp.sin(angles))  4.5 us
  transfers between devices with their start and end apart: 2, of which 1 were waited for; matrix products, arithmetic and copies ran while one was open for 8% of the time, Pallas kernels for 0%

profile of v5, /device:TPU:1, one launch (start us, length us, event | category | flops | bytes accessed | tf_op | source)
XLA Modules:
  0.0 102.7 jit_solution(6740428729805924444)
XLA Ops:
  0.6 6.6 %all-to-all-start = ((f32[8,1,512]{2,1,0:T(1,128)}), f32[8,1,512]{2,1,0:T(1,128)S(1)}, u32[]{:S(2)}, u32[]{:S(2)}) async-start(f32[8,1,512]{2,1,0:T(1,128)} %bitcast.79), calls=%async_computation | async-start | bytes 32768 | tf_op jit(solution)/shard_map/all_to_all | solution.py:62
  7.2 2.6 %fusion.20 = (f32[512,128]{1,0:T(8,128)S(1)}, f32[512,128]{1,0:T(8,128)}) fusion(s32[512]{0:T(512)} %param.19), kind=kLoop, calls=%fused_computation.45 | loop fusion | flops 917504 | bytes 526336 | tf_op jit(solution)/shard_map/cos | solution.py:20
  9.8 1.9 %fusion.28 = (f32[512,64]{0,1:T(8,128)S(1)}, f32[512,64]{0,1:T(8,128)}) fusion(s32[64]{0:T(128)S(1)} %iota_multiply_fusion, s32[512]{0:T(512)} %param.19), kind=kLoop, calls=%fused_computation.59 | loop fusion | flops 458752 | bytes 264448 | tf_op jit(solution)/shard_map/cos | solution.py:20
  11.7 1.3 %iota_compare_fusion = pred[128,32]{0,1:T(8,128)(4,1)} fusion(s32[128]{0:T(128)} %param.23), kind=kLoop, calls=%fused_computation.63 | loop fusion | flops 4096 | bytes 4608 | tf_op jit(solution)/shard_map/eq | solution.py:25
  13.0 1.0 mul.277
  14.4 1.6 %fusion.3 = f32[16,16,64]{2,1,0:T(8,128)S(1)} fusion(bf16[16,64,4096]{2,1,0:T(8,128)(2,1)} %param.18, s32[]{:T(128)S(6)} %select_n.35, f32[16,16,512]{2,1,0:T(8,128)S(1)} %mul.278, f32[16,512]{1,0:T(8,128)S(1)} %mul.275), kind=kOutput, calls=%fused_computation.8 | convolution fusion | flops 17039360 | bytes 1671172 | tf_op jit(solution)/shard_map/sql,srl->sqr/dot_general | solution.py:69
  16.2 0.9 copy.69
  18.5 14.0 %all-to-all-start.1 = ((f32[256,1,64]{2,1,0:T(1,128)}), f32[256,1,64]{2,1,0:T(1,128)S(1)}, u32[]{:S(2)}, u32[]{:S(2)}) async-start(f32[256,1,64]{2,1,0:T(1,128)} %copy.70), calls=%async_computation.1 | async-start | bytes 262144 | tf_op jit(solution)/shard_map/all_to_all | solution.py:75
  34.1 11.2 %all-to-all-done.1 = f32[256,1,64]{2,1,0:T(1,128)S(1)} async-done(((f32[256,1,64]{2,1,0:T(1,128)}), f32[256,1,64]{2,1,0:T(1,128)S(1)}, u32[]{:S(2)}, u32[]{:S(2)}) %all-to-all-start.1) | async-done | bytes 65568 | tf_op jit(solution)/shard_map/all_to_all | solution.py:75
  46.0 1.4 %reshape.223 = f32[32,8,16,2,2]{1,0,4,3,2:T(8,128)S(1)} reshape(f32[256,1,64]{0,2,1:T(8,128)} %copy.71) | data formatting | bytes 131072 | tf_op jit(solution)/shard_map/reshape | solution.py:77
  47.4 1.0 reduce_sum.54
  48.5 0.9 copy.72
  49.5 1.0 multiply_subtract_fusion
  50.5 1.6 %convolution_multiply_fusion = f32[2,64,128]{2,1,0:T(8,128)S(1)} fusion(f32[512,2,64]{0,2,1:T(8,128)S(1)} %get-tuple-element.16, f32[512,2,64]{0,2,1:T(8,128)S(1)} %get-tuple-element.15, f32[512,128]{1,0:T(8,128)} %get-tuple-element.30, f32[512,128]{1,0:T(8,128)S(1)} %get-tuple-element.29), kind=kOutput, calls=%fused_computation.4 | convolution fusion | flops 201605120 | bytes 1114112 | tf_op jit(solution)/shard_map/mra,mb->rab/dot_general | solution.py:88
  52.2 0.8 gather_fusion
  52.9 1.7 %fusion = f32[128,64]{0,1:T(8,128)S(1)} fusion(f32[32,64,64]{2,1,0:T(8,128)S(1)} %copy-done, pred[128,32]{0,1:T(8,128)(4,1)} %iota_compare_fusion, f32[128,64]{1,0:T(8,128)S(1)} %gather_fusion), kind=kOutput, calls=%fused_computation.3 | convolution fusion | flops 201842688 | bytes 593920 | tf_op jit(solution)/shard_map/kij,tj->tki/dot_general | solution.py:32
  54.6 1.0 fusion.37
  55.6 0.8 select_reduce_fusion
  56.5 1.2 %scatter_custom_fusion = f32[256,64]{1,0:T(8,128)S(1)} fusion(s32[128]{0:T(128)} %copy-done.7, f32[128,64]{1,0:T(8,128)S(1)} %copy.75, f32[]{:T(128)} %constant.46.clone.1), kind=kCustom, calls=%fused_computation.56 | custom fusion | flops 8192 | bytes 66048 | tf_op jit(solution)/shard_map/scatter-add | solution.py:36
  57.8 1.6 %fusion.8 = f32[1024,2,64]{0,2,1:T(8,128)S(1)} fusion(f32[512,128]{1,0:T(8,128)} %get-tuple-element.30, f32[512,128]{1,0:T(8,128)S(1)} %get-tuple-element.29, f32[2,64,128]{2,1,0:T(8,128)S(1)} %reshape.225, f32[2,64,128]{2,1,0:T(8,128)S(1)} %convolution_multiply_fusion, f32[1,2,64,128]{3,1,2,0:T(2,128)} %bitcast.78), kind=kOutput, calls=%fused_computation.16 | convolution fusion | flops 201490432 | bytes 1245184 | tf_op jit(solution)/shard_map/rab,mb->mra/dot_general | solution.py:97
  60.2 18.4 %all_to_all.33 = bf16[256,1,64]{2,1,0:T(2,128)(2,1)S(1)} all-to-all(bf16[256,1,64]{2,1,0:T(2,128)(2,1)S(1)} %copy.77), channel_id=1, replica_groups=mesh['blk'=32,'band'=8] {'blk','band'}, dimensions={0} | all-to-all | bytes 65536 | tf_op jit(solution)/shard_map/all_to_all | solution.py:111
  79.3 0.8 copy.79
  80.3 1.5 %fusion.1 = f32[16,16,512]{2,1,0:T(8,128)S(1)} fusion(bf16[16,16,64]{2,1,0:T(8,128)(2,1)S(1)} %copy.80, bf16[16,64,4096]{2,1,0:T(8,128)(2,1)} %param.18, s32[]{:T(128)S(6)} %select_n.35), kind=kOutput, calls=%fused_computation.6 | convolution fusion | flops 16777216 | bytes 1605636 | tf_op jit(solution)/shard_map/sqr,srl->sql/dot_general | solution.py:114
  83.4 18.2 %all_to_all.34 = f32[256,1,4]{2,1,0:T(1,128)S(1)} all-to-all(f32[256,1,4]{2,1,0:T(1,128)S(1)} %broadcast_in_dim.31), channel_id=1, replica_groups=mesh['blk'=32,'band'=8] {'blk','band'}, dimensions={0} | all-to-all | bytes 8192 | tf_op jit(solution)/shard_map/all_to_all | solution.py:127
  (59 shorter events, 8.9 us)
Async XLA Ops:
  0.6 32.5 %copy-start = (f32[32,64,64]{2,1,0:T(8,128)S(1)}, f32[32,64,64]{2,1,0:T(8,128)}, u32[]{:S(2)}) copy-start(f32[32,64,64]{2,1,0:T(8,128)} %param.21) | copy-start | bytes 1572868
  0.6 13.7 %all-to-all-start = ((f32[8,1,512]{2,1,0:T(1,128)}), f32[8,1,512]{2,1,0:T(1,128)S(1)}, u32[]{:S(2)}, u32[]{:S(2)}) async-start(f32[8,1,512]{2,1,0:T(1,128)} %bitcast.79), calls=%async_computation | async-start | bytes 32768 | tf_op jit(solution)/shard_map/all_to_all | solution.py:62
  18.5 26.8 %all-to-all-start.1 = ((f32[256,1,64]{2,1,0:T(1,128)}), f32[256,1,64]{2,1,0:T(1,128)S(1)}, u32[]{:S(2)}, u32[]{:S(2)}) async-start(f32[256,1,64]{2,1,0:T(1,128)} %copy.70), calls=%async_computation.1 | async-start | bytes 262144 | tf_op jit(solution)/shard_map/all_to_all | solution.py:75
  33.2 12.1 %copy-start.7 = (s32[128]{0:T(128)}, s32[128]{0:T(128)S(1)}, u32[]{:S(2)}) copy-start(s32[128]{0:T(128)S(1)} %compare_select_fusion) | copy-start | bytes 1540
  48.5 10.9 %copy-start.1 = (f32[512,64]{0,1:T(8,128)S(1)}, f32[512,64]{0,1:T(8,128)}, u32[]{:S(2)}) copy-start(f32[512,64]{0,1:T(8,128)} %get-tuple-element.28) | copy-start | bytes 393220
  48.5 33.8 %copy-start.2 = (f32[16,2,512]{2,1,0:T(2,128)S(1)}, f32[16,2,512]{2,1,0:T(2,128)}, u32[]{:S(2)}) copy-start(f32[16,2,512]{2,1,0:T(2,128)} %param.14) | copy-start | bytes 196612
  48.5 33.8 %copy-start.6 = (f32[512]{0:T(512)S(1)}, f32[512]{0:T(512)}, u32[]{:S(2)}) copy-start(f32[512]{0:T(512)} %param.15) | copy-start | bytes 6148
  48.5 34.0 %copy-start.3 = (f32[16,2,512]{2,1,0:T(2,128)S(1)}, f32[16,2,512]{2,1,0:T(2,128)}, u32[]{:S(2)}) copy-start(f32[16,2,512]{2,1,0:T(2,128)} %param.13) | copy-start | bytes 196612
  48.5 34.0 %copy-start.5 = (f32[512]{0:T(512)S(1)}, f32[512]{0:T(512)}, u32[]{:S(2)}) copy-start(f32[512]{0:T(512)} %param.16) | copy-start | bytes 6148
  50.4 51.5 %copy-start.4 = (f32[16,2,512]{2,1,0:T(2,128)S(1)}, f32[16,2,512]{2,1,0:T(2,128)}, u32[]{:S(2)}) copy-start(f32[16,2,512]{2,1,0:T(2,128)} %param.12) | copy-start | bytes 196612

commit v6 on v4

--- a/solution.py
+++ b/solution.py
@@ -72,14 +72,28 @@
     partial = partial.reshape(orders_dev, nband, parts, nblk, cycles_dev)
     chunk = orders_dev * parts * cycles_dev
     outgoing = partial.transpose(3, 1, 0, 2, 4).reshape(nblk * nband, chunk)
+    outer_cos, outer_sin = phases(mode_orders, NPHI // 128, 128)
+    inner_cos, inner_sin = phases(mode_orders, 128, 1)
+    outgoing, outer_cos, outer_sin, inner_cos, inner_sin = lax.optimization_barrier(
+        (outgoing, outer_cos, outer_sin, inner_cos, inner_sin)
+    )
     incoming = lax.all_to_all(outgoing, EVERY, split_axis=0, concat_axis=0, tiled=True)
+    (
+        incoming, outer_cos, outer_sin, inner_cos, inner_sin, tile_slots, tile_kinds,
+        smoother_blocks, noise_weight, solution, residual, direction, prior_inverse,
+        preconditioner, legendre_here, beam_here,
+    ) = lax.optimization_barrier(
+        (
+            incoming, outer_cos, outer_sin, inner_cos, inner_sin, tile_slots, tile_kinds,
+            smoother_blocks, noise_weight, solution, residual, direction, prior_inverse,
+            preconditioner, legendre_here, beam_here,
+        )
+    )
     cycle_coefficients = jnp.sum(
         incoming.reshape(nblk, nband, orders_dev, parts, cycles_dev), axis=1
     ).reshape(order_count, parts, cycles_dev)
 
     cycle_count = cycles_dev
-    outer_cos, outer_sin = phases(mode_orders, NPHI // 128, 128)
-    inner_cos, inner_sin = phases(mode_orders, 128, 1)
     real_part = cycle_coefficients[:, 0, :, None]
     imag_part = cycle_coefficients[:, 1, :, None]
     upper_part = real_part * outer_cos[:, None, :] - imag_part * outer_sin[:, None, :]

time: 96.3 us -> 110 us (1.14)
  blocking collectives: 36.3 us -> 62.5 us
  starting transfers between devices: 19.2 us -> 7.17 us
  waiting for transfers between devices: 11.9 us -> 0.01 us
  local copies, waits for them, and re-layouts: 10.3 us -> 17.3 us
  other arithmetic: 6.13 us -> 11.7 us
  matrix products: 10.8 us -> 9.09 us
    all_to_all x0 -> x1, blocking collectives: none -> 26 us  [per_device(): lax.all_to_all(outgoing, EVERY, split_axis=0, concat_axis=0, tiled=True)]
    all_to_all x1 -> x0, starting transfers between devices: 12.7 us -> none  [per_device(): lax.all_to_all(outgoing, EVERY, split_axis=0, concat_axis=0, tiled=True)]
    all_to_all x1 -> x0, waiting for transfers between devices: 10.6 us -> none  [per_device(): lax.all_to_all(outgoing, EVERY, split_axis=0, concat_axis=0, tiled=True)]
    sin x0 -> x2, other arithmetic: none -> 4.46 us  [phases(): return (jnp.cos(angles), jnp.sin(angles))]
    all_to_all x1, waiting for transfers between devices: 1.38 us -> 0.01 us  [per_device(): lax.all_to_all(beam_window.reshape(nband, width), 'band', split_axis=0, c...]
    dynamic_slice x0 -> x1, local copies, waits for them, and re-layouts: none -> 1.36 us  [per_device(): legendre_here = lax.dynamic_slice_in_dim(legendre, band * width, width, 2)]
    cos x1 -> x0, other arithmetic: 1.27 us -> none  [phases(): return (jnp.cos(angles), jnp.sin(angles))]
    dot_general x1, matrix products: 1.49 us -> 0.25 us  [per_device(): jnp.einsum('sqr,srl->sql', mode_terms, legendre_here, preferred_element_t...]
  transfers between devices with their start and end apart: 2 -> 1, of which waited for: 2 -> 0; matrix products, arithmetic and copies ran while one was open for 6% -> 7% of each run, Pallas kernels for 0% -> 0%
where the time goes in v6:
time: 110 us; the launch traced here: 109 us
  blocking collectives  62.5 us (57%)
  local copies, waits for them, and re-layouts  17.3 us (16%)
  other arithmetic  11.7 us (11%)
  matrix products  9.09 us (8%)
  starting transfers between devices  7.17 us (7%)
    all_to_all x1, blocking collectives, per_device(): lax.all_to_all(outgoing, EVERY, split_axis=0, concat_axis=0, tiled=True)  26 us
    all_to_all x1, blocking collectives, per_device(): lax.all_to_all(returning, EVERY, split_axis=0, concat_axis=0, tiled=True)  18.3 us
    all_to_all x1, blocking collectives, per_device(): lax.all_to_all(shared, EVERY, split_axis=0, concat_axis=0, tiled=True)  18.2 us
    all_to_all x1, starting transfers between devices, per_device(): lax.all_to_all(beam_window.reshape(nband, width), 'band', split_axis=0, c...  7.17 us
    sin x2, other arithmetic, phases(): return (jnp.cos(angles), jnp.sin(angles))  4.46 us
  transfers between devices with their start and end apart: 1, of which 0 were waited for; matrix products, arithmetic and copies ran while one was open for 7% of the time, Pallas kernels for 0%

profile of v6, /device:TPU:1, one launch (start us, length us, event | category | flops | bytes accessed | tf_op | source)
XLA Modules:
  0.0 108.9 jit_solution(4630226785234866616)
XLA Ops:
  0.6 7.2 %all-to-all-start = ((f32[8,1,512]{2,1,0:T(1,128)}), f32[8,1,512]{2,1,0:T(1,128)}, u32[]{:S(2)}, u32[]{:S(2)}) async-start(f32[8,1,512]{2,1,0:T(1,128)} %bitcast.89), calls=%async_computation | async-start | bytes 32768 | tf_op jit(solution)/shard_map/all_to_all | solution.py:62
  7.8 2.5 %fusion.32 = (f32[512,128]{1,0:T(8,128)}, f32[512,128]{1,0:T(8,128)S(1)}) fusion(s32[512]{0:T(512)} %param.19), kind=kLoop, calls=%fused_computation.54 | loop fusion | flops 917504 | bytes 526336 | tf_op jit(solution)/shard_map/sin | solution.py:20
  10.4 1.9 %fusion.38 = (f32[512,64]{0,1:T(8,128)S(1)}, f32[512,64]{0,1:T(8,128)}) fusion(s32[64]{0:T(128)S(1)} %iota_multiply_fusion, s32[512]{0:T(512)} %param.19), kind=kLoop, calls=%fused_computation.68 | loop fusion | flops 458752 | bytes 264448 | tf_op jit(solution)/shard_map/sin | solution.py:20
  12.3 1.4 %constant_dynamic-slice_fusion = bf16[16,64,512]{2,1,0:T(8,128)(2,1)S(1)} fusion(bf16[16,64,4096]{2,1,0:T(8,128)(2,1)} %param.18, s32[]{:T(128)S(6)} %select_n.27), kind=kLoop, calls=%fused_computation.85 | loop fusion | bytes 2097156 | tf_op jit(solution)/shard_map/dynamic_slice | solution.py:65
  13.6 1.0 mul.252
  16.1 1.0 copy.68
  17.2 1.9 %copy.69 = f32[32,8,16,2,2]{1,0,4,3,2:T(8,128)S(1)} copy(f32[32,8,16,2,2]{2,4,0,3,1:T(2,128)} %bitcast.80) | data formatting | bytes 131072 | tf_op jit(solution)/shard_map/transpose | solution.py:74
  19.1 1.2 %reshape.170 = f32[256,64]{0,1:T(8,128)} reshape(f32[32,8,16,2,2]{1,0,4,3,2:T(8,128)S(1)} %copy.69) | data formatting | bytes 131072 | tf_op jit(solution)/shard_map/reshape | solution.py:74
  20.3 0.9 copy.70
  21.2 26.0 %all_to_all.36 = f32[256,1,64]{2,1,0:T(1,128)S(1)} all-to-all(f32[256,1,64]{2,1,0:T(1,128)S(1)} %copy.70), channel_id=1, replica_groups=mesh['blk'=32,'band'=8] {'blk','band'}, dimensions={0} | all-to-all | bytes 131072 | tf_op jit(solution)/shard_map/all_to_all | solution.py:80
  47.9 1.3 %iota_compare_fusion = pred[128,32]{0,1:T(8,128)(4,1)} fusion(s32[128]{0:T(128)} %param.23), kind=kLoop, calls=%fused_computation.72 | loop fusion | flops 4096 | bytes 4608 | tf_op jit(solution)/shard_map/eq | solution.py:25
  50.5 1.4 %reshape.171 = f32[32,8,16,2,2]{1,0,4,3,2:T(8,128)S(1)} reshape(f32[256,64]{0,1:T(8,128)} %copy.71) | data formatting | bytes 131072 | tf_op jit(solution)/shard_map/reshape | solution.py:93
  51.9 1.0 reduce_sum.54
  52.9 0.8 copy.72
  53.9 1.3 %fusion.9 = f32[2,64,128]{2,1,0:T(8,128)S(1)} fusion(f32[512,128]{1,0:T(8,128)S(1)} %get-tuple-element.35, f32[512,64]{0,1:T(8,128)S(1)} %get-tuple-element.39, f32[512,2]{0,1:T(2,128)S(1)} %get-tuple-element.66, f32[512,64]{0,1:T(8,128)} %get-tuple-element.38, f32[512,2]{0,1:T(2,128)S(1)} %get-tuple-element.65), kind=kOutput, calls=%fused_computation.22 | convolution fusion | flops 100859904 | bytes 598016 | tf_op jit(solution)/shard_map/mra,mb->rab/dot_general | solution.py:101
  55.2 1.4 %fusion.1 = f32[2,64,128]{2,1,0:T(8,128)S(1)} fusion(f32[2,64,128]{2,1,0:T(8,128)S(1)} %fusion.9, f32[512,128]{1,0:T(8,128)} %get-tuple-element.40, f32[512,64]{0,1:T(8,128)S(1)} %get-tuple-element.39, f32[512,2]{0,1:T(2,128)S(1)} %get-tuple-element.66, f32[512,64]{0,1:T(8,128)} %get-tuple-element.38, f32[512,2]{0,1:T(2,128)S(1)} %get-tuple-element.65), kind=kOutput, calls=%fused_computation.7 | convolution fusion | flops 100892672 | bytes 663552 | tf_op jit(solution)/shard_map/mra,mb->rab/dot_general | solution.py:101
  57.7 1.4 %gather_fusion = f32[128,64]{1,0:T(8,128)} fusion(f32[256,64]{1,0:T(8,128)S(1)} %mul.287, s32[1024]{0:T(1024)} %pad_clamp_fusion), kind=kCustom, calls=%fused_computation | custom fusion | bytes 66048 | tf_op jit(solution)/shard_map/gather | solution.py:31
  59.1 1.9 %fusion = f32[128,64]{0,1:T(8,128)S(1)} fusion(f32[32,64,64]{2,1,0:T(8,128)S(1)} %copy-done, pred[128,32]{0,1:T(8,128)(4,1)} %iota_compare_fusion, f32[128,64]{1,0:T(8,128)} %gather_fusion), kind=kOutput, calls=%fused_computation.3 | convolution fusion | flops 201842688 | bytes 593920 | tf_op jit(solution)/shard_map/kij,tj->tki/dot_general | solution.py:32
  61.0 1.0 fusion.46
  62.9 1.2 %scatter_custom_fusion = f32[256,64]{1,0:T(8,128)S(1)} fusion(s32[128]{0:T(128)} %copy-done.8, f32[128,64]{1,0:T(8,128)S(1)} %copy.75, f32[]{:T(128)} %constant.25.clone.1), kind=kCustom, calls=%fused_computation.65 | custom fusion | flops 8192 | bytes 66048 | tf_op jit(solution)/shard_map/scatter-add | solution.py:36
  64.1 1.4 %convolution_bitcast_fusion = f32[512,64,2]{0,1,2:T(8,128)S(1)} fusion(f32[512,128]{1,0:T(8,128)} %get-tuple-element.40, f32[2,64,128]{2,1,0:T(8,128)S(1)} %reshape.173, f32[2,64,128]{2,1,0:T(8,128)} %copy-done.2, f32[1,2,64,128]{3,1,2,0:T(2,128)} %bitcast.85), kind=kOutput, calls=%fused_computation.4 | convolution fusion | flops 100696064 | bytes 720896 | tf_op jit(solution)/shard_map/rab,mb->mra/dot_general | solution.py:108
  65.5 1.5 %multiply_reduce_fusion.4 = (f32[512,2]{0,1:T(2,128)S(1)}, f32[512,2]{0,1:T(2,128)S(1)}, f32[512,2]{0,1:T(2,128)S(1)}, f32[512,2]{0,1:T(2,128)S(1)}) fusion(f32[512,64]{0,1:T(8,128)} %get-tuple-element.38, f32[512,64]{0,1:T(8,128)} %copy-done.1, f32[512,64,2]{0,1,2:T(8,128)S(1)} %convolution_bitcast_fusion, f32[2,64,128]{2,1,0:T(8,128)S(1)} %reshape.173, ...), kind=kOutput, calls=%fused_computation.27 | convolution fusion | flops 101216256 | bytes 999424 | tf_op jit(solution)/shard_map/rab,mb->mra/dot_general | solution.py:107
  67.7 18.3 %all_to_all.37 = bf16[256,1,64]{2,1,0:T(2,128)(2,1)S(1)} all-to-all(bf16[256,1,64]{2,1,0:T(2,128)(2,1)S(1)} %copy.77), channel_id=1, replica_groups=mesh['blk'=32,'band'=8] {'blk','band'}, dimensions={0} | all-to-all | bytes 65536 | tf_op jit(solution)/shard_map/all_to_all | solution.py:121
  89.6 18.2 %all_to_all.38 = f32[256,1,4]{2,1,0:T(1,128)S(1)} all-to-all(f32[256,1,4]{2,1,0:T(1,128)S(1)} %broadcast_in_dim.31), channel_id=1, replica_groups=mesh['blk'=32,'band'=8] {'blk','band'}, dimensions={0} | all-to-all | bytes 8192 | tf_op jit(solution)/shard_map/all_to_all | solution.py:137
  (61 shorter events, 10.8 us)
Async XLA Ops:
  0.6 56.7 %copy-start = (f32[32,64,64]{2,1,0:T(8,128)S(1)}, f32[32,64,64]{2,1,0:T(8,128)}, u32[]{:S(2)}) copy-start(f32[32,64,64]{2,1,0:T(8,128)} %param.21) | copy-start | bytes 1572868
  0.6 14.4 %all-to-all-start = ((f32[8,1,512]{2,1,0:T(1,128)}), f32[8,1,512]{2,1,0:T(1,128)}, u32[]{:S(2)}, u32[]{:S(2)}) async-start(f32[8,1,512]{2,1,0:T(1,128)} %bitcast.89), calls=%async_computation | async-start | bytes 32768 | tf_op jit(solution)/shard_map/all_to_all | solution.py:62
  12.3 42.9 %copy-start.1 = (f32[512,64]{0,1:T(8,128)}, f32[512,64]{0,1:T(8,128)S(1)}, u32[]{:S(2)}) copy-start(f32[512,64]{0,1:T(8,128)S(1)} %get-tuple-element.39) | copy-start | bytes 393220
  47.9 1.9 %copy-start.8 = (s32[128]{0:T(128)}, s32[128]{0:T(128)S(1)}, u32[]{:S(2)}) copy-start(s32[128]{0:T(128)S(1)} %compare_select_fusion) | copy-start | bytes 1540
  56.6 0.6 copy-start.2
  59.1 29.5 %copy-start.3 = (f32[16,2,512]{2,1,0:T(2,128)S(1)}, f32[16,2,512]{2,1,0:T(2,128)}, u32[]{:S(2)}) copy-start(f32[16,2,512]{2,1,0:T(2,128)} %param.14) | copy-start | bytes 196612
  59.1 29.6 %copy-start.4 = (f32[16,2,512]{2,1,0:T(2,128)S(1)}, f32[16,2,512]{2,1,0:T(2,128)}, u32[]{:S(2)}) copy-start(f32[16,2,512]{2,1,0:T(2,128)} %param.13) | copy-start | bytes 196612
  61.0 27.6 %copy-start.7 = (f32[512]{0:T(512)S(1)}, f32[512]{0:T(512)}, u32[]{:S(2)}) copy-start(f32[512]{0:T(512)} %param.15) | copy-start | bytes 6148
  61.0 27.8 %copy-start.6 = (f32[512]{0:T(512)S(1)}, f32[512]{0:T(512)}, u32[]{:S(2)}) copy-start(f32[512]{0:T(512)} %param.16) | copy-start | bytes 6148
  61.0 47.2 %copy-start.5 = (f32[16,2,512]{2,1,0:T(2,128)S(1)}, f32[16,2,512]{2,1,0:T(2,128)}, u32[]{:S(2)}) copy-start(f32[16,2,512]{2,1,0:T(2,128)} %param.12) | copy-start | bytes 196612

commit v7 on v4

--- a/solution.py
+++ b/solution.py
@@ -72,7 +72,12 @@
     partial = partial.reshape(orders_dev, nband, parts, nblk, cycles_dev)
     chunk = orders_dev * parts * cycles_dev
     outgoing = partial.transpose(3, 1, 0, 2, 4).reshape(nblk * nband, chunk)
-    incoming = lax.all_to_all(outgoing, EVERY, split_axis=0, concat_axis=0, tiled=True)
+    high = outgoing.astype(jnp.bfloat16)
+    low = (outgoing - high.astype(jnp.float32)).astype(jnp.bfloat16)
+    pair = lax.all_to_all(
+        jnp.concatenate([high, low], axis=1), EVERY, split_axis=0, concat_axis=0, tiled=True
+    )
+    incoming = pair[:, :chunk].astype(jnp.float32) + pair[:, chunk:].astype(jnp.float32)
     cycle_coefficients = jnp.sum(
         incoming.reshape(nblk, nband, orders_dev, parts, cycles_dev), axis=1
     ).reshape(order_count, parts, cycles_dev)

time: 96.3 us -> 96.4 us (level)
  waiting for transfers between devices: 11.9 us -> 13.2 us
  local copies, waits for them, and re-layouts: 10.3 us -> 9.15 us
    all_to_all x1, waiting for transfers between devices: 10.6 us -> 11.8 us  [per_device(): lax.all_to_all(jnp.concatenate([high, low], axis=1), EVERY, split_axis=0,...]
    unnamed x18 -> x19, local copies, waits for them, and re-layouts: 1.61 us -> 0.39 us
  transfers between devices with their start and end apart: 2 -> 2, of which waited for: 2 -> 2; matrix products, arithmetic and copies ran while one was open for 6% -> 4% of each run, Pallas kernels for 0% -> 0%
where the time goes in v7:
time: 96.4 us; the launch traced here: 96 us
  blocking collectives  36.3 us (38%)
  starting transfers between devices  19.2 us (20%)
  waiting for transfers between devices  13.2 us (14%)
  matrix products  10.8 us (11%)
  local copies, waits for them, and re-layouts  9.15 us (9%)
  other arithmetic  6.23 us (6%)
  between operations  1.07 us (1%)
    all_to_all x1, blocking collectives, per_device(): lax.all_to_all(returning, EVERY, split_axis=0, concat_axis=0, tiled=True)  18.2 us
    all_to_all x1, blocking collectives, per_device(): lax.all_to_all(shared, EVERY, split_axis=0, concat_axis=0, tiled=True)  18.2 us
    all_to_all x1, starting transfers between devices, per_device(): lax.all_to_all(jnp.concatenate([high, low], axis=1), EVERY, split_axis=0,...  12.7 us
    all_to_all x1, waiting for transfers between devices, per_device(): lax.all_to_all(jnp.concatenate([high, low], axis=1), EVERY, split_axis=0,...  11.8 us
    all_to_all x1, starting transfers between devices, per_device(): lax.all_to_all(beam_window.reshape(nband, width), 'band', split_axis=0, c...  6.58 us
  transfers between devices with their start and end apart: 2, of which 2 were waited for; matrix products, arithmetic and copies ran while one was open for 4% of the time, Pallas kernels for 0%

profile of v7, /device:TPU:1, one launch (start us, length us, event | category | flops | bytes accessed | tf_op | source)
XLA Modules:
  0.0 96.0 jit_solution(16846997795660616841)
XLA Ops:
  0.7 6.6 %all-to-all-start = ((f32[8,1,512]{2,1,0:T(1,128)}), f32[8,1,512]{2,1,0:T(1,128)S(1)}, u32[]{:S(2)}, u32[]{:S(2)}) async-start(f32[8,1,512]{2,1,0:T(1,128)} %bitcast.87), calls=%async_computation | async-start | bytes 32768 | tf_op jit(solution)/shard_map/all_to_all | solution.py:62
  7.2 1.3 %fusion.46 = (f32[512,64]{0,1:T(8,128)S(1)}, f32[512,64]{0,1:T(8,128)S(1)}) fusion(s32[64]{0:T(128)S(1)} %iota_multiply_fusion, s32[512]{0:T(512)} %param.19), kind=kLoop, calls=%fused_computation.74 | loop fusion | flops 458752 | bytes 264448 | tf_op jit(solution)/shard_map/cos | solution.py:20
  8.5 0.7 iota_compare_fusion
  9.2 1.0 %mul.277 = f32[16,8,2,512]{3,2,1,0:T(2,128)S(1)} broadcast(f32[16,2,512]{2,1,0:T(2,128)} %param.14), dimensions={0,2,3} | broadcast | bytes 589824 | tf_op jit(solution)/shard_map/mul | solution.py:67
  10.5 1.4 %all-to-all-done = f32[8,1,512]{2,1,0:T(1,128)S(1)} async-done(((f32[8,1,512]{2,1,0:T(1,128)}), f32[8,1,512]{2,1,0:T(1,128)S(1)}, u32[]{:S(2)}, u32[]{:S(2)}) %all-to-all-start) | async-done | bytes 16416 | tf_op jit(solution)/shard_map/all_to_all | solution.py:62
  12.0 1.6 %fusion.4 = f32[16,16,64]{2,1,0:T(8,128)S(1)} fusion(bf16[16,64,4096]{2,1,0:T(8,128)(2,1)} %param.18, s32[]{:T(128)S(6)} %select_n.35, f32[16,16,512]{2,1,0:T(8,128)S(1)} %mul.278, f32[16,512]{1,0:T(8,128)S(1)} %mul.275), kind=kOutput, calls=%fused_computation.11 | convolution fusion | flops 17039360 | bytes 1671172 | tf_op jit(solution)/shard_map/sql,srl->sqr/dot_general | solution.py:69
  13.8 0.9 copy.69
  15.3 0.8 copy.70
  16.1 12.7 %all-to-all-start.1 = ((bf16[256,1,128]{2,1,0:T(2,128)(2,1)}), bf16[256,1,128]{2,1,0:T(2,128)(2,1)S(1)}, u32[]{:S(2)}, u32[]{:S(2)}) async-start(bf16[256,1,128]{2,1,0:T(2,128)(2,1)} %copy.70), calls=%async_computation.1 | async-start | bytes 262144 | tf_op jit(solution)/shard_map/all_to_all | solution.py:77
  28.7 0.7 compare_select_fusion
  29.7 11.8 %all-to-all-done.1 = bf16[256,1,128]{2,1,0:T(2,128)(2,1)S(1)} async-done(((bf16[256,1,128]{2,1,0:T(2,128)(2,1)}), bf16[256,1,128]{2,1,0:T(2,128)(2,1)S(1)}, u32[]{:S(2)}, u32[]{:S(2)}) %all-to-all-start.1) | async-done | bytes 65568 | tf_op jit(solution)/shard_map/all_to_all | solution.py:77
  42.9 1.4 %fusion.12 = f32[2,64,128]{2,1,0:T(8,128)S(1)} fusion(f32[512,64]{0,1:T(8,128)S(1)} %get-tuple-element.28, f32[512,2]{0,1:T(2,128)S(1)} %get-tuple-element.26, f32[512,64]{0,1:T(8,128)S(1)} %get-tuple-element.27, f32[512,2]{0,1:T(2,128)S(1)} %get-tuple-element.25, s32[512]{0:T(512)S(1)} %copy-done.5), kind=kOutput, calls=%fused_computation.25 | convolution fusion | flops 101777408 | bytes 337920 | tf_op jit(solution)/shard_map/mra,mb->rab/dot_general | solution.py:92
  44.4 1.4 %fusion.1 = f32[2,64,128]{2,1,0:T(8,128)S(1)} fusion(f32[2,64,128]{2,1,0:T(8,128)S(1)} %fusion.12, f32[512,64]{0,1:T(8,128)S(1)} %get-tuple-element.28, f32[512,2]{0,1:T(2,128)S(1)} %get-tuple-element.26, f32[512,64]{0,1:T(8,128)S(1)} %get-tuple-element.27, f32[512,2]{0,1:T(2,128)S(1)} %get-tuple-element.25, s32[512]{0:T(512)S(1)} %copy-done.5), kind=kOutput, calls=%fused_computation.7 | convolution fusion | flops 101810176 | bytes 403456 | tf_op jit(solution)/shard_map/mra,mb->rab/dot_general | solution.py:92
  46.0 0.6 gather_fusion
  46.6 1.0 %fusion = f32[128,64]{0,1:T(8,128)S(1)} fusion(f32[32,64,64]{2,1,0:T(8,128)S(1)} %copy-done, pred[128,32]{0,1:T(8,128)(4,1)S(1)} %iota_compare_fusion, f32[128,64]{1,0:T(8,128)S(1)} %gather_fusion), kind=kOutput, calls=%fused_computation.3 | convolution fusion | flops 201842688 | bytes 593920 | tf_op jit(solution)/shard_map/kij,tj->tki/dot_general | solution.py:32
  47.6 1.0 %fusion.71 = f32[128,2048]{0,1:S(1)} fusion(f32[128,64]{0,1:T(8,128)S(1)} %fusion, f32[64,2048]{0,1:T(8,128)S(1)} %bitcast.79), kind=kOutput, calls=%fused_computation.112 | convolution fusion | flops 201326592 | bytes 1605632
  48.8 1.2 %scatter_custom_fusion = f32[256,64]{1,0:T(8,128)S(1)} fusion(s32[128]{0:T(128)S(1)} %compare_select_fusion, f32[128,64]{1,0:T(8,128)S(1)} %copy.75, f32[]{:T(128)} %constant.46.clone.1), kind=kCustom, calls=%fused_computation.71 | custom fusion | flops 8192 | bytes 65540 | tf_op jit(solution)/shard_map/scatter-add | solution.py:36
  50.1 1.4 %convolution_bitcast_fusion = f32[512,64,2]{0,1,2:T(8,128)S(1)} fusion(s32[512]{0:T(512)S(1)} %copy-done.5, f32[2,64,128]{2,1,0:T(8,128)S(1)} %reshape.226, f32[2,64,128]{2,1,0:T(8,128)S(1)} %fusion.1, f32[1,2,64,128]{3,1,2,0:T(2,128)S(1)} %bitcast.92), kind=kOutput, calls=%fused_computation.4 | convolution fusion | flops 101613568 | bytes 460800 | tf_op jit(solution)/shard_map/rab,mb->mra/dot_general | solution.py:99
  51.6 1.4 %multiply_reduce_fusion.4 = (f32[512,2]{0,1:T(2,128)S(1)}, f32[512,2]{0,1:T(2,128)S(1)}, f32[512,2]{0,1:T(2,128)S(1)}, f32[512,2]{0,1:T(2,128)S(1)}) fusion(f32[512,64]{0,1:T(8,128)S(1)} %get-tuple-element.27, f32[512,64]{0,1:T(8,128)S(1)} %get-tuple-element.28, f32[512,64,2]{0,1,2:T(8,128)S(1)} %convolution_bitcast_fusion, ...), kind=kOutput, calls=%fused_computation.30 | convolution fusion | flops 102133760 | bytes 739328 | tf_op jit(solution)/shard_map/rab,mb->mra/dot_general | solution.py:98
  53.7 18.2 %all_to_all.36 = bf16[256,1,64]{2,1,0:T(2,128)(2,1)S(1)} all-to-all(bf16[256,1,64]{2,1,0:T(2,128)(2,1)S(1)} %copy.77), channel_id=1, replica_groups=mesh['blk'=32,'band'=8] {'blk','band'}, dimensions={0} | all-to-all | bytes 65536 | tf_op jit(solution)/shard_map/all_to_all | solution.py:112
  72.6 0.8 copy.79
  73.6 1.5 %fusion.2 = f32[16,16,512]{2,1,0:T(8,128)S(1)} fusion(bf16[16,16,64]{2,1,0:T(8,128)(2,1)S(1)} %copy.80, bf16[16,64,4096]{2,1,0:T(8,128)(2,1)} %param.18, s32[]{:T(128)S(6)} %select_n.35), kind=kOutput, calls=%fused_computation.9 | convolution fusion | flops 16777216 | bytes 1605636 | tf_op jit(solution)/shard_map/sqr,srl->sql/dot_general | solution.py:115
  76.7 18.2 %all_to_all.37 = f32[256,1,4]{2,1,0:T(1,128)S(1)} all-to-all(f32[256,1,4]{2,1,0:T(1,128)S(1)} %broadcast_in_dim.31), channel_id=1, replica_groups=mesh['blk'=32,'band'=8] {'blk','band'}, dimensions={0} | all-to-all | bytes 8192 | tf_op jit(solution)/shard_map/all_to_all | solution.py:128
  95.2 0.7 multiply_add_fusion
  (62 shorter events, 6.7 us)
Async XLA Ops:
  0.6 42.3 %copy-start.5 = (s32[512]{0:T(512)S(1)}, s32[512]{0:T(512)}, u32[]{:S(2)}) copy-start(s32[512]{0:T(512)} %param.19) | copy-start | bytes 6148
  0.6 28.8 %copy-start = (f32[32,64,64]{2,1,0:T(8,128)S(1)}, f32[32,64,64]{2,1,0:T(8,128)}, u32[]{:S(2)}) copy-start(f32[32,64,64]{2,1,0:T(8,128)} %param.21) | copy-start | bytes 1572868
  0.7 11.3 %all-to-all-start = ((f32[8,1,512]{2,1,0:T(1,128)}), f32[8,1,512]{2,1,0:T(1,128)S(1)}, u32[]{:S(2)}, u32[]{:S(2)}) async-start(f32[8,1,512]{2,1,0:T(1,128)} %bitcast.87), calls=%async_computation | async-start | bytes 32768 | tf_op jit(solution)/shard_map/all_to_all | solution.py:62
  16.1 25.5 %all-to-all-start.1 = ((bf16[256,1,128]{2,1,0:T(2,128)(2,1)}), bf16[256,1,128]{2,1,0:T(2,128)(2,1)S(1)}, u32[]{:S(2)}, u32[]{:S(2)}) async-start(bf16[256,1,128]{2,1,0:T(2,128)(2,1)} %copy.70), calls=%async_computation.1 | async-start | bytes 262144 | tf_op jit(solution)/shard_map/all_to_all | solution.py:77
  42.7 7.4 %copy-start.7 = (f32[1,2,8192]{2,1,0:T(2,128)S(1)}, f32[1,2,8192]{2,1,0:T(2,128)}, u32[]{:S(2)}) copy-start(f32[1,2,8192]{2,1,0:T(2,128)} %param.20) | copy-start | bytes 196612
  42.9 32.7 %copy-start.1 = (f32[16,2,512]{2,1,0:T(2,128)S(1)}, f32[16,2,512]{2,1,0:T(2,128)}, u32[]{:S(2)}) copy-start(f32[16,2,512]{2,1,0:T(2,128)} %param.14) | copy-start | bytes 196612
  42.9 32.7 %copy-start.6 = (f32[512]{0:T(512)S(1)}, f32[512]{0:T(512)}, u32[]{:S(2)}) copy-start(f32[512]{0:T(512)} %param.15) | copy-start | bytes 6148
  44.4 31.4 %copy-start.2 = (f32[16,2,512]{2,1,0:T(2,128)S(1)}, f32[16,2,512]{2,1,0:T(2,128)}, u32[]{:S(2)}) copy-start(f32[16,2,512]{2,1,0:T(2,128)} %param.13) | copy-start | bytes 196612
  44.4 31.4 %copy-start.4 = (f32[512]{0:T(512)S(1)}, f32[512]{0:T(512)}, u32[]{:S(2)}) copy-start(f32[512]{0:T(512)} %param.16) | copy-start | bytes 6148
  45.9 49.4 %copy-start.3 = (f32[16,2,512]{2,1,0:T(2,128)S(1)}, f32[16,2,512]{2,1,0:T(2,128)}, u32[]{:S(2)}) copy-start(f32[16,2,512]{2,1,0:T(2,128)} %param.12) | copy-start | bytes 196612

commit v8 on v4

--- a/solution.py
+++ b/solution.py
@@ -59,23 +59,34 @@
     order_count = mode_orders.shape[0]
     norm_scale = 1.0 / math.sqrt(order_count)
 
-    beam_here = lax.all_to_all(
-        beam_window.reshape(nband, width), "band", split_axis=0, concat_axis=0, tiled=True
+    sub = orders_dev // nband
+    multipoles = width * nband
+    direction_rows = direction.reshape(nband, sub * parts * width)
+    beam_rows = jnp.broadcast_to(beam_window.reshape(1, multipoles), (nband, multipoles))
+    arrived_rows = lax.all_to_all(
+        jnp.concatenate([direction_rows, beam_rows], axis=1), "band", 0, 0, tiled=True
     )
+    direction_share = (
+        arrived_rows[:, : sub * parts * width]
+        .reshape(nband, sub, parts, width)
+        .transpose(1, 2, 0, 3)
+        .reshape(sub, parts, multipoles)
+    )
+    beam_all = arrived_rows[:, sub * parts * width :]
+    beam_here = lax.dynamic_slice_in_dim(beam_all, band * width, width, 1)
     legendre_here = lax.dynamic_slice_in_dim(legendre, band * width, width, 2)
+    legendre_share = lax.dynamic_slice_in_dim(legendre, band * sub, sub, 0)
 
-    weighted = (beam_here[None, :, None, :] * direction[:, None, :, :]).astype(jnp.bfloat16)
-    weighted = weighted.reshape(orders_dev, nband * parts, width)
-    partial = jnp.einsum(
-        "sql,srl->sqr", weighted, legendre_here, preferred_element_type=jnp.float32
+    weighted = (beam_all[None, :, None, :] * direction_share[:, None, :, :]).astype(jnp.bfloat16)
+    weighted = weighted.reshape(sub, nband * parts, multipoles)
+    coefficients = jnp.einsum(
+        "sql,srl->sqr", weighted, legendre_share, preferred_element_type=jnp.float32
     )
-    partial = partial.reshape(orders_dev, nband, parts, nblk, cycles_dev)
-    chunk = orders_dev * parts * cycles_dev
-    outgoing = partial.transpose(3, 1, 0, 2, 4).reshape(nblk * nband, chunk)
+    coefficients = coefficients.reshape(sub, nband, parts, nblk, cycles_dev)
+    chunk = sub * parts * cycles_dev
+    outgoing = coefficients.transpose(3, 1, 0, 2, 4).reshape(nblk * nband, chunk)
     incoming = lax.all_to_all(outgoing, EVERY, split_axis=0, concat_axis=0, tiled=True)
-    cycle_coefficients = jnp.sum(
-        incoming.reshape(nblk, nband, orders_dev, parts, cycles_dev), axis=1
-    ).reshape(order_count, parts, cycles_dev)
+    cycle_coefficients = incoming.reshape(order_count, parts, cycles_dev)
 
     cycle_count = cycles_dev
     outer_cos, outer_sin = phases(mode_orders, NPHI // 128, 128)
@@ -102,8 +113,11 @@
     )
     cycle_terms = jnp.stack([real_terms, imag_terms], axis=1).astype(jnp.bfloat16)
 
-    per_owner = cycle_terms.reshape(nblk, 1, chunk)
-    returning = jnp.broadcast_to(per_owner, (nblk, nband, chunk)).reshape(nblk * nband, chunk)
+    back_chunk = orders_dev * parts * cycles_dev
+    per_owner = cycle_terms.reshape(nblk, 1, back_chunk)
+    returning = jnp.broadcast_to(per_owner, (nblk, nband, back_chunk)).reshape(
+        nblk * nband, back_chunk
+    )
     arrived = lax.all_to_all(returning, EVERY, split_axis=0, concat_axis=0, tiled=True)
     mode_terms = arrived.reshape(nblk, nband, orders_dev, parts, cycles_dev)
     mode_terms = mode_terms.transpose(2, 1, 3, 0, 4).reshape(orders_dev, nband * parts, cycles_all)

time: 96.3 us -> 107 us (1.11)
  blocking collectives: 36.3 us -> 18.2 us
  waiting for transfers between devices: 11.9 us -> 28 us
  starting transfers between devices: 19.2 us -> 24.6 us
  matrix products: 10.8 us -> 14.4 us
  local copies, waits for them, and re-layouts: 10.3 us -> 12.5 us
  other arithmetic: 6.13 us -> 7.36 us
    all_to_all x1 -> x0, blocking collectives: 18.2 us -> none  [per_device(): lax.all_to_all(returning, EVERY, split_axis=0, concat_axis=0, tiled=True)]
    all_to_all x1 -> x2, waiting for transfers between devices: 1.38 us -> 15.6 us  [the longest x1 12.9 us: per_device(): lax.all_to_all(returning, EVERY, split_axis=0, concat_axis=0, tiled=True)]
    all_to_all x1 -> x2, starting transfers between devices: 6.58 us -> 12 us  [the longest x1 6.49 us: per_device(): lax.all_to_all(jnp.concatenate([direction_rows, beam_rows], axis=1), 'ban...]
    all_to_all x1, waiting for transfers between devices: 10.6 us -> 12.4 us  [per_device(): lax.all_to_all(outgoing, EVERY, split_axis=0, concat_axis=0, tiled=True)]
    reshape x2 -> x3, local copies, waits for them, and re-layouts: 0.68 us -> 1.97 us  [the longest x1 0.99 us: per_device(): direction_rows = direction.reshape(nband, sub * parts * width)]
    unnamed x18 -> x16, local copies, waits for them, and re-layouts: 1.61 us -> 0.43 us
  transfers between devices with their start and end apart: 2 -> 3, of which waited for: 2 -> 3; matrix products, arithmetic and copies ran while one was open for 6% -> 3% of each run, Pallas kernels for 0% -> 0%
where the time goes in v8:
time: 107 us; the launch traced here: 106 us
  waiting for transfers between devices  28 us (26%)
  starting transfers between devices  24.6 us (23%)
  blocking collectives  18.2 us (17%)
  matrix products  14.4 us (13%)
  local copies, waits for them, and re-layouts  12.5 us (12%)
  other arithmetic  7.36 us (7%)
  between operations  1.07 us (1%)
    all_to_all x1, blocking collectives, per_device(): lax.all_to_all(shared, EVERY, split_axis=0, concat_axis=0, tiled=True)  18.2 us
    all_to_all x1, waiting for transfers between devices, per_device(): lax.all_to_all(returning, EVERY, split_axis=0, concat_axis=0, tiled=True)  12.9 us
    all_to_all x1, starting transfers between devices, per_device(): lax.all_to_all(outgoing, EVERY, split_axis=0, concat_axis=0, tiled=True)  12.5 us
    all_to_all x1, waiting for transfers between devices, per_device(): lax.all_to_all(outgoing, EVERY, split_axis=0, concat_axis=0, tiled=True)  12.4 us
    all_to_all x1, starting transfers between devices, per_device(): lax.all_to_all(jnp.concatenate([direction_rows, beam_rows], axis=1), 'ban...  6.49 us
    all_to_all x1, starting transfers between devices, per_device(): lax.all_to_all(returning, EVERY, split_axis=0, concat_axis=0, tiled=True)  5.54 us
    all_to_all x1, waiting for transfers between devices, per_device(): lax.all_to_all(jnp.concatenate([direction_rows, beam_rows], axis=1), 'ban...  2.64 us
    dot_general x1, matrix products, per_device(): jnp.einsum('rab,mb->mra', noisy_grid, inner_cos, precision=precise)  2.39 us
  transfers between devices with their start and end apart: 3, of which 3 were waited for; matrix products, arithmetic and copies ran while one was open for 3% of the time, Pallas kernels for 0%

profile of v8, /device:TPU:1, one launch (start us, length us, event | category | flops | bytes accessed | tf_op | source)
XLA Modules:
  0.0 106.1 jit_solution(7806087456607733890)
XLA Ops:
  0.7 1.0 reshape.223
  2.4 0.8 all_to_all.24
  3.2 6.5 %all-to-all-start = ((f32[8,1,6144]{2,1,0:T(1,128)}), f32[8,1,6144]{2,1,0:T(1,128)S(1)}, u32[]{:S(2)}, u32[]{:S(2)}) async-start(f32[8,1,6144]{2,1,0:T(1,128)} %all_to_all.24), calls=%async_computation | async-start | bytes 393216 | tf_op jit(solution)/shard_map/all_to_all | solution.py:66
  10.4 1.9 %fusion.46 = (f32[512,64]{0,1:T(8,128)S(1)}, f32[512,64]{0,1:T(8,128)}) fusion(s32[64]{0:T(128)S(1)} %iota_multiply_fusion, s32[512]{0:T(512)} %param.19), kind=kLoop, calls=%fused_computation.73 | loop fusion | flops 458752 | bytes 264448 | tf_op jit(solution)/shard_map/cos | solution.py:20
  12.9 2.6 %all-to-all-done = f32[8,1,6144]{2,1,0:T(1,128)S(1)} async-done(((f32[8,1,6144]{2,1,0:T(1,128)}), f32[8,1,6144]{2,1,0:T(1,128)S(1)}, u32[]{:S(2)}, u32[]{:S(2)}) %all-to-all-start) | async-done | bytes 196640 | tf_op jit(solution)/shard_map/all_to_all | solution.py:66
  16.6 1.6 %fusion.4 = f32[2,16,64]{2,1,0:T(8,128)S(1)} fusion(bf16[16,64,4096]{2,1,0:T(8,128)(2,1)} %param.18, s32[]{:T(128)S(6)} %select_n.40, f32[2,16,4096]{2,1,0:T(8,128)S(1)} %mul.283, f32[16,4096]{1,0:T(8,128)S(1)} %mul.279), kind=kOutput, calls=%fused_computation.11 | convolution fusion | flops 17039360 | bytes 1843204 | tf_op jit(solution)/shard_map/sql,srl->sqr/dot_general | solution.py:82
  18.8 0.9 copy.69
  19.8 0.8 copy.70
  20.6 12.5 %all-to-all-start.1 = ((f32[256,1,8]{2,1,0:T(1,128)}), f32[256,1,8]{2,1,0:T(1,128)S(1)}, u32[]{:S(2)}, u32[]{:S(2)}) async-start(f32[256,1,8]{2,1,0:T(1,128)} %copy.70), calls=%async_computation.1 | async-start | bytes 262144 | tf_op jit(solution)/shard_map/all_to_all | solution.py:88
  33.5 12.4 %all-to-all-done.1 = f32[256,1,8]{2,1,0:T(1,128)S(1)} async-done(((f32[256,1,8]{2,1,0:T(1,128)}), f32[256,1,8]{2,1,0:T(1,128)S(1)}, u32[]{:S(2)}, u32[]{:S(2)}) %all-to-all-start.1) | async-done | bytes 8224 | tf_op jit(solution)/shard_map/all_to_all | solution.py:88
  46.4 1.0 reduce.12
  48.5 2.4 %fusion.12 = f32[2,64,128]{2,1,0:T(8,128)S(1)} fusion(f32[512,64]{0,1:T(8,128)} %get-tuple-element.26, f32[512,2]{0,1:T(2,128)S(1)} %copy.72, f32[512,64]{0,1:T(8,128)S(1)} %get-tuple-element.25, f32[512,2]{0,1:T(2,128)S(1)} %copy.71, s32[512]{0:T(512)S(1)} %copy-done.5), kind=kOutput, calls=%fused_computation.25 | convolution fusion | flops 101777408 | bytes 337920 | tf_op jit(solution)/shard_map/mra,mb->rab/dot_general | solution.py:98
  50.9 2.4 %fusion.1 = f32[2,64,128]{2,1,0:T(8,128)S(1)} fusion(f32[2,64,128]{2,1,0:T(8,128)S(1)} %fusion.12, f32[512,64]{0,1:T(8,128)} %get-tuple-element.26, f32[512,2]{0,1:T(2,128)S(1)} %copy.72, f32[512,64]{0,1:T(8,128)S(1)} %get-tuple-element.25, f32[512,2]{0,1:T(2,128)S(1)} %copy.71, s32[512]{0:T(512)S(1)} %copy-done.5), kind=kOutput, calls=%fused_computation.7 | convolution fusion | flops 101810176 | bytes 403456 | tf_op jit(solution)/shard_map/mra,mb->rab/dot_general | solution.py:98
  54.0 1.0 fusion
  55.0 1.0 fusion.72
  56.2 1.2 %scatter_custom_fusion = f32[256,64]{1,0:T(8,128)S(1)} fusion(s32[128]{0:T(128)S(1)} %compare_select_fusion, f32[128,64]{1,0:T(8,128)S(1)} %copy.75, f32[]{:T(128)} %constant.52.clone.1), kind=kCustom, calls=%fused_computation.70 | custom fusion | flops 8192 | bytes 65540 | tf_op jit(solution)/shard_map/scatter-add | solution.py:36
  57.5 2.3 %convolution_bitcast_fusion = f32[512,64,2]{0,1,2:T(8,128)S(1)} fusion(s32[512]{0:T(512)S(1)} %copy-done.5, f32[2,64,128]{2,1,0:T(8,128)S(1)} %reshape.227, f32[2,64,128]{2,1,0:T(8,128)S(1)} %fusion.1, f32[1,2,64,128]{3,1,2,0:T(2,128)} %bitcast.84), kind=kOutput, calls=%fused_computation.4 | convolution fusion | flops 101613568 | bytes 460800 | tf_op jit(solution)/shard_map/rab,mb->mra/dot_general | solution.py:105
  59.8 2.4 %multiply_reduce_fusion.4 = (f32[512,2]{0,1:T(2,128)S(1)}, f32[512,2]{0,1:T(2,128)S(1)}, f32[512,2]{0,1:T(2,128)S(1)}, f32[512,2]{0,1:T(2,128)S(1)}) fusion(f32[512,64]{0,1:T(8,128)S(1)} %get-tuple-element.25, f32[512,64]{0,1:T(8,128)} %get-tuple-element.26, f32[512,64,2]{0,1,2:T(8,128)S(1)} %convolution_bitcast_fusion, f32[2,64,128]{2,1,0:T(8,128)S(1)} %reshape.227, ...), kind=kOutput, calls=%fused_computation.30 | convolution fusion | flops 102133760 | bytes 739328 | tf_op jit(solution)/shard_map/rab,mb->mra/dot_general | solution.py:104
  63.5 5.5 %all-to-all-start.2 = ((bf16[256,1,64]{2,1,0:T(2,128)(2,1)}), bf16[256,1,64]{2,1,0:T(2,128)(2,1)S(1)}, u32[]{:S(2)}, u32[]{:S(2)}) async-start(bf16[256,1,64]{2,1,0:T(2,128)(2,1)} %copy.77), calls=%async_computation.2 | async-start | bytes 262144 | tf_op jit(solution)/shard_map/all_to_all | solution.py:121
  69.1 12.9 %all-to-all-done.2 = bf16[256,1,64]{2,1,0:T(2,128)(2,1)S(1)} async-done(((bf16[256,1,64]{2,1,0:T(2,128)(2,1)}), bf16[256,1,64]{2,1,0:T(2,128)(2,1)S(1)}, u32[]{:S(2)}, u32[]{:S(2)}) %all-to-all-start.2) | async-done | bytes 32800 | tf_op jit(solution)/shard_map/all_to_all | solution.py:121
  82.8 0.8 copy.79
  83.7 1.5 %fusion.2 = f32[16,16,512]{2,1,0:T(8,128)S(1)} fusion(bf16[16,16,64]{2,1,0:T(8,128)(2,1)S(1)} %copy.80, bf16[16,64,4096]{2,1,0:T(8,128)(2,1)} %param.18, s32[]{:T(128)S(6)} %select_n.38), kind=kOutput, calls=%fused_computation.8 | convolution fusion | flops 16777216 | bytes 1605636 | tf_op jit(solution)/shard_map/sqr,srl->sql/dot_general | solution.py:124
  86.8 18.2 %all_to_all.36 = f32[256,1,4]{2,1,0:T(1,128)S(1)} all-to-all(f32[256,1,4]{2,1,0:T(1,128)S(1)} %broadcast_in_dim.37), channel_id=1, replica_groups=mesh['blk'=32,'band'=8] {'blk','band'}, dimensions={0} | all-to-all | bytes 8192 | tf_op jit(solution)/shard_map/all_to_all | solution.py:137
  105.4 0.7 multiply_add_fusion
  (65 shorter events, 10.8 us)
Async XLA Ops:
  0.6 47.8 %copy-start.5 = (s32[512]{0:T(512)S(1)}, s32[512]{0:T(512)}, u32[]{:S(2)}) copy-start(s32[512]{0:T(512)} %param.19) | copy-start | bytes 6148
  0.6 32.5 %copy-start = (f32[32,64,64]{2,1,0:T(8,128)S(1)}, f32[32,64,64]{2,1,0:T(8,128)}, u32[]{:S(2)}) copy-start(f32[32,64,64]{2,1,0:T(8,128)} %param.21) | copy-start | bytes 1572868
  3.2 12.4 %all-to-all-start = ((f32[8,1,6144]{2,1,0:T(1,128)}), f32[8,1,6144]{2,1,0:T(1,128)S(1)}, u32[]{:S(2)}, u32[]{:S(2)}) async-start(f32[8,1,6144]{2,1,0:T(1,128)} %all_to_all.24), calls=%async_computation | async-start | bytes 393216 | tf_op jit(solution)/shard_map/all_to_all | solution.py:66
  20.6 25.3 %all-to-all-start.1 = ((f32[256,1,8]{2,1,0:T(1,128)}), f32[256,1,8]{2,1,0:T(1,128)S(1)}, u32[]{:S(2)}, u32[]{:S(2)}) async-start(f32[256,1,8]{2,1,0:T(1,128)} %copy.70), calls=%async_computation.1 | async-start | bytes 262144 | tf_op jit(solution)/shard_map/all_to_all | solution.py:88
  48.5 37.3 %copy-start.1 = (f32[16,2,512]{2,1,0:T(2,128)S(1)}, f32[16,2,512]{2,1,0:T(2,128)}, u32[]{:S(2)}) copy-start(f32[16,2,512]{2,1,0:T(2,128)} %param.14) | copy-start | bytes 196612
  48.5 37.3 %copy-start.6 = (f32[512]{0:T(512)S(1)}, f32[512]{0:T(512)}, u32[]{:S(2)}) copy-start(f32[512]{0:T(512)} %param.15) | copy-start | bytes 6148
  50.9 35.1 %copy-start.2 = (f32[16,2,512]{2,1,0:T(2,128)S(1)}, f32[16,2,512]{2,1,0:T(2,128)}, u32[]{:S(2)}) copy-start(f32[16,2,512]{2,1,0:T(2,128)} %param.13) | copy-start | bytes 196612
  50.9 35.1 %copy-start.4 = (f32[512]{0:T(512)S(1)}, f32[512]{0:T(512)}, u32[]{:S(2)}) copy-start(f32[512]{0:T(512)} %param.16) | copy-start | bytes 6148
  53.3 52.1 %copy-start.3 = (f32[16,2,512]{2,1,0:T(2,128)S(1)}, f32[16,2,512]{2,1,0:T(2,128)}, u32[]{:S(2)}) copy-start(f32[16,2,512]{2,1,0:T(2,128)} %param.12) | copy-start | bytes 196612
  63.5 18.5 %all-to-all-start.2 = ((bf16[256,1,64]{2,1,0:T(2,128)(2,1)}), bf16[256,1,64]{2,1,0:T(2,128)(2,1)S(1)}, u32[]{:S(2)}, u32[]{:S(2)}) async-start(bf16[256,1,64]{2,1,0:T(2,128)(2,1)} %copy.77), calls=%async_computation.2 | async-start | bytes 262144 | tf_op jit(solution)/shard_map/all_to_all | solution.py:121

commit v9 on v4

--- a/solution.py
+++ b/solution.py
@@ -9,7 +9,7 @@
 TILE = 64
 
 
-precise = lax.Precision.HIGHEST
+precise = lax.Precision.HIGH
 EVERY = ("blk", "band")
 
 

time: 96.3 us -> 94.9 us (0.985)
  matrix products: 10.8 us -> 9.45 us
where the time goes in v9:
time: 94.9 us; the launch traced here: 94.5 us
  blocking collectives  36.3 us (38%)
  starting transfers between devices  19.2 us (20%)
  waiting for transfers between devices  11.9 us (13%)
  local copies, waits for them, and re-layouts  10.3 us (11%)
  matrix products  9.45 us (10%)
  other arithmetic  6.13 us (6%)
  between operations  1.05 us (1%)
    all_to_all x1, blocking collectives, per_device(): lax.all_to_all(returning, EVERY, split_axis=0, concat_axis=0, tiled=True)  18.2 us
    all_to_all x1, blocking collectives, per_device(): lax.all_to_all(shared, EVERY, split_axis=0, concat_axis=0, tiled=True)  18.2 us
    all_to_all x1, starting transfers between devices, per_device(): lax.all_to_all(outgoing, EVERY, split_axis=0, concat_axis=0, tiled=True)  12.7 us
    all_to_all x1, waiting for transfers between devices, per_device(): lax.all_to_all(outgoing, EVERY, split_axis=0, concat_axis=0, tiled=True)  10.6 us
    all_to_all x1, starting transfers between devices, per_device(): lax.all_to_all(beam_window.reshape(nband, width), 'band', split_axis=0, c...  6.58 us
  transfers between devices with their start and end apart: 2, of which 2 were waited for; matrix products, arithmetic and copies ran while one was open for 6% of the time, Pallas kernels for 0%

profile of v9, /device:TPU:1, one launch (start us, length us, event | category | flops | bytes accessed | tf_op | source)
XLA Modules:
  0.0 94.5 jit_solution(10837659563820589955)
XLA Ops:
  0.7 6.6 %all-to-all-start = ((f32[8,1,512]{2,1,0:T(1,128)}), f32[8,1,512]{2,1,0:T(1,128)S(1)}, u32[]{:S(2)}, u32[]{:S(2)}) async-start(f32[8,1,512]{2,1,0:T(1,128)} %bitcast.81), calls=%async_computation | async-start | bytes 32768 | tf_op jit(solution)/shard_map/all_to_all | solution.py:62
  7.2 1.3 %fusion.46 = (f32[512,64]{0,1:T(8,128)S(1)}, f32[512,64]{0,1:T(8,128)S(1)}) fusion(s32[64]{0:T(128)S(1)} %iota_multiply_fusion, s32[512]{0:T(512)} %param.19), kind=kLoop, calls=%fused_computation.71 | loop fusion | flops 458752 | bytes 264448 | tf_op jit(solution)/shard_map/cos | solution.py:20
  8.5 0.7 iota_compare_fusion
  9.2 1.0 %mul.277 = f32[16,8,2,512]{3,2,1,0:T(2,128)S(1)} broadcast(f32[16,2,512]{2,1,0:T(2,128)} %param.14), dimensions={0,2,3} | broadcast | bytes 589824 | tf_op jit(solution)/shard_map/mul | solution.py:67
  10.5 1.4 %all-to-all-done = f32[8,1,512]{2,1,0:T(1,128)S(1)} async-done(((f32[8,1,512]{2,1,0:T(1,128)}), f32[8,1,512]{2,1,0:T(1,128)S(1)}, u32[]{:S(2)}, u32[]{:S(2)}) %all-to-all-start) | async-done | bytes 16416 | tf_op jit(solution)/shard_map/all_to_all | solution.py:62
  12.0 1.6 %fusion.4 = f32[16,16,64]{2,1,0:T(8,128)S(1)} fusion(bf16[16,64,4096]{2,1,0:T(8,128)(2,1)} %param.18, s32[]{:T(128)S(6)} %select_n.35, f32[16,16,512]{2,1,0:T(8,128)S(1)} %mul.278, f32[16,512]{1,0:T(8,128)S(1)} %mul.275), kind=kOutput, calls=%fused_computation.11 | convolution fusion | flops 17039360 | bytes 1671172 | tf_op jit(solution)/shard_map/sql,srl->sqr/dot_general | solution.py:69
  13.8 0.9 copy.69
  15.3 0.7 copy.70
  16.0 12.7 %all-to-all-start.1 = ((f32[256,1,64]{2,1,0:T(1,128)}), f32[256,1,64]{2,1,0:T(1,128)S(1)}, u32[]{:S(2)}, u32[]{:S(2)}) async-start(f32[256,1,64]{2,1,0:T(1,128)} %copy.70), calls=%async_computation.1 | async-start | bytes 262144 | tf_op jit(solution)/shard_map/all_to_all | solution.py:75
  28.7 0.7 compare_select_fusion
  29.3 1.6 %copy.74 = f32[32,64,64]{1,2,0:T(8,128)S(1)} copy(f32[32,64,64]{2,1,0:T(8,128)} %param.21) | data formatting | bytes 1048576 | tf_op args[9]
  30.9 10.6 %all-to-all-done.1 = f32[256,1,64]{2,1,0:T(1,128)S(1)} async-done(((f32[256,1,64]{2,1,0:T(1,128)}), f32[256,1,64]{2,1,0:T(1,128)S(1)}, u32[]{:S(2)}, u32[]{:S(2)}) %all-to-all-start.1) | async-done | bytes 65568 | tf_op jit(solution)/shard_map/all_to_all | solution.py:75
  42.8 1.3 %fusion.12 = f32[2,64,128]{2,1,0:T(8,128)S(1)} fusion(f32[512,64]{0,1:T(8,128)S(1)} %get-tuple-element.26, f32[512,2]{0,1:T(2,128)S(1)} %get-tuple-element.24, f32[512,64]{0,1:T(8,128)S(1)} %get-tuple-element.25, f32[512,2]{0,1:T(2,128)S(1)} %get-tuple-element.23, s32[512]{0:T(512)S(1)} %copy-done.5), kind=kOutput, calls=%fused_computation.25 | convolution fusion | flops 51445760 | bytes 337920 | tf_op jit(solution)/shard_map/mra,mb->rab/dot_general | solution.py:87
  44.1 1.3 %fusion.1 = f32[2,64,128]{2,1,0:T(8,128)S(1)} fusion(f32[2,64,128]{2,1,0:T(8,128)S(1)} %fusion.12, f32[512,64]{0,1:T(8,128)S(1)} %get-tuple-element.26, f32[512,2]{0,1:T(2,128)S(1)} %get-tuple-element.24, f32[512,64]{0,1:T(8,128)S(1)} %get-tuple-element.25, f32[512,2]{0,1:T(2,128)S(1)} %get-tuple-element.23, s32[512]{0:T(512)S(1)} %copy-done.5), kind=kOutput, calls=%fused_computation.7 | convolution fusion | flops 51478528 | bytes 403456 | tf_op jit(solution)/shard_map/mra,mb->rab/dot_general | solution.py:87
  45.5 0.6 gather_fusion
  47.6 1.2 %scatter_custom_fusion = f32[256,64]{1,0:T(8,128)S(1)} fusion(s32[128]{0:T(128)S(1)} %compare_select_fusion, f32[128,64]{1,0:T(8,128)S(1)} %copy.75, f32[]{:T(128)} %constant.46.clone.1), kind=kCustom, calls=%fused_computation.68 | custom fusion | flops 8192 | bytes 65540 | tf_op jit(solution)/shard_map/scatter-add | solution.py:36
  48.9 1.3 %convolution_bitcast_fusion = f32[512,64,2]{0,1,2:T(8,128)S(1)} fusion(s32[512]{0:T(512)S(1)} %copy-done.5, f32[2,64,128]{2,1,0:T(8,128)S(1)} %reshape.225, f32[2,64,128]{2,1,0:T(8,128)S(1)} %fusion.1, f32[1,2,64,128]{3,1,2,0:T(2,128)S(1)} %bitcast.86), kind=kOutput, calls=%fused_computation.4 | convolution fusion | flops 51281920 | bytes 460800 | tf_op jit(solution)/shard_map/rab,mb->mra/dot_general | solution.py:94
  50.2 1.3 %multiply_reduce_fusion.4 = (f32[512,2]{0,1:T(2,128)S(1)}, f32[512,2]{0,1:T(2,128)S(1)}, f32[512,2]{0,1:T(2,128)S(1)}, f32[512,2]{0,1:T(2,128)S(1)}) fusion(f32[512,64]{0,1:T(8,128)S(1)} %get-tuple-element.25, f32[512,64]{0,1:T(8,128)S(1)} %get-tuple-element.26, f32[512,64,2]{0,1,2:T(8,128)S(1)} %convolution_bitcast_fusion, ...), kind=kOutput, calls=%fused_computation.30 | convolution fusion | flops 51802112 | bytes 739328 | tf_op jit(solution)/shard_map/rab,mb->mra/dot_general | solution.py:93
  52.3 18.2 %all_to_all.33 = bf16[256,1,64]{2,1,0:T(2,128)(2,1)S(1)} all-to-all(bf16[256,1,64]{2,1,0:T(2,128)(2,1)S(1)} %copy.77), channel_id=1, replica_groups=mesh['blk'=32,'band'=8] {'blk','band'}, dimensions={0} | all-to-all | bytes 65536 | tf_op jit(solution)/shard_map/all_to_all | solution.py:107
  70.5 0.6 reshape.226
  71.2 0.8 copy.79
  72.1 1.5 %fusion.2 = f32[16,16,512]{2,1,0:T(8,128)S(1)} fusion(bf16[16,16,64]{2,1,0:T(8,128)(2,1)S(1)} %copy.80, bf16[16,64,4096]{2,1,0:T(8,128)(2,1)} %param.18, s32[]{:T(128)S(6)} %select_n.35), kind=kOutput, calls=%fused_computation.9 | convolution fusion | flops 16777216 | bytes 1605636 | tf_op jit(solution)/shard_map/sqr,srl->sql/dot_general | solution.py:110
  75.2 18.2 %all_to_all.34 = f32[256,1,4]{2,1,0:T(1,128)S(1)} all-to-all(f32[256,1,4]{2,1,0:T(1,128)S(1)} %broadcast_in_dim.31), channel_id=1, replica_groups=mesh['blk'=32,'band'=8] {'blk','band'}, dimensions={0} | all-to-all | bytes 8192 | tf_op jit(solution)/shard_map/all_to_all | solution.py:123
  93.8 0.7 multiply_add_fusion
  (58 shorter events, 6.8 us)
Async XLA Ops:
  0.6 42.1 %copy-start.5 = (s32[512]{0:T(512)S(1)}, s32[512]{0:T(512)}, u32[]{:S(2)}) copy-start(s32[512]{0:T(512)} %param.19) | copy-start | bytes 6148
  0.6 45.5 %copy-start = (f32[32,64,64]{2,1,0:T(8,128)S(1)}, f32[32,64,64]{2,1,0:T(8,128)}, u32[]{:S(2)}) copy-start(f32[32,64,64]{2,1,0:T(8,128)} %param.21) | copy-start | bytes 1572868
  0.7 11.3 %all-to-all-start = ((f32[8,1,512]{2,1,0:T(1,128)}), f32[8,1,512]{2,1,0:T(1,128)S(1)}, u32[]{:S(2)}, u32[]{:S(2)}) async-start(f32[8,1,512]{2,1,0:T(1,128)} %bitcast.81), calls=%async_computation | async-start | bytes 32768 | tf_op jit(solution)/shard_map/all_to_all | solution.py:62
  16.0 25.5 %all-to-all-start.1 = ((f32[256,1,64]{2,1,0:T(1,128)}), f32[256,1,64]{2,1,0:T(1,128)S(1)}, u32[]{:S(2)}, u32[]{:S(2)}) async-start(f32[256,1,64]{2,1,0:T(1,128)} %copy.70), calls=%async_computation.1 | async-start | bytes 262144 | tf_op jit(solution)/shard_map/all_to_all | solution.py:75
  42.6 6.4 %copy-start.7 = (f32[1,2,8192]{2,1,0:T(2,128)S(1)}, f32[1,2,8192]{2,1,0:T(2,128)}, u32[]{:S(2)}) copy-start(f32[1,2,8192]{2,1,0:T(2,128)} %param.20) | copy-start | bytes 196612
  42.8 31.4 %copy-start.1 = (f32[16,2,512]{2,1,0:T(2,128)S(1)}, f32[16,2,512]{2,1,0:T(2,128)}, u32[]{:S(2)}) copy-start(f32[16,2,512]{2,1,0:T(2,128)} %param.14) | copy-start | bytes 196612
  42.8 31.4 %copy-start.6 = (f32[512]{0:T(512)S(1)}, f32[512]{0:T(512)}, u32[]{:S(2)}) copy-start(f32[512]{0:T(512)} %param.15) | copy-start | bytes 6148
  44.1 30.2 %copy-start.2 = (f32[16,2,512]{2,1,0:T(2,128)S(1)}, f32[16,2,512]{2,1,0:T(2,128)}, u32[]{:S(2)}) copy-start(f32[16,2,512]{2,1,0:T(2,128)} %param.13) | copy-start | bytes 196612
  44.1 30.2 %copy-start.4 = (f32[512]{0:T(512)S(1)}, f32[512]{0:T(512)}, u32[]{:S(2)}) copy-start(f32[512]{0:T(512)} %param.16) | copy-start | bytes 6148
  45.4 48.3 %copy-start.3 = (f32[16,2,512]{2,1,0:T(2,128)S(1)}, f32[16,2,512]{2,1,0:T(2,128)}, u32[]{:S(2)}) copy-start(f32[16,2,512]{2,1,0:T(2,128)} %param.12) | copy-start | bytes 196612

commit v10 on v9

--- a/solution.py
+++ b/solution.py
@@ -33,7 +33,10 @@
     inner_part = pick_kind(inner_all, tile_kinds)
     outer_all = jnp.einsum("kji,tj->tki", smoother_blocks, inner_part, precision=precise)
     outer_part = pick_kind(outer_all, tile_kinds)
-    return jnp.zeros_like(tile_rows).at[tile_slots].add(outer_part).reshape(pixels.shape)
+    rows = jnp.arange(tile_rows.shape[0], dtype=jnp.int32)
+    placed = (rows[:, None] == tile_slots[None, :]).astype(jnp.float32)
+    spread = jnp.dot(placed, outer_part, precision=lax.Precision.HIGHEST)
+    return spread.reshape(pixels.shape)
 
 
 def per_device(

time: 94.9 us -> 94.8 us (level)
  other arithmetic: 6.13 us -> 4.91 us
  matrix products: 9.45 us -> 10.5 us
    scatter-add x1 -> x0, other arithmetic: 1.23 us -> none  [smooth(): jnp.zeros_like(tile_rows).at[tile_slots].add(outer_part)]
where the time goes in v10:
time: 94.8 us; the launch traced here: 94.3 us
  blocking collectives  36.4 us (38%)
  starting transfers between devices  19.2 us (20%)
  waiting for transfers between devices  11.9 us (13%)
  matrix products  10.5 us (11%)
  local copies, waits for them, and re-layouts  10.3 us (11%)
  other arithmetic  4.91 us (5%)
  between operations  1.06 us (1%)
    all_to_all x1, blocking collectives, per_device(): lax.all_to_all(shared, EVERY, split_axis=0, concat_axis=0, tiled=True)  18.2 us
    all_to_all x1, blocking collectives, per_device(): lax.all_to_all(returning, EVERY, split_axis=0, concat_axis=0, tiled=True)  18.2 us
    all_to_all x1, starting transfers between devices, per_device(): lax.all_to_all(outgoing, EVERY, split_axis=0, concat_axis=0, tiled=True)  12.7 us
    all_to_all x1, waiting for transfers between devices, per_device(): lax.all_to_all(outgoing, EVERY, split_axis=0, concat_axis=0, tiled=True)  10.6 us
    all_to_all x1, starting transfers between devices, per_device(): lax.all_to_all(beam_window.reshape(nband, width), 'band', split_axis=0, c...  6.58 us
    dot_general x1, matrix products, per_device(): jnp.einsum('rab,mb->mra', noisy_grid, inner_sin, precision=precise)  2.12 us
  transfers between devices with their start and end apart: 2, of which 2 were waited for; matrix products, arithmetic and copies ran while one was open for 6% of the time, Pallas kernels for 0%

profile of v10, /device:TPU:1, one launch (start us, length us, event | category | flops | bytes accessed | tf_op | source)
XLA Modules:
  0.0 94.3 jit_solution(4595005623809292977)
XLA Ops:
  0.7 6.6 %all-to-all-start = ((f32[8,1,512]{2,1,0:T(1,128)}), f32[8,1,512]{2,1,0:T(1,128)S(1)}, u32[]{:S(2)}, u32[]{:S(2)}) async-start(f32[8,1,512]{2,1,0:T(1,128)} %bitcast.82), calls=%async_computation | async-start | bytes 32768 | tf_op jit(solution)/shard_map/all_to_all | solution.py:65
  7.2 1.3 %fusion.46 = (f32[512,64]{0,1:T(8,128)S(1)}, f32[512,64]{0,1:T(8,128)S(1)}) fusion(s32[64]{0:T(128)S(1)} %iota_multiply_fusion, s32[512]{0:T(512)} %param.19), kind=kLoop, calls=%fused_computation.71 | loop fusion | flops 458752 | bytes 264448 | tf_op jit(solution)/shard_map/cos | solution.py:20
  8.5 0.7 iota_compare_fusion.2
  9.2 1.0 %mul.277 = f32[16,8,2,512]{3,2,1,0:T(2,128)S(1)} broadcast(f32[16,2,512]{2,1,0:T(2,128)} %param.14), dimensions={0,2,3} | broadcast | bytes 589824 | tf_op jit(solution)/shard_map/mul | solution.py:70
  10.5 1.4 %all-to-all-done = f32[8,1,512]{2,1,0:T(1,128)S(1)} async-done(((f32[8,1,512]{2,1,0:T(1,128)}), f32[8,1,512]{2,1,0:T(1,128)S(1)}, u32[]{:S(2)}, u32[]{:S(2)}) %all-to-all-start) | async-done | bytes 16416 | tf_op jit(solution)/shard_map/all_to_all | solution.py:65
  12.0 1.6 %fusion.4 = f32[16,16,64]{2,1,0:T(8,128)S(1)} fusion(bf16[16,64,4096]{2,1,0:T(8,128)(2,1)} %param.18, s32[]{:T(128)S(6)} %select_n.34, f32[16,16,512]{2,1,0:T(8,128)S(1)} %mul.278, f32[16,512]{1,0:T(8,128)S(1)} %mul.275), kind=kOutput, calls=%fused_computation.10 | convolution fusion | flops 17039360 | bytes 1671172 | tf_op jit(solution)/shard_map/sql,srl->sqr/dot_general | solution.py:72
  13.8 0.9 copy.58
  15.3 0.7 copy.59
  16.0 12.7 %all-to-all-start.1 = ((f32[256,1,64]{2,1,0:T(1,128)}), f32[256,1,64]{2,1,0:T(1,128)S(1)}, u32[]{:S(2)}, u32[]{:S(2)}) async-start(f32[256,1,64]{2,1,0:T(1,128)} %copy.59), calls=%async_computation.1 | async-start | bytes 262144 | tf_op jit(solution)/shard_map/all_to_all | solution.py:78
  28.7 0.7 compare_select_fusion
  29.4 1.6 %copy.63 = f32[32,64,64]{1,2,0:T(8,128)S(1)} copy(f32[32,64,64]{2,1,0:T(8,128)} %param.21) | data formatting | bytes 1048576 | tf_op args[9]
  30.9 10.6 %all-to-all-done.1 = f32[256,1,64]{2,1,0:T(1,128)S(1)} async-done(((f32[256,1,64]{2,1,0:T(1,128)}), f32[256,1,64]{2,1,0:T(1,128)S(1)}, u32[]{:S(2)}, u32[]{:S(2)}) %all-to-all-start.1) | async-done | bytes 65568 | tf_op jit(solution)/shard_map/all_to_all | solution.py:78
  42.8 1.3 %fusion.12 = f32[2,64,128]{2,1,0:T(8,128)S(1)} fusion(f32[512,64]{0,1:T(8,128)S(1)} %get-tuple-element.26, f32[512,2]{0,1:T(2,128)S(1)} %get-tuple-element.24, f32[512,64]{0,1:T(8,128)S(1)} %get-tuple-element.25, f32[512,2]{0,1:T(2,128)S(1)} %get-tuple-element.23, s32[512]{0:T(512)S(1)} %copy-done.5), kind=kOutput, calls=%fused_computation.24 | convolution fusion | flops 51445760 | bytes 337920 | tf_op jit(solution)/shard_map/mra,mb->rab/dot_general | solution.py:90
  44.1 1.3 %fusion.1 = f32[2,64,128]{2,1,0:T(8,128)S(1)} fusion(f32[2,64,128]{2,1,0:T(8,128)S(1)} %fusion.12, f32[512,64]{0,1:T(8,128)S(1)} %get-tuple-element.26, f32[512,2]{0,1:T(2,128)S(1)} %get-tuple-element.24, f32[512,64]{0,1:T(8,128)S(1)} %get-tuple-element.25, f32[512,2]{0,1:T(2,128)S(1)} %get-tuple-element.23, s32[512]{0:T(512)S(1)} %copy-done.5), kind=kOutput, calls=%fused_computation.6 | convolution fusion | flops 51478528 | bytes 403456 | tf_op jit(solution)/shard_map/mra,mb->rab/dot_general | solution.py:90
  45.5 0.6 gather_fusion
  46.2 0.6 fusion
  47.8 2.1 %convolution_bitcast_fusion = f32[512,64,2]{0,1,2:T(8,128)S(1)} fusion(s32[512]{0:T(512)S(1)} %copy-done.5, f32[2,64,128]{2,1,0:T(8,128)S(1)} %reshape.226, f32[2,64,128]{2,1,0:T(8,128)S(1)} %fusion.1, f32[1,2,64,128]{3,1,2,0:T(2,128)} %bitcast.87), kind=kOutput, calls=%fused_computation.3 | convolution fusion | flops 51281920 | bytes 460800 | tf_op jit(solution)/shard_map/rab,mb->mra/dot_general | solution.py:97
  49.9 1.3 %multiply_reduce_fusion.4 = (f32[512,2]{0,1:T(2,128)S(1)}, f32[512,2]{0,1:T(2,128)S(1)}, f32[512,2]{0,1:T(2,128)S(1)}, f32[512,2]{0,1:T(2,128)S(1)}) fusion(f32[512,64]{0,1:T(8,128)S(1)} %get-tuple-element.25, f32[512,64]{0,1:T(8,128)S(1)} %get-tuple-element.26, f32[512,64,2]{0,1,2:T(8,128)S(1)} %convolution_bitcast_fusion, ...), kind=kOutput, calls=%fused_computation.29 | convolution fusion | flops 51802112 | bytes 739328 | tf_op jit(solution)/shard_map/rab,mb->mra/dot_general | solution.py:96
  52.0 18.2 %all_to_all.33 = bf16[256,1,64]{2,1,0:T(2,128)(2,1)S(1)} all-to-all(bf16[256,1,64]{2,1,0:T(2,128)(2,1)S(1)} %copy.66), channel_id=1, replica_groups=mesh['blk'=32,'band'=8] {'blk','band'}, dimensions={0} | all-to-all | bytes 65536 | tf_op jit(solution)/shard_map/all_to_all | solution.py:110
  70.3 0.6 reshape.227
  70.9 0.8 copy.68
  71.9 1.5 %fusion.2 = f32[16,16,512]{2,1,0:T(8,128)S(1)} fusion(bf16[16,16,64]{2,1,0:T(8,128)(2,1)S(1)} %copy.69, bf16[16,64,4096]{2,1,0:T(8,128)(2,1)} %param.18, s32[]{:T(128)S(6)} %select_n.34), kind=kOutput, calls=%fused_computation.8 | convolution fusion | flops 16777216 | bytes 1605636 | tf_op jit(solution)/shard_map/sqr,srl->sql/dot_general | solution.py:113
  74.9 18.2 %all_to_all.34 = f32[256,1,4]{2,1,0:T(1,128)S(1)} all-to-all(f32[256,1,4]{2,1,0:T(1,128)S(1)} %broadcast_in_dim.28), channel_id=1, replica_groups=mesh['blk'=32,'band'=8] {'blk','band'}, dimensions={0} | all-to-all | bytes 8192 | tf_op jit(solution)/shard_map/all_to_all | solution.py:126
  93.6 0.7 multiply_add_fusion
  (59 shorter events, 6.3 us)
Async XLA Ops:
  0.6 42.1 %copy-start.5 = (s32[512]{0:T(512)S(1)}, s32[512]{0:T(512)}, u32[]{:S(2)}) copy-start(s32[512]{0:T(512)} %param.19) | copy-start | bytes 6148
  0.6 45.5 %copy-start = (f32[32,64,64]{2,1,0:T(8,128)S(1)}, f32[32,64,64]{2,1,0:T(8,128)}, u32[]{:S(2)}) copy-start(f32[32,64,64]{2,1,0:T(8,128)} %param.21) | copy-start | bytes 1572868
  0.7 11.3 %all-to-all-start = ((f32[8,1,512]{2,1,0:T(1,128)}), f32[8,1,512]{2,1,0:T(1,128)S(1)}, u32[]{:S(2)}, u32[]{:S(2)}) async-start(f32[8,1,512]{2,1,0:T(1,128)} %bitcast.82), calls=%async_computation | async-start | bytes 32768 | tf_op jit(solution)/shard_map/all_to_all | solution.py:65
  13.6 33.9 %copy-start.7 = (s32[128]{0:T(128)S(1)}, s32[128]{0:T(128)}, u32[]{:S(2)}) copy-start(s32[128]{0:T(128)} %param.22) | copy-start | bytes 1540
  16.0 25.5 %all-to-all-start.1 = ((f32[256,1,64]{2,1,0:T(1,128)}), f32[256,1,64]{2,1,0:T(1,128)S(1)}, u32[]{:S(2)}, u32[]{:S(2)}) async-start(f32[256,1,64]{2,1,0:T(1,128)} %copy.59), calls=%async_computation.1 | async-start | bytes 262144 | tf_op jit(solution)/shard_map/all_to_all | solution.py:78
  42.6 7.4 %copy-start.8 = (f32[1,2,8192]{2,1,0:T(2,128)S(1)}, f32[1,2,8192]{2,1,0:T(2,128)}, u32[]{:S(2)}) copy-start(f32[1,2,8192]{2,1,0:T(2,128)} %param.20) | copy-start | bytes 196612
  42.8 31.1 %copy-start.1 = (f32[16,2,512]{2,1,0:T(2,128)S(1)}, f32[16,2,512]{2,1,0:T(2,128)}, u32[]{:S(2)}) copy-start(f32[16,2,512]{2,1,0:T(2,128)} %param.14) | copy-start | bytes 196612
  42.8 31.1 %copy-start.6 = (f32[512]{0:T(512)S(1)}, f32[512]{0:T(512)}, u32[]{:S(2)}) copy-start(f32[512]{0:T(512)} %param.15) | copy-start | bytes 6148
  44.1 30.0 %copy-start.2 = (f32[16,2,512]{2,1,0:T(2,128)S(1)}, f32[16,2,512]{2,1,0:T(2,128)}, u32[]{:S(2)}) copy-start(f32[16,2,512]{2,1,0:T(2,128)} %param.13) | copy-start | bytes 196612
  44.1 30.0 %copy-start.4 = (f32[512]{0:T(512)S(1)}, f32[512]{0:T(512)}, u32[]{:S(2)}) copy-start(f32[512]{0:T(512)} %param.16) | copy-start | bytes 6148
  45.4 48.1 %copy-start.3 = (f32[16,2,512]{2,1,0:T(2,128)S(1)}, f32[16,2,512]{2,1,0:T(2,128)}, u32[]{:S(2)}) copy-start(f32[16,2,512]{2,1,0:T(2,128)} %param.12) | copy-start | bytes 196612

commit v11 on v10

--- a/solution.py
+++ b/solution.py
@@ -28,13 +28,13 @@
 
 def smooth(pixels, smoother_blocks, tile_slots, tile_kinds):
     tile_rows = pixels.reshape(-1, TILE)
-    picked = tile_rows[tile_slots]
+    rows = jnp.arange(tile_rows.shape[0], dtype=jnp.int32)
+    placed = (rows[:, None] == tile_slots[None, :]).astype(jnp.float32)
+    picked = jnp.dot(placed.T, tile_rows, precision=lax.Precision.HIGHEST)
     inner_all = jnp.einsum("kij,tj->tki", smoother_blocks, picked, precision=precise)
     inner_part = pick_kind(inner_all, tile_kinds)
     outer_all = jnp.einsum("kji,tj->tki", smoother_blocks, inner_part, precision=precise)
     outer_part = pick_kind(outer_all, tile_kinds)
-    rows = jnp.arange(tile_rows.shape[0], dtype=jnp.int32)
-    placed = (rows[:, None] == tile_slots[None, :]).astype(jnp.float32)
     spread = jnp.dot(placed, outer_part, precision=lax.Precision.HIGHEST)
     return spread.reshape(pixels.shape)
 

time: 94.8 us -> 97.1 us (1.024)
  other arithmetic: 4.91 us -> 3.58 us
  waiting for transfers between devices: 11.9 us -> 13.2 us
  local copies, waits for them, and re-layouts: 10.3 us -> 11.4 us
    all_to_all x1, waiting for transfers between devices: 10.6 us -> 12.8 us  [per_device(): lax.all_to_all(outgoing, EVERY, split_axis=0, concat_axis=0, tiled=True)]
    transpose x1, local copies, waits for them, and re-layouts: 0.94 us -> 1.92 us  [per_device(): outgoing = partial.transpose(3, 1, 0, 2, 4).reshape(nblk * nband, chunk)]
  transfers between devices with their start and end apart: 2 -> 2, of which waited for: 2 -> 2; matrix products, arithmetic and copies ran while one was open for 6% -> 4% of each run, Pallas kernels for 0% -> 0%
where the time goes in v11:
time: 97.1 us; the launch traced here: 96.6 us
  blocking collectives  36.4 us (37%)
  starting transfers between devices  20.1 us (21%)
  waiting for transfers between devices  13.2 us (14%)
  local copies, waits for them, and re-layouts  11.4 us (12%)
  matrix products  10.7 us (11%)
  other arithmetic  3.58 us (4%)
  between operations  1.08 us (1%)
    all_to_all x1, blocking collectives, per_device(): lax.all_to_all(shared, EVERY, split_axis=0, concat_axis=0, tiled=True)  18.2 us
    all_to_all x1, blocking collectives, per_device(): lax.all_to_all(returning, EVERY, split_axis=0, concat_axis=0, tiled=True)  18.2 us
    all_to_all x1, starting transfers between devices, per_device(): lax.all_to_all(outgoing, EVERY, split_axis=0, concat_axis=0, tiled=True)  13.6 us
    all_to_all x1, waiting for transfers between devices, per_device(): lax.all_to_all(outgoing, EVERY, split_axis=0, concat_axis=0, tiled=True)  12.8 us
    all_to_all x1, starting transfers between devices, per_device(): lax.all_to_all(beam_window.reshape(nband, width), 'band', split_axis=0, c...  6.58 us
    dot_general x1, matrix products, per_device(): jnp.einsum('rab,mb->mra', noisy_grid, inner_sin, precision=precise)  2.12 us
  transfers between devices with their start and end apart: 2, of which 2 were waited for; matrix products, arithmetic and copies ran while one was open for 4% of the time, Pallas kernels for 0%

profile of v11, /device:TPU:1, one launch (start us, length us, event | category | flops | bytes accessed | tf_op | source)
XLA Modules:
  0.0 96.6 jit_solution(8428610473056878698)
XLA Ops:
  0.7 6.6 %all-to-all-start = ((f32[8,1,512]{2,1,0:T(1,128)}), f32[8,1,512]{2,1,0:T(1,128)S(1)}, u32[]{:S(2)}, u32[]{:S(2)}) async-start(f32[8,1,512]{2,1,0:T(1,128)} %bitcast.83), calls=%async_computation | async-start | bytes 32768 | tf_op jit(solution)/shard_map/all_to_all | solution.py:65
  7.3 1.3 %fusion.46 = (f32[512,64]{0,1:T(8,128)S(1)}, f32[512,64]{0,1:T(8,128)S(1)}) fusion(s32[64]{0:T(128)S(1)} %iota_multiply_fusion, s32[512]{0:T(512)} %param.19), kind=kLoop, calls=%fused_computation.71 | loop fusion | flops 458752 | bytes 264448 | tf_op jit(solution)/shard_map/cos | solution.py:20
  8.5 1.0 %mul.277 = f32[16,8,2,512]{3,2,1,0:T(2,128)S(1)} broadcast(f32[16,2,512]{2,1,0:T(2,128)} %param.14), dimensions={0,2,3} | broadcast | bytes 589824 | tf_op jit(solution)/shard_map/mul | solution.py:70
  9.9 1.6 %copy.59 = f32[32,64,64]{1,2,0:T(8,128)S(1)} copy(f32[32,64,64]{2,1,0:T(8,128)} %param.21) | data formatting | bytes 1048576 | tf_op args[9]
  12.0 1.6 %fusion.4 = f32[16,16,64]{2,1,0:T(8,128)S(1)} fusion(bf16[16,64,4096]{2,1,0:T(8,128)(2,1)} %param.18, s32[]{:T(128)S(6)} %select_n.31, f32[16,16,512]{2,1,0:T(8,128)S(1)} %mul.278, f32[16,512]{1,0:T(8,128)S(1)} %mul.275), kind=kOutput, calls=%fused_computation.10 | convolution fusion | flops 17039360 | bytes 1671172 | tf_op jit(solution)/shard_map/sql,srl->sqr/dot_general | solution.py:72
  13.6 1.0 %copy.54 = f32[16,16,64]{0,2,1:T(8,128)} copy(f32[16,16,64]{2,1,0:T(8,128)S(1)} %fusion.4) | data formatting | bytes 131072 | tf_op jit(solution)/shard_map/sql,srl->sqr/dot_general | solution.py:72
  14.6 1.9 %copy.55 = f32[32,8,16,2,2]{1,0,4,3,2:T(8,128)S(1)} copy(f32[32,8,16,2,2]{2,4,0,3,1:T(2,128)} %bitcast.78) | data formatting | bytes 131072 | tf_op jit(solution)/shard_map/transpose | solution.py:77
  16.5 0.5 all_to_all.24
  17.1 0.7 copy.56
  17.8 13.6 %all-to-all-start.1 = ((f32[256,1,64]{2,1,0:T(1,128)}), f32[256,1,64]{2,1,0:T(1,128)S(1)}, u32[]{:S(2)}, u32[]{:S(2)}) async-start(f32[256,1,64]{2,1,0:T(1,128)} %copy.56), calls=%async_computation.1 | async-start | bytes 262144 | tf_op jit(solution)/shard_map/all_to_all | solution.py:78
  31.4 12.8 %all-to-all-done.1 = f32[256,1,64]{2,1,0:T(1,128)S(1)} async-done(((f32[256,1,64]{2,1,0:T(1,128)}), f32[256,1,64]{2,1,0:T(1,128)S(1)}, u32[]{:S(2)}, u32[]{:S(2)}) %all-to-all-start.1) | async-done | bytes 65568 | tf_op jit(solution)/shard_map/all_to_all | solution.py:78
  44.3 0.6 reshape.224
  45.5 1.3 %fusion.12 = f32[2,64,128]{2,1,0:T(8,128)S(1)} fusion(f32[512,64]{0,1:T(8,128)S(1)} %get-tuple-element.26, f32[512,2]{0,1:T(2,128)S(1)} %get-tuple-element.24, f32[512,64]{0,1:T(8,128)S(1)} %get-tuple-element.25, f32[512,2]{0,1:T(2,128)S(1)} %get-tuple-element.23, s32[512]{0:T(512)S(1)} %copy-done.5), kind=kOutput, calls=%fused_computation.24 | convolution fusion | flops 51445760 | bytes 337920 | tf_op jit(solution)/shard_map/mra,mb->rab/dot_general | solution.py:90
  46.8 1.3 %fusion.1 = f32[2,64,128]{2,1,0:T(8,128)S(1)} fusion(f32[2,64,128]{2,1,0:T(8,128)S(1)} %fusion.12, f32[512,64]{0,1:T(8,128)S(1)} %get-tuple-element.26, f32[512,2]{0,1:T(2,128)S(1)} %get-tuple-element.24, f32[512,64]{0,1:T(8,128)S(1)} %get-tuple-element.25, f32[512,2]{0,1:T(2,128)S(1)} %get-tuple-element.23, s32[512]{0:T(512)S(1)} %copy-done.5), kind=kOutput, calls=%fused_computation.5 | convolution fusion | flops 51478528 | bytes 403456 | tf_op jit(solution)/shard_map/mra,mb->rab/dot_general | solution.py:90
  48.5 0.6 fusion
  49.1 0.6 fusion.71
  50.1 2.1 %convolution_bitcast_fusion = f32[512,64,2]{0,1,2:T(8,128)S(1)} fusion(s32[512]{0:T(512)S(1)} %copy-done.5, f32[2,64,128]{2,1,0:T(8,128)S(1)} %reshape.226, f32[2,64,128]{2,1,0:T(8,128)S(1)} %fusion.1, f32[1,2,64,128]{3,1,2,0:T(2,128)} %bitcast.88), kind=kOutput, calls=%fused_computation.2 | convolution fusion | flops 51281920 | bytes 460800 | tf_op jit(solution)/shard_map/rab,mb->mra/dot_general | solution.py:97
  52.2 1.3 %multiply_reduce_fusion.4 = (f32[512,2]{0,1:T(2,128)S(1)}, f32[512,2]{0,1:T(2,128)S(1)}, f32[512,2]{0,1:T(2,128)S(1)}, f32[512,2]{0,1:T(2,128)S(1)}) fusion(f32[512,64]{0,1:T(8,128)S(1)} %get-tuple-element.25, f32[512,64]{0,1:T(8,128)S(1)} %get-tuple-element.26, f32[512,64,2]{0,1,2:T(8,128)S(1)} %convolution_bitcast_fusion, ...), kind=kOutput, calls=%fused_computation.29 | convolution fusion | flops 51802112 | bytes 739328 | tf_op jit(solution)/shard_map/rab,mb->mra/dot_general | solution.py:96
  54.3 18.2 %all_to_all.33 = bf16[256,1,64]{2,1,0:T(2,128)(2,1)S(1)} all-to-all(bf16[256,1,64]{2,1,0:T(2,128)(2,1)S(1)} %copy.62), channel_id=1, replica_groups=mesh['blk'=32,'band'=8] {'blk','band'}, dimensions={0} | all-to-all | bytes 65536 | tf_op jit(solution)/shard_map/all_to_all | solution.py:110
  72.6 0.6 reshape.227
  73.2 0.8 copy.64
  74.1 1.5 %fusion.2 = f32[16,16,512]{2,1,0:T(8,128)S(1)} fusion(bf16[16,16,64]{2,1,0:T(8,128)(2,1)S(1)} %copy.65, bf16[16,64,4096]{2,1,0:T(8,128)(2,1)} %param.18, s32[]{:T(128)S(6)} %select_n.31), kind=kOutput, calls=%fused_computation.8 | convolution fusion | flops 16777216 | bytes 1605636 | tf_op jit(solution)/shard_map/sqr,srl->sql/dot_general | solution.py:113
  77.2 18.2 %all_to_all.34 = f32[256,1,4]{2,1,0:T(1,128)S(1)} all-to-all(f32[256,1,4]{2,1,0:T(1,128)S(1)} %broadcast_in_dim.25), channel_id=1, replica_groups=mesh['blk'=32,'band'=8] {'blk','band'}, dimensions={0} | all-to-all | bytes 8192 | tf_op jit(solution)/shard_map/all_to_all | solution.py:126
  95.9 0.7 multiply_add_fusion
  (59 shorter events, 5.2 us)
Async XLA Ops:
  0.6 44.8 %copy-start.5 = (s32[512]{0:T(512)S(1)}, s32[512]{0:T(512)}, u32[]{:S(2)}) copy-start(s32[512]{0:T(512)} %param.19) | copy-start | bytes 6148
  0.6 47.9 %copy-start = (f32[32,64,64]{2,1,0:T(8,128)S(1)}, f32[32,64,64]{2,1,0:T(8,128)}, u32[]{:S(2)}) copy-start(f32[32,64,64]{2,1,0:T(8,128)} %param.21) | copy-start | bytes 1572868
  0.7 30.7 %copy-start.8 = (s32[128]{0:T(128)S(1)}, s32[128]{0:T(128)}, u32[]{:S(2)}) copy-start(s32[128]{0:T(128)} %param.23) | copy-start | bytes 1540
  0.7 47.6 %copy-start.7 = (s32[128]{0:T(128)S(1)}, s32[128]{0:T(128)}, u32[]{:S(2)}) copy-start(s32[128]{0:T(128)} %param.22) | copy-start | bytes 1540
  0.7 11.3 %all-to-all-start = ((f32[8,1,512]{2,1,0:T(1,128)}), f32[8,1,512]{2,1,0:T(1,128)S(1)}, u32[]{:S(2)}, u32[]{:S(2)}) async-start(f32[8,1,512]{2,1,0:T(1,128)} %bitcast.83), calls=%async_computation | async-start | bytes 32768 | tf_op jit(solution)/shard_map/all_to_all | solution.py:65
  17.8 26.4 %all-to-all-start.1 = ((f32[256,1,64]{2,1,0:T(1,128)}), f32[256,1,64]{2,1,0:T(1,128)S(1)}, u32[]{:S(2)}, u32[]{:S(2)}) async-start(f32[256,1,64]{2,1,0:T(1,128)} %copy.56), calls=%async_computation.1 | async-start | bytes 262144 | tf_op jit(solution)/shard_map/all_to_all | solution.py:78
  45.3 7.0 %copy-start.9 = (f32[1,2,8192]{2,1,0:T(2,128)S(1)}, f32[1,2,8192]{2,1,0:T(2,128)}, u32[]{:S(2)}) copy-start(f32[1,2,8192]{2,1,0:T(2,128)} %param.20) | copy-start | bytes 196612
  45.4 30.8 %copy-start.1 = (f32[16,2,512]{2,1,0:T(2,128)S(1)}, f32[16,2,512]{2,1,0:T(2,128)}, u32[]{:S(2)}) copy-start(f32[16,2,512]{2,1,0:T(2,128)} %param.14) | copy-start | bytes 196612
  45.4 30.8 %copy-start.6 = (f32[512]{0:T(512)S(1)}, f32[512]{0:T(512)}, u32[]{:S(2)}) copy-start(f32[512]{0:T(512)} %param.15) | copy-start | bytes 6148
  45.5 30.9 %copy-start.2 = (f32[16,2,512]{2,1,0:T(2,128)S(1)}, f32[16,2,512]{2,1,0:T(2,128)}, u32[]{:S(2)}) copy-start(f32[16,2,512]{2,1,0:T(2,128)} %param.13) | copy-start | bytes 196612
  45.5 30.9 %copy-start.4 = (f32[512]{0:T(512)S(1)}, f32[512]{0:T(512)}, u32[]{:S(2)}) copy-start(f32[512]{0:T(512)} %param.16) | copy-start | bytes 6148
  46.8 49.0 %copy-start.3 = (f32[16,2,512]{2,1,0:T(2,128)S(1)}, f32[16,2,512]{2,1,0:T(2,128)}, u32[]{:S(2)}) copy-start(f32[16,2,512]{2,1,0:T(2,128)} %param.12) | copy-start | bytes 196612

commit v12 on v10

--- a/solution.py
+++ b/solution.py
@@ -109,10 +109,12 @@
     returning = jnp.broadcast_to(per_owner, (nblk, nband, chunk)).reshape(nblk * nband, chunk)
     arrived = lax.all_to_all(returning, EVERY, split_axis=0, concat_axis=0, tiled=True)
     mode_terms = arrived.reshape(nblk, nband, orders_dev, parts, cycles_dev)
-    mode_terms = mode_terms.transpose(2, 1, 3, 0, 4).reshape(orders_dev, nband * parts, cycles_all)
     harmonic = jnp.einsum(
-        "sqr,srl->sql", mode_terms, legendre_here, preferred_element_type=jnp.float32
-    ).reshape(orders_dev, nband, parts, width)
+        "kbscj,skjl->sbcl",
+        mode_terms,
+        legendre_here.reshape(orders_dev, nblk, cycles_dev, width),
+        preferred_element_type=jnp.float32,
+    )
     summed = jnp.sum(beam_here[None, :, None, :] * harmonic, axis=1)
 
     image = prior_inverse[None, None, :] * direction + summed

time: 94.8 us -> 106 us (1.12)
  blocking collectives: 36.4 us -> 18.2 us
  waiting for transfers between devices: 11.9 us -> 24.2 us
  starting transfers between devices: 19.2 us -> 26.2 us
  local copies, waits for them, and re-layouts: 10.3 us -> 14.1 us
  matrix products: 10.5 us -> 14.1 us
  other arithmetic: 4.91 us -> 7.72 us
    all_to_all x1 -> x0, blocking collectives: 18.2 us -> none  [per_device(): lax.all_to_all(returning, EVERY, split_axis=0, concat_axis=0, tiled=True)]
    all_to_all x0 -> x1, waiting for transfers between devices: none -> 12.3 us  [per_device(): lax.all_to_all(returning, EVERY, split_axis=0, concat_axis=0, tiled=True)]
    all_to_all x0 -> x1, starting transfers between devices: none -> 5.56 us  [per_device(): lax.all_to_all(returning, EVERY, split_axis=0, concat_axis=0, tiled=True)]
    dynamic_slice x0 -> x2, local copies, waits for them, and re-layouts: none -> 1.94 us  [per_device(): legendre_here = lax.dynamic_slice_in_dim(legendre, band * width, width, 2)]
    dot_general x1, matrix products: 1.3 us -> 2.87 us  [per_device(): jnp.einsum('mra,mb->rab', lower_part, inner_sin, precision=precise)]
    all_to_all x1, waiting for transfers between devices: 1.38 us -> 0.01 us  [per_device(): lax.all_to_all(beam_window.reshape(nband, width), 'band', split_axis=0, c...]
    all_to_all x1, starting transfers between devices: 12.7 us -> 14 us  [per_device(): lax.all_to_all(outgoing, EVERY, split_axis=0, concat_axis=0, tiled=True)]
    all_to_all x1, waiting for transfers between devices: 10.6 us -> 11.8 us  [per_device(): lax.all_to_all(outgoing, EVERY, split_axis=0, concat_axis=0, tiled=True)]
  transfers between devices with their start and end apart: 2 -> 3, of which waited for: 2 -> 2; matrix products, arithmetic and copies ran while one was open for 6% -> 7% of each run, Pallas kernels for 0% -> 0%
where the time goes in v12:
time: 106 us; the launch traced here: 105 us
  starting transfers between devices  26.2 us (25%)
  waiting for transfers between devices  24.2 us (23%)
  blocking collectives  18.2 us (17%)
  local copies, waits for them, and re-layouts  14.1 us (13%)
  matrix products  14.1 us (13%)
  other arithmetic  7.72 us (7%)
    all_to_all x1, blocking collectives, per_device(): lax.all_to_all(shared, EVERY, split_axis=0, concat_axis=0, tiled=True)  18.2 us
    all_to_all x1, starting transfers between devices, per_device(): lax.all_to_all(outgoing, EVERY, split_axis=0, concat_axis=0, tiled=True)  14 us
    all_to_all x1, waiting for transfers between devices, per_device(): lax.all_to_all(returning, EVERY, split_axis=0, concat_axis=0, tiled=True)  12.3 us
    all_to_all x1, waiting for transfers between devices, per_device(): lax.all_to_all(outgoing, EVERY, split_axis=0, concat_axis=0, tiled=True)  11.8 us
    all_to_all x1, starting transfers between devices, per_device(): lax.all_to_all(beam_window.reshape(nband, width), 'band', split_axis=0, c...  6.58 us
    all_to_all x1, starting transfers between devices, per_device(): lax.all_to_all(returning, EVERY, split_axis=0, concat_axis=0, tiled=True)  5.56 us
    dot_general x1, matrix products, per_device(): jnp.einsum('mra,mb->rab', lower_part, inner_sin, precision=precise)  2.87 us
    dot_general x1, matrix products, per_device(): jnp.einsum('rab,mb->mra', noisy_grid, inner_cos, precision=precise)  2.37 us
  transfers between devices with their start and end apart: 3, of which 2 were waited for; matrix products, arithmetic and copies ran while one was open for 7% of the time, Pallas kernels for 0%

profile of v12, /device:TPU:1, one launch (start us, length us, event | category | flops | bytes accessed | tf_op | source)
XLA Modules:
  0.0 105.4 jit_solution(14046951918238599026)
XLA Ops:
  0.7 6.6 %all-to-all-start = ((f32[8,1,512]{2,1,0:T(1,128)}), f32[8,1,512]{2,1,0:T(1,128)S(1)}, u32[]{:S(2)}, u32[]{:S(2)}) async-start(f32[8,1,512]{2,1,0:T(1,128)} %bitcast.90), calls=%async_computation | async-start | bytes 32768 | tf_op jit(solution)/shard_map/all_to_all | solution.py:65
  7.2 1.3 %iota_compare_fusion.2 = pred[128,32]{0,1:T(8,128)(4,1)} fusion(s32[128]{0:T(128)} %param.23), kind=kLoop, calls=%fused_computation.75 | loop fusion | flops 4096 | bytes 4608 | tf_op jit(solution)/shard_map/eq | solution.py:25
  8.5 1.9 %fusion.46 = (f32[512,64]{0,1:T(8,128)S(1)}, f32[512,64]{0,1:T(8,128)}) fusion(s32[64]{0:T(128)S(1)} %iota_multiply_fusion, s32[512]{0:T(512)} %param.19), kind=kLoop, calls=%fused_computation.71 | loop fusion | flops 458752 | bytes 264448 | tf_op jit(solution)/shard_map/cos | solution.py:20
  10.4 1.4 %constant_dynamic-slice_fusion = bf16[16,64,512]{2,1,0:T(8,128)(2,1)S(1)} fusion(bf16[16,64,4096]{2,1,0:T(8,128)(2,1)} %param.18, s32[]{:T(128)S(6)} %select_n.34), kind=kLoop, calls=%fused_computation.91 | loop fusion | bytes 2097156 | tf_op jit(solution)/shard_map/dynamic_slice | solution.py:68
  11.8 1.0 mul.277
  13.6 1.0 copy.61
  14.6 1.9 %copy.62 = f32[32,8,16,2,2]{1,0,4,3,2:T(8,128)S(1)} copy(f32[32,8,16,2,2]{2,4,0,3,1:T(2,128)} %bitcast.87) | data formatting | bytes 131072 | tf_op jit(solution)/shard_map/transpose | solution.py:77
  17.8 14.0 %all-to-all-start.1 = ((f32[256,1,64]{2,1,0:T(1,128)}), f32[256,1,64]{2,1,0:T(1,128)S(1)}, u32[]{:S(2)}, u32[]{:S(2)}) async-start(f32[256,1,64]{2,1,0:T(1,128)} %copy.63), calls=%async_computation.1 | async-start | bytes 262144 | tf_op jit(solution)/shard_map/all_to_all | solution.py:78
  32.8 11.8 %all-to-all-done.1 = f32[256,1,64]{2,1,0:T(1,128)S(1)} async-done(((f32[256,1,64]{2,1,0:T(1,128)}), f32[256,1,64]{2,1,0:T(1,128)S(1)}, u32[]{:S(2)}, u32[]{:S(2)}) %all-to-all-start.1) | async-done | bytes 65568 | tf_op jit(solution)/shard_map/all_to_all | solution.py:78
  44.7 1.6 %reshape.221 = f32[32,8,16,2,2]{1,0,4,3,2:T(8,128)} reshape(f32[256,1,64]{0,2,1:T(8,128)S(1)} %copy.64) | data formatting | bytes 131072 | tf_op jit(solution)/shard_map/reshape | solution.py:80
  46.3 1.6 %reduce_sum.54 = f32[32,16,2,2]{0,3,2,1:T(2,128)S(1)} reduce(f32[32,8,16,2,2]{1,0,4,3,2:T(8,128)} %reshape.221, f32[]{:T(128)} %constant.45.clone.1), dimensions={1}, to_apply=%region_0.0 | reduce | flops 14336 | bytes 73732 | tf_op jit(solution)/shard_map/reduce_sum | solution.py:79
  48.1 2.2 %fusion.12 = f32[2,64,128]{2,1,0:T(8,128)S(1)} fusion(f32[512,64]{0,1:T(8,128)} %get-tuple-element.26, f32[512,2]{0,1:T(2,128)S(1)} %get-tuple-element.24, f32[512,64]{0,1:T(8,128)S(1)} %get-tuple-element.25, f32[512,2]{0,1:T(2,128)S(1)} %get-tuple-element.23, s32[512]{0:T(512)S(1)} %copy-done.6), kind=kOutput, calls=%fused_computation.24 | convolution fusion | flops 51445760 | bytes 337920 | tf_op jit(solution)/shard_map/mra,mb->rab/dot_general | solution.py:90
  50.4 2.9 %fusion.3 = f32[2,64,128]{2,1,0:T(8,128)} fusion(f32[2,64,128]{2,1,0:T(8,128)S(1)} %fusion.12, f32[512,64]{0,1:T(8,128)} %get-tuple-element.26, f32[512,2]{0,1:T(2,128)S(1)} %get-tuple-element.24, f32[512,64]{0,1:T(8,128)S(1)} %get-tuple-element.25, f32[512,2]{0,1:T(2,128)S(1)} %get-tuple-element.23, s32[512]{0:T(512)} %param.19), kind=kOutput, calls=%fused_computation.9 | convolution fusion | flops 51478528 | bytes 403456 | tf_op jit(solution)/shard_map/mra,mb->rab/dot_general | solution.py:90
  53.3 0.9 mul.301
  54.2 0.8 gather_fusion
  55.0 1.3 %fusion = f32[128,64]{0,1:T(8,128)S(1)} fusion(f32[32,64,64]{2,1,0:T(8,128)S(1)} %copy-done, pred[128,32]{0,1:T(8,128)(4,1)} %iota_compare_fusion.2, f32[128,64]{1,0:T(8,128)S(1)} %gather_fusion), kind=kOutput, calls=%fused_computation.2 | convolution fusion | flops 101179392 | bytes 593920 | tf_op jit(solution)/shard_map/kij,tj->tki/dot_general | solution.py:32
  56.9 0.8 select_reduce_fusion
  57.7 0.9 fusion.41
  58.6 2.2 %convolution_bitcast_fusion.1 = f32[512,64,2]{0,1,2:T(8,128)S(1)} fusion(s32[512]{0:T(512)} %param.19, f32[2,64,128]{2,1,0:T(8,128)S(1)} %reshape.223, f32[2,64,128]{2,1,0:T(8,128)} %fusion.3, f32[1,2,64,128]{3,1,2,0:T(2,128)} %bitcast.95), kind=kOutput, calls=%fused_computation.6 | convolution fusion | flops 51281920 | bytes 460800 | tf_op jit(solution)/shard_map/rab,mb->mra/dot_general | solution.py:97
  60.8 2.4 %multiply_reduce_fusion.3 = (f32[512,2]{0,1:T(2,128)S(1)}, f32[512,2]{0,1:T(2,128)S(1)}, f32[512,2]{0,1:T(2,128)S(1)}, f32[512,2]{0,1:T(2,128)S(1)}) fusion(f32[512,64]{0,1:T(8,128)} %copy-done.3, f32[512,64]{0,1:T(8,128)} %get-tuple-element.26, f32[512,64,2]{0,1,2:T(8,128)S(1)} %convolution_bitcast_fusion.1, f32[2,64,128]{2,1,0:T(8,128)S(1)} %reshape.223, ...), kind=kOutput, calls=%fused_computation.29 | convolution fusion | flops 51802112 | bytes 739328 | tf_op jit(solution)/shard_map/rab,mb->mra/dot_general | solution.py:96
  64.5 5.6 %all-to-all-start.2 = ((bf16[256,1,64]{2,1,0:T(2,128)(2,1)}), bf16[256,1,64]{2,1,0:T(2,128)(2,1)S(1)}, u32[]{:S(2)}, u32[]{:S(2)}) async-start(bf16[256,1,64]{2,1,0:T(2,128)(2,1)} %copy.70), calls=%async_computation.2 | async-start | bytes 262144 | tf_op jit(solution)/shard_map/all_to_all | solution.py:110
  70.7 12.3 %all-to-all-done.2 = bf16[256,1,64]{2,1,0:T(2,128)(2,1)S(1)} async-done(((bf16[256,1,64]{2,1,0:T(2,128)(2,1)}), bf16[256,1,64]{2,1,0:T(2,128)(2,1)S(1)}, u32[]{:S(2)}, u32[]{:S(2)}) %all-to-all-start.2) | async-done | bytes 32800 | tf_op jit(solution)/shard_map/all_to_all | solution.py:110
  83.7 1.3 %fusion.2 = f32[16,2,512]{2,1,0:T(2,128)S(1)} fusion(bf16[32,8,16,2,2]{1,0,4,3,2:T(8,128)(2,1)S(1)} %reshape.224, bf16[16,32,2,512,1]{3,0,2,1,4:T(8,128)(2,1)S(1)} %bitcast.85, f32[8,512]{1,0:T(8,128)S(1)} %bitcast.89), kind=kOutput, calls=%fused_computation.5 | convolution fusion | flops 17022976 | bytes 1163264 | tf_op jit(solution)/shard_map/kbscj,skjl->sbcl/dot_general | solution.py:112
  86.1 18.2 %all_to_all.33 = f32[256,1,4]{2,1,0:T(1,128)S(1)} all-to-all(f32[256,1,4]{2,1,0:T(1,128)S(1)} %broadcast_in_dim.28), channel_id=1, replica_groups=mesh['blk'=32,'band'=8] {'blk','band'}, dimensions={0} | all-to-all | bytes 8192 | tf_op jit(solution)/shard_map/all_to_all | solution.py:128
  (58 shorter events, 8.6 us)
Async XLA Ops:
  0.6 47.5 %copy-start.6 = (s32[512]{0:T(512)S(1)}, s32[512]{0:T(512)}, u32[]{:S(2)}) copy-start(s32[512]{0:T(512)} %param.19) | copy-start | bytes 6148
  0.6 31.2 %copy-start.8 = (s32[128]{0:T(128)S(1)}, s32[128]{0:T(128)}, u32[]{:S(2)}) copy-start(s32[128]{0:T(128)} %param.22) | copy-start | bytes 1540
  0.7 31.2 %copy-start = (f32[32,64,64]{2,1,0:T(8,128)S(1)}, f32[32,64,64]{2,1,0:T(8,128)}, u32[]{:S(2)}) copy-start(f32[32,64,64]{2,1,0:T(8,128)} %param.21) | copy-start | bytes 1572868
  0.7 12.5 %all-to-all-start = ((f32[8,1,512]{2,1,0:T(1,128)}), f32[8,1,512]{2,1,0:T(1,128)S(1)}, u32[]{:S(2)}, u32[]{:S(2)}) async-start(f32[8,1,512]{2,1,0:T(1,128)} %bitcast.90), calls=%async_computation | async-start | bytes 32768 | tf_op jit(solution)/shard_map/all_to_all | solution.py:65
  10.4 40.0 %copy-start.3 = (f32[512,64]{0,1:T(8,128)}, f32[512,64]{0,1:T(8,128)S(1)}, u32[]{:S(2)}) copy-start(f32[512,64]{0,1:T(8,128)S(1)} %get-tuple-element.25) | copy-start | bytes 393220
  17.8 26.8 %all-to-all-start.1 = ((f32[256,1,64]{2,1,0:T(1,128)}), f32[256,1,64]{2,1,0:T(1,128)S(1)}, u32[]{:S(2)}, u32[]{:S(2)}) async-start(f32[256,1,64]{2,1,0:T(1,128)} %copy.63), calls=%async_computation.1 | async-start | bytes 262144 | tf_op jit(solution)/shard_map/all_to_all | solution.py:78
  47.9 37.2 %copy-start.1 = (f32[16,2,512]{2,1,0:T(2,128)S(1)}, f32[16,2,512]{2,1,0:T(2,128)}, u32[]{:S(2)}) copy-start(f32[16,2,512]{2,1,0:T(2,128)} %param.14) | copy-start | bytes 196612
  48.1 37.1 %copy-start.2 = (f32[16,2,512]{2,1,0:T(2,128)S(1)}, f32[16,2,512]{2,1,0:T(2,128)}, u32[]{:S(2)}) copy-start(f32[16,2,512]{2,1,0:T(2,128)} %param.13) | copy-start | bytes 196612
  50.4 54.3 %copy-start.4 = (f32[16,2,512]{2,1,0:T(2,128)S(1)}, f32[16,2,512]{2,1,0:T(2,128)}, u32[]{:S(2)}) copy-start(f32[16,2,512]{2,1,0:T(2,128)} %param.12) | copy-start | bytes 196612
  55.0 30.1 %copy-start.7 = (f32[512]{0:T(512)S(1)}, f32[512]{0:T(512)}, u32[]{:S(2)}) copy-start(f32[512]{0:T(512)} %param.15) | copy-start | bytes 6148
  55.0 30.3 %copy-start.5 = (f32[512]{0:T(512)S(1)}, f32[512]{0:T(512)}, u32[]{:S(2)}) copy-start(f32[512]{0:T(512)} %param.16) | copy-start | bytes 6148
  64.5 18.5 %all-to-all-start.2 = ((bf16[256,1,64]{2,1,0:T(2,128)(2,1)}), bf16[256,1,64]{2,1,0:T(2,128)(2,1)S(1)}, u32[]{:S(2)}, u32[]{:S(2)}) async-start(bf16[256,1,64]{2,1,0:T(2,128)(2,1)} %copy.70), calls=%async_computation.2 | async-start | bytes 262144 | tf_op jit(solution)/shard_map/all_to_all | solution.py:110

commit v13 on v10

--- a/solution.py
+++ b/solution.py
@@ -76,9 +76,9 @@
     chunk = orders_dev * parts * cycles_dev
     outgoing = partial.transpose(3, 1, 0, 2, 4).reshape(nblk * nband, chunk)
     incoming = lax.all_to_all(outgoing, EVERY, split_axis=0, concat_axis=0, tiled=True)
-    cycle_coefficients = jnp.sum(
-        incoming.reshape(nblk, nband, orders_dev, parts, cycles_dev), axis=1
-    ).reshape(order_count, parts, cycles_dev)
+    cycle_coefficients = jnp.sum(incoming.reshape(nblk, nband, chunk), axis=1).reshape(
+        order_count, parts, cycles_dev
+    )
 
     cycle_count = cycles_dev
     outer_cos, outer_sin = phases(mode_orders, NPHI // 128, 128)

time: 94.8 us -> 95.9 us (1.012)
  no operation moved by 1% of the time
where the time goes in v13:
time: 95.9 us; the launch traced here: 95.4 us
  blocking collectives  36.4 us (38%)
  starting transfers between devices  19.2 us (20%)
  waiting for transfers between devices  11.9 us (12%)
  matrix products  11.3 us (12%)
  local copies, waits for them, and re-layouts  10.9 us (11%)
  other arithmetic  4.55 us (5%)
  between operations  1.02 us (1%)
    all_to_all x1, blocking collectives, per_device(): lax.all_to_all(shared, EVERY, split_axis=0, concat_axis=0, tiled=True)  18.2 us
    all_to_all x1, blocking collectives, per_device(): lax.all_to_all(returning, EVERY, split_axis=0, concat_axis=0, tiled=True)  18.2 us
    all_to_all x1, starting transfers between devices, per_device(): lax.all_to_all(outgoing, EVERY, split_axis=0, concat_axis=0, tiled=True)  12.7 us
    all_to_all x1, waiting for transfers between devices, per_device(): lax.all_to_all(outgoing, EVERY, split_axis=0, concat_axis=0, tiled=True)  10.6 us
    all_to_all x1, starting transfers between devices, per_device(): lax.all_to_all(beam_window.reshape(nband, width), 'band', split_axis=0, c...  6.58 us
    dot_general x1, matrix products, per_device(): jnp.einsum('rab,mb->mra', noisy_grid, inner_cos, precision=precise)  2.16 us
    dot_general x1, matrix products, per_device(): jnp.einsum('rab,mb->mra', noisy_grid, inner_sin, precision=precise)  2.12 us
  transfers between devices with their start and end apart: 2, of which 2 were waited for; matrix products, arithmetic and copies ran while one was open for 6% of the time, Pallas kernels for 0%

profile of v13, /device:TPU:1, one launch (start us, length us, event | category | flops | bytes accessed | tf_op | source)
XLA Modules:
  0.0 95.4 jit_solution(14650564020677539908)
XLA Ops:
  0.7 6.6 %all-to-all-start = ((f32[8,1,512]{2,1,0:T(1,128)}), f32[8,1,512]{2,1,0:T(1,128)S(1)}, u32[]{:S(2)}, u32[]{:S(2)}) async-start(f32[8,1,512]{2,1,0:T(1,128)} %bitcast.80), calls=%async_computation | async-start | bytes 32768 | tf_op jit(solution)/shard_map/all_to_all | solution.py:65
  7.2 1.3 %fusion.46 = (f32[512,64]{0,1:T(8,128)S(1)}, f32[512,64]{0,1:T(8,128)S(1)}) fusion(s32[64]{0:T(128)S(1)} %iota_multiply_fusion, s32[512]{0:T(512)} %param.19), kind=kLoop, calls=%fused_computation.72 | loop fusion | flops 458752 | bytes 264448 | tf_op jit(solution)/shard_map/cos | solution.py:20
  8.5 0.7 iota_compare_fusion.2
  9.2 1.0 %mul.277 = f32[16,8,2,512]{3,2,1,0:T(2,128)S(1)} broadcast(f32[16,2,512]{2,1,0:T(2,128)} %param.14), dimensions={0,2,3} | broadcast | bytes 589824 | tf_op jit(solution)/shard_map/mul | solution.py:70
  10.5 1.4 %all-to-all-done = f32[8,1,512]{2,1,0:T(1,128)S(1)} async-done(((f32[8,1,512]{2,1,0:T(1,128)}), f32[8,1,512]{2,1,0:T(1,128)S(1)}, u32[]{:S(2)}, u32[]{:S(2)}) %all-to-all-start) | async-done | bytes 16416 | tf_op jit(solution)/shard_map/all_to_all | solution.py:65
  12.0 1.6 %fusion.4 = f32[16,16,64]{2,1,0:T(8,128)S(1)} fusion(bf16[16,64,4096]{2,1,0:T(8,128)(2,1)} %param.18, s32[]{:T(128)S(6)} %select_n.34, f32[16,16,512]{2,1,0:T(8,128)S(1)} %mul.278, f32[16,512]{1,0:T(8,128)S(1)} %mul.275), kind=kOutput, calls=%fused_computation.10 | convolution fusion | flops 17039360 | bytes 1671172 | tf_op jit(solution)/shard_map/sql,srl->sqr/dot_general | solution.py:72
  13.8 0.9 copy.63
  15.3 0.7 copy.64
  16.0 12.7 %all-to-all-start.1 = ((f32[256,1,64]{2,1,0:T(1,128)}), f32[256,1,64]{2,1,0:T(1,128)S(1)}, u32[]{:S(2)}, u32[]{:S(2)}) async-start(f32[256,1,64]{2,1,0:T(1,128)} %copy.64), calls=%async_computation.1 | async-start | bytes 262144 | tf_op jit(solution)/shard_map/all_to_all | solution.py:78
  28.7 0.7 compare_select_fusion
  29.4 1.6 %copy.68 = f32[32,64,64]{1,2,0:T(8,128)S(1)} copy(f32[32,64,64]{2,1,0:T(8,128)} %param.21) | data formatting | bytes 1048576 | tf_op args[9]
  30.9 10.6 %all-to-all-done.1 = f32[256,1,64]{2,1,0:T(1,128)S(1)} async-done(((f32[256,1,64]{2,1,0:T(1,128)}), f32[256,1,64]{2,1,0:T(1,128)S(1)}, u32[]{:S(2)}, u32[]{:S(2)}) %all-to-all-start.1) | async-done | bytes 65568 | tf_op jit(solution)/shard_map/all_to_all | solution.py:78
  41.5 0.8 reshape.225
  43.0 1.3 %fusion.12 = f32[2,64,128]{2,1,0:T(8,128)S(1)} fusion(f32[512,64]{0,1:T(8,128)S(1)} %get-tuple-element.26, f32[512,2]{0,1:T(2,128)S(1)} %copy.66, f32[512,64]{0,1:T(8,128)S(1)} %get-tuple-element.25, f32[512,2]{0,1:T(2,128)S(1)} %copy.65, s32[512]{0:T(512)S(1)} %copy-done.5), kind=kOutput, calls=%fused_computation.24 | convolution fusion | flops 51445760 | bytes 337920 | tf_op jit(solution)/shard_map/mra,mb->rab/dot_general | solution.py:90
  44.3 1.3 %fusion.1 = f32[2,64,128]{2,1,0:T(8,128)S(1)} fusion(f32[2,64,128]{2,1,0:T(8,128)S(1)} %fusion.12, f32[512,64]{0,1:T(8,128)S(1)} %get-tuple-element.26, f32[512,2]{0,1:T(2,128)S(1)} %copy.66, f32[512,64]{0,1:T(8,128)S(1)} %get-tuple-element.25, f32[512,2]{0,1:T(2,128)S(1)} %copy.65, s32[512]{0:T(512)S(1)} %copy-done.5), kind=kOutput, calls=%fused_computation.6 | convolution fusion | flops 51478528 | bytes 403456 | tf_op jit(solution)/shard_map/mra,mb->rab/dot_general | solution.py:90
  45.7 0.6 gather_fusion
  48.0 2.1 %convolution_bitcast_fusion = f32[512,64,2]{0,1,2:T(8,128)S(1)} fusion(s32[512]{0:T(512)S(1)} %copy-done.5, f32[2,64,128]{2,1,0:T(8,128)S(1)} %reshape.226, f32[2,64,128]{2,1,0:T(8,128)S(1)} %fusion.1, f32[1,2,64,128]{3,1,2,0:T(2,128)} %bitcast.85), kind=kOutput, calls=%fused_computation.3 | convolution fusion | flops 51281920 | bytes 460800 | tf_op jit(solution)/shard_map/rab,mb->mra/dot_general | solution.py:97
  50.1 2.2 %multiply_reduce_fusion.4 = (f32[512,2]{0,1:T(2,128)S(1)}, f32[512,2]{0,1:T(2,128)S(1)}, f32[512,2]{0,1:T(2,128)S(1)}, f32[512,2]{0,1:T(2,128)S(1)}) fusion(f32[512,64]{0,1:T(8,128)S(1)} %get-tuple-element.25, f32[512,64]{0,1:T(8,128)S(1)} %get-tuple-element.26, f32[512,64,2]{0,1,2:T(8,128)S(1)} %convolution_bitcast_fusion, ...), kind=kOutput, calls=%fused_computation.29 | convolution fusion | flops 51802112 | bytes 739328 | tf_op jit(solution)/shard_map/rab,mb->mra/dot_general | solution.py:96
  53.0 18.2 %all_to_all.33 = bf16[256,1,64]{2,1,0:T(2,128)(2,1)S(1)} all-to-all(bf16[256,1,64]{2,1,0:T(2,128)(2,1)S(1)} %copy.71), channel_id=1, replica_groups=mesh['blk'=32,'band'=8] {'blk','band'}, dimensions={0} | all-to-all | bytes 65536 | tf_op jit(solution)/shard_map/all_to_all | solution.py:110
  71.3 0.6 reshape.227
  71.9 0.8 copy.73
  72.9 1.5 %fusion.2 = f32[16,16,512]{2,1,0:T(8,128)S(1)} fusion(bf16[16,16,64]{2,1,0:T(8,128)(2,1)S(1)} %copy.74, bf16[16,64,4096]{2,1,0:T(8,128)(2,1)} %param.18, s32[]{:T(128)S(6)} %select_n.34), kind=kOutput, calls=%fused_computation.8 | convolution fusion | flops 16777216 | bytes 1605636 | tf_op jit(solution)/shard_map/sqr,srl->sql/dot_general | solution.py:113
  76.0 18.2 %all_to_all.34 = f32[256,1,4]{2,1,0:T(1,128)S(1)} all-to-all(f32[256,1,4]{2,1,0:T(1,128)S(1)} %broadcast_in_dim.28), channel_id=1, replica_groups=mesh['blk'=32,'band'=8] {'blk','band'}, dimensions={0} | all-to-all | bytes 8192 | tf_op jit(solution)/shard_map/all_to_all | solution.py:126
  94.6 0.7 multiply_add_fusion
  (56 shorter events, 6.3 us)
Async XLA Ops:
  0.6 42.4 %copy-start.5 = (s32[512]{0:T(512)S(1)}, s32[512]{0:T(512)}, u32[]{:S(2)}) copy-start(s32[512]{0:T(512)} %param.19) | copy-start | bytes 6148
  0.6 45.8 %copy-start = (f32[32,64,64]{2,1,0:T(8,128)S(1)}, f32[32,64,64]{2,1,0:T(8,128)}, u32[]{:S(2)}) copy-start(f32[32,64,64]{2,1,0:T(8,128)} %param.21) | copy-start | bytes 1572868
  0.7 11.3 %all-to-all-start = ((f32[8,1,512]{2,1,0:T(1,128)}), f32[8,1,512]{2,1,0:T(1,128)S(1)}, u32[]{:S(2)}, u32[]{:S(2)}) async-start(f32[8,1,512]{2,1,0:T(1,128)} %bitcast.80), calls=%async_computation | async-start | bytes 32768 | tf_op jit(solution)/shard_map/all_to_all | solution.py:65
  13.6 34.1 %copy-start.7 = (s32[128]{0:T(128)S(1)}, s32[128]{0:T(128)}, u32[]{:S(2)}) copy-start(s32[128]{0:T(128)} %param.22) | copy-start | bytes 1540
  16.0 25.5 %all-to-all-start.1 = ((f32[256,1,64]{2,1,0:T(1,128)}), f32[256,1,64]{2,1,0:T(1,128)S(1)}, u32[]{:S(2)}, u32[]{:S(2)}) async-start(f32[256,1,64]{2,1,0:T(1,128)} %copy.64), calls=%async_computation.1 | async-start | bytes 262144 | tf_op jit(solution)/shard_map/all_to_all | solution.py:78
  43.0 31.9 %copy-start.1 = (f32[16,2,512]{2,1,0:T(2,128)S(1)}, f32[16,2,512]{2,1,0:T(2,128)}, u32[]{:S(2)}) copy-start(f32[16,2,512]{2,1,0:T(2,128)} %param.14) | copy-start | bytes 196612
  43.0 31.9 %copy-start.6 = (f32[512]{0:T(512)S(1)}, f32[512]{0:T(512)}, u32[]{:S(2)}) copy-start(f32[512]{0:T(512)} %param.15) | copy-start | bytes 6148
  44.3 30.8 %copy-start.2 = (f32[16,2,512]{2,1,0:T(2,128)S(1)}, f32[16,2,512]{2,1,0:T(2,128)}, u32[]{:S(2)}) copy-start(f32[16,2,512]{2,1,0:T(2,128)} %param.13) | copy-start | bytes 196612
  44.3 30.8 %copy-start.4 = (f32[512]{0:T(512)S(1)}, f32[512]{0:T(512)}, u32[]{:S(2)}) copy-start(f32[512]{0:T(512)} %param.16) | copy-start | bytes 6148
  45.6 49.0 %copy-start.3 = (f32[16,2,512]{2,1,0:T(2,128)S(1)}, f32[16,2,512]{2,1,0:T(2,128)}, u32[]{:S(2)}) copy-start(f32[16,2,512]{2,1,0:T(2,128)} %param.12) | copy-start | bytes 196612

commit v14 on v10

--- a/solution.py
+++ b/solution.py
@@ -95,15 +95,11 @@
     noisy_grid = noisy.reshape(cycle_count, NPHI // 128, 128)
     cos_sums = jnp.einsum("rab,mb->mra", noisy_grid, inner_cos, precision=precise)
     sin_sums = jnp.einsum("rab,mb->mra", noisy_grid, inner_sin, precision=precise)
-    real_terms = norm_scale * (
-        jnp.einsum("mra,ma->mr", cos_sums, outer_cos, precision=precise)
-        - jnp.einsum("mra,ma->mr", sin_sums, outer_sin, precision=precise)
+    oc, os_ = outer_cos[:, None, :], outer_sin[:, None, :]
+    both_terms = jnp.stack(
+        [cos_sums * oc - sin_sums * os_, -(cos_sums * os_ + sin_sums * oc)], axis=1
     )
-    imag_terms = -norm_scale * (
-        jnp.einsum("mra,ma->mr", cos_sums, outer_sin, precision=precise)
-        + jnp.einsum("mra,ma->mr", sin_sums, outer_cos, precision=precise)
-    )
-    cycle_terms = jnp.stack([real_terms, imag_terms], axis=1).astype(jnp.bfloat16)
+    cycle_terms = (norm_scale * jnp.sum(both_terms, axis=3)).astype(jnp.bfloat16)
 
     per_owner = cycle_terms.reshape(nblk, 1, chunk)
     returning = jnp.broadcast_to(per_owner, (nblk, nband, chunk)).reshape(nblk * nband, chunk)

time: 94.8 us -> 94.9 us (level)
  no operation moved by 1% of the time
where the time goes in v14:
time: 94.9 us; the launch traced here: 94.4 us
  blocking collectives  36.5 us (38%)
  starting transfers between devices  19.2 us (20%)
  waiting for transfers between devices  11.9 us (13%)
  matrix products  10.5 us (11%)
  local copies, waits for them, and re-layouts  10.3 us (11%)
  other arithmetic  4.95 us (5%)
  between operations  1.05 us (1%)
    all_to_all x1, blocking collectives, per_device(): lax.all_to_all(returning, EVERY, split_axis=0, concat_axis=0, tiled=True)  18.2 us
    all_to_all x1, blocking collectives, per_device(): lax.all_to_all(shared, EVERY, split_axis=0, concat_axis=0, tiled=True)  18.2 us
    all_to_all x1, starting transfers between devices, per_device(): lax.all_to_all(outgoing, EVERY, split_axis=0, concat_axis=0, tiled=True)  12.7 us
    all_to_all x1, waiting for transfers between devices, per_device(): lax.all_to_all(outgoing, EVERY, split_axis=0, concat_axis=0, tiled=True)  10.5 us
    all_to_all x1, starting transfers between devices, per_device(): lax.all_to_all(beam_window.reshape(nband, width), 'band', split_axis=0, c...  6.58 us
    dot_general x1, matrix products, per_device(): jnp.einsum('rab,mb->mra', noisy_grid, inner_sin, precision=precise)  2.12 us
  transfers between devices with their start and end apart: 2, of which 2 were waited for; matrix products, arithmetic and copies ran while one was open for 6% of the time, Pallas kernels for 0%

profile of v14, /device:TPU:1, one launch (start us, length us, event | category | flops | bytes accessed | tf_op | source)
XLA Modules:
  0.0 94.4 jit_solution(16240394224682269804)
XLA Ops:
  0.7 6.6 %all-to-all-start = ((f32[8,1,512]{2,1,0:T(1,128)}), f32[8,1,512]{2,1,0:T(1,128)S(1)}, u32[]{:S(2)}, u32[]{:S(2)}) async-start(f32[8,1,512]{2,1,0:T(1,128)} %bitcast.76), calls=%async_computation | async-start | bytes 32768 | tf_op jit(solution)/shard_map/all_to_all | solution.py:65
  7.2 1.3 %fusion.48 = (f32[512,64]{0,1:T(8,128)S(1)}, f32[512,64]{0,1:T(8,128)S(1)}) fusion(s32[64]{0:T(128)S(1)} %iota_multiply_fusion, s32[512]{0:T(512)} %param.19), kind=kLoop, calls=%fused_computation.70 | loop fusion | flops 458752 | bytes 264448 | tf_op jit(solution)/shard_map/cos | solution.py:20
  8.5 0.7 iota_compare_fusion.2
  9.2 1.0 %mul.300 = f32[16,8,2,512]{3,2,1,0:T(2,128)S(1)} broadcast(f32[16,2,512]{2,1,0:T(2,128)} %param.14), dimensions={0,2,3} | broadcast | bytes 589824 | tf_op jit(solution)/shard_map/mul | solution.py:70
  10.5 1.4 %all-to-all-done = f32[8,1,512]{2,1,0:T(1,128)S(1)} async-done(((f32[8,1,512]{2,1,0:T(1,128)}), f32[8,1,512]{2,1,0:T(1,128)S(1)}, u32[]{:S(2)}, u32[]{:S(2)}) %all-to-all-start) | async-done | bytes 16416 | tf_op jit(solution)/shard_map/all_to_all | solution.py:65
  12.0 1.6 %fusion.4 = f32[16,16,64]{2,1,0:T(8,128)S(1)} fusion(bf16[16,64,4096]{2,1,0:T(8,128)(2,1)} %param.18, s32[]{:T(128)S(6)} %select_n.34, f32[16,16,512]{2,1,0:T(8,128)S(1)} %mul.301, f32[16,512]{1,0:T(8,128)S(1)} %mul.298), kind=kOutput, calls=%fused_computation.8 | convolution fusion | flops 17039360 | bytes 1671172 | tf_op jit(solution)/shard_map/sql,srl->sqr/dot_general | solution.py:72
  13.8 0.9 copy.57
  15.3 0.8 copy.58
  16.0 12.7 %all-to-all-start.1 = ((f32[256,1,64]{2,1,0:T(1,128)}), f32[256,1,64]{2,1,0:T(1,128)S(1)}, u32[]{:S(2)}, u32[]{:S(2)}) async-start(f32[256,1,64]{2,1,0:T(1,128)} %copy.58), calls=%async_computation.1 | async-start | bytes 262144 | tf_op jit(solution)/shard_map/all_to_all | solution.py:78
  28.7 0.7 compare_select_fusion
  29.4 1.6 %copy.62 = f32[32,64,64]{1,2,0:T(8,128)S(1)} copy(f32[32,64,64]{2,1,0:T(8,128)} %param.21) | data formatting | bytes 1048576 | tf_op args[9]
  30.9 10.5 %all-to-all-done.1 = f32[256,1,64]{2,1,0:T(1,128)S(1)} async-done(((f32[256,1,64]{2,1,0:T(1,128)}), f32[256,1,64]{2,1,0:T(1,128)S(1)}, u32[]{:S(2)}, u32[]{:S(2)}) %all-to-all-start.1) | async-done | bytes 65568 | tf_op jit(solution)/shard_map/all_to_all | solution.py:78
  42.8 1.3 %fusion.14 = f32[2,64,128]{2,1,0:T(8,128)S(1)} fusion(f32[512,64]{0,1:T(8,128)S(1)} %get-tuple-element.22, f32[512,2]{0,1:T(2,128)S(1)} %get-tuple-element.20, f32[512,64]{0,1:T(8,128)S(1)} %get-tuple-element.21, f32[512,2]{0,1:T(2,128)S(1)} %get-tuple-element.19, s32[512]{0:T(512)S(1)} %copy-done.5), kind=kOutput, calls=%fused_computation.25 | convolution fusion | flops 51445760 | bytes 337920 | tf_op jit(solution)/shard_map/mra,mb->rab/dot_general | solution.py:90
  44.1 1.3 %fusion.1 = f32[2,64,128]{2,1,0:T(8,128)S(1)} fusion(f32[2,64,128]{2,1,0:T(8,128)S(1)} %fusion.14, f32[512,64]{0,1:T(8,128)S(1)} %get-tuple-element.22, f32[512,2]{0,1:T(2,128)S(1)} %get-tuple-element.20, f32[512,64]{0,1:T(8,128)S(1)} %get-tuple-element.21, f32[512,2]{0,1:T(2,128)S(1)} %get-tuple-element.19, s32[512]{0:T(512)S(1)} %copy-done.5), kind=kOutput, calls=%fused_computation.4 | convolution fusion | flops 51478528 | bytes 403456 | tf_op jit(solution)/shard_map/mra,mb->rab/dot_general | solution.py:90
  45.5 0.6 gather_fusion
  46.2 0.6 fusion
  47.8 2.1 %fusion.9 = f32[512,2,64]{0,2,1:T(8,128)S(1)} fusion(s32[512]{0:T(512)S(1)} %copy-done.5, f32[2,64,128]{2,1,0:T(8,128)S(1)} %reshape.229, f32[2,64,128]{2,1,0:T(8,128)S(1)} %fusion.1, f32[1,2,64,128]{3,1,2,0:T(2,128)} %bitcast.81), kind=kOutput, calls=%fused_computation.20 | convolution fusion | flops 51281920 | bytes 460800 | tf_op jit(solution)/shard_map/rab,mb->mra/dot_general | solution.py:97
  49.9 1.3 %subtract_bitcast_fusion = (f32[512,1,2,64]{0,3,2,1:T(8,128)S(1)}, f32[512,1,2,64]{0,3,2,1:T(8,128)S(1)}) fusion(f32[512,2,64]{0,2,1:T(8,128)S(1)} %fusion.9, f32[512,64]{0,1:T(8,128)S(1)} %get-tuple-element.22, f32[512,64]{0,1:T(8,128)S(1)} %get-tuple-element.21, f32[2,64,128]{2,1,0:T(8,128)S(1)} %reshape.229, f32[2,64,128]{2,1,0:T(8,128)S(1)} %fusion.1, ...), kind=kOutput, calls=%fused_computation.28 | convolution fusion | flops 51740672 | bytes 1247232 | tf_op jit(solution)/shard_map/rab,mb->mra/dot_general | solution.py:96
  52.0 18.2 %all_to_all.33 = bf16[256,1,64]{2,1,0:T(2,128)(2,1)S(1)} all-to-all(bf16[256,1,64]{2,1,0:T(2,128)(2,1)S(1)} %copy.65), channel_id=1, replica_groups=mesh['blk'=32,'band'=8] {'blk','band'}, dimensions={0} | all-to-all | bytes 65536 | tf_op jit(solution)/shard_map/all_to_all | solution.py:106
  70.4 0.6 reshape.230
  71.0 0.8 copy.67
  71.9 1.5 %fusion.2 = f32[16,16,512]{2,1,0:T(8,128)S(1)} fusion(bf16[16,16,64]{2,1,0:T(8,128)(2,1)S(1)} %copy.68, bf16[16,64,4096]{2,1,0:T(8,128)(2,1)} %param.18, s32[]{:T(128)S(6)} %select_n.34), kind=kOutput, calls=%fused_computation.6 | convolution fusion | flops 16777216 | bytes 1605636 | tf_op jit(solution)/shard_map/sqr,srl->sql/dot_general | solution.py:109
  75.0 18.2 %all_to_all.34 = f32[256,1,4]{2,1,0:T(1,128)S(1)} all-to-all(f32[256,1,4]{2,1,0:T(1,128)S(1)} %broadcast_in_dim.28), channel_id=1, replica_groups=mesh['blk'=32,'band'=8] {'blk','band'}, dimensions={0} | all-to-all | bytes 8192 | tf_op jit(solution)/shard_map/all_to_all | solution.py:122
  93.6 0.7 multiply_add_fusion
  (59 shorter events, 6.4 us)
Async XLA Ops:
  0.6 42.1 %copy-start.5 = (s32[512]{0:T(512)S(1)}, s32[512]{0:T(512)}, u32[]{:S(2)}) copy-start(s32[512]{0:T(512)} %param.19) | copy-start | bytes 6148
  0.6 45.5 %copy-start = (f32[32,64,64]{2,1,0:T(8,128)S(1)}, f32[32,64,64]{2,1,0:T(8,128)}, u32[]{:S(2)}) copy-start(f32[32,64,64]{2,1,0:T(8,128)} %param.21) | copy-start | bytes 1572868
  0.7 11.3 %all-to-all-start = ((f32[8,1,512]{2,1,0:T(1,128)}), f32[8,1,512]{2,1,0:T(1,128)S(1)}, u32[]{:S(2)}, u32[]{:S(2)}) async-start(f32[8,1,512]{2,1,0:T(1,128)} %bitcast.76), calls=%async_computation | async-start | bytes 32768 | tf_op jit(solution)/shard_map/all_to_all | solution.py:65
  13.6 33.9 %copy-start.7 = (s32[128]{0:T(128)S(1)}, s32[128]{0:T(128)}, u32[]{:S(2)}) copy-start(s32[128]{0:T(128)} %param.22) | copy-start | bytes 1540
  16.0 25.5 %all-to-all-start.1 = ((f32[256,1,64]{2,1,0:T(1,128)}), f32[256,1,64]{2,1,0:T(1,128)S(1)}, u32[]{:S(2)}, u32[]{:S(2)}) async-start(f32[256,1,64]{2,1,0:T(1,128)} %copy.58), calls=%async_computation.1 | async-start | bytes 262144 | tf_op jit(solution)/shard_map/all_to_all | solution.py:78
  42.6 7.4 %copy-start.8 = (f32[1,2,8192]{2,1,0:T(2,128)S(1)}, f32[1,2,8192]{2,1,0:T(2,128)}, u32[]{:S(2)}) copy-start(f32[1,2,8192]{2,1,0:T(2,128)} %param.20) | copy-start | bytes 196612
  44.1 29.9 %copy-start.1 = (f32[16,2,512]{2,1,0:T(2,128)S(1)}, f32[16,2,512]{2,1,0:T(2,128)}, u32[]{:S(2)}) copy-start(f32[16,2,512]{2,1,0:T(2,128)} %param.14) | copy-start | bytes 196612
  44.1 29.9 %copy-start.6 = (f32[512]{0:T(512)S(1)}, f32[512]{0:T(512)}, u32[]{:S(2)}) copy-start(f32[512]{0:T(512)} %param.15) | copy-start | bytes 6148
  44.1 30.0 %copy-start.2 = (f32[16,2,512]{2,1,0:T(2,128)S(1)}, f32[16,2,512]{2,1,0:T(2,128)}, u32[]{:S(2)}) copy-start(f32[16,2,512]{2,1,0:T(2,128)} %param.13) | copy-start | bytes 196612
  44.1 30.0 %copy-start.4 = (f32[512]{0:T(512)S(1)}, f32[512]{0:T(512)}, u32[]{:S(2)}) copy-start(f32[512]{0:T(512)} %param.16) | copy-start | bytes 6148
  45.5 48.1 %copy-start.3 = (f32[16,2,512]{2,1,0:T(2,128)S(1)}, f32[16,2,512]{2,1,0:T(2,128)}, u32[]{:S(2)}) copy-start(f32[16,2,512]{2,1,0:T(2,128)} %param.12) | copy-start | bytes 196612
